TPU v7x, 256 devices: a whole 4x4x8 slice. The times are simulated.
256 devices in a mesh: expert: 16 (over y, x), tensor: 8 (over z), dp: 2 (over core).
Axes of the slice: x: 4, y: 4, z: 8, core: 2. Of those that a mesh axis runs over, the one named last changes fastest.
Arguments:
- out_grad: bfloat16 [16384, 2048], P(('expert', 'dp'), 'tensor'), may hold values from -1.5 to 1.5
- expert_ids: int32 [16384, 2], P(('expert', 'dp')), may hold values from 0 to 31, all different within a row; in each aligned block of 512 rows (0 to 511, 512 to 1023, ...) at most 36 rows name the same one
- gate_weights: float32 [16384, 2], P(('expert', 'dp')), may hold values from 0.05 to 1
- keep: int32 [16384, 2], P(('expert', 'dp')), may hold values 0 or 1
- hidden_act: bfloat16 [32, 1152, 7168], P('expert', 'dp', 'tensor'), may hold values from -3 to 3
- down_weight: bfloat16 [32, 7168, 2048], P('expert', 'tensor', 'dp'), may hold values from -0.0625 to 0.0625
Outputs:
- grad_down: bfloat16 [32, 7168, 2048], P('expert', 'tensor', 'dp')
- grad_hidden: bfloat16 [32, 1152, 7168], P('expert', 'dp', 'tensor')
- gate_grad: float32 [16384, 2], P(('expert', 'dp'))
Inputs may be any that keep to these rules, and one draw needn't show every extreme that they name: `expert_ids`: each row names two different experts; among the 512 rows of one device no expert is named more than 36 times, and in every draw some device names some expert exactly 36 times.
All inputs are finite; a program needn't handle non-finite values. No bound on the sum of `keep` on one device may be relied on, other than what follows from the above.
Results may differ from a plain program's by a relative error of at most 0.0064.
Values may be sent and summed in bfloat16 or wider, within the bound.
No kernel may reach another device: no remote copies, remote signals or barrier semaphores. Data moves between devices by JAX's collectives and lax.ppermute only.
A program may use at most 128 MiB of HBM per device.

v0:
```python
import jax
import jax.numpy as jnp
from jax import lax
from jax.sharding import PartitionSpec as P


def from_partner(value, axis, stride):
    mask = 2**stride
    pairs = [(source, source ^ mask) for source in range(lax.axis_size(axis))]
    return lax.ppermute(value, axis, pairs)


def body(out_grad, expert_ids, gate_weights, keep, hidden_act, down_weight):
    token_count = out_grad.shape[0]
    experts = lax.axis_size("expert")
    local_experts = hidden_act.shape[0]
    total_experts = experts * local_experts
    slot_count = hidden_act.shape[1]
    capacity = slot_count // experts
    chosen = expert_ids.reshape(-1)
    onehot = (chosen[:, None] == jnp.arange(total_experts, dtype=jnp.int32)[None, :]).astype(
        jnp.int32
    )
    ranking = jnp.cumsum(onehot, axis=0) - onehot
    position = chosen * capacity + jnp.sum(ranking * onehot, axis=1)
    placing = (
        position[None, :] == jnp.arange(total_experts * capacity, dtype=jnp.int32)[:, None]
    ).astype(jnp.bfloat16)
    kept_mask = keep.reshape(-1).astype(jnp.float32)
    scale_flat = (gate_weights.reshape(-1) * kept_mask).astype(jnp.bfloat16)
    slot_scale = (
        jnp.dot(placing, scale_flat[:, None], preferred_element_type=jnp.float32)
        .astype(jnp.bfloat16)
        .reshape(experts, local_experts, capacity)
    )
    gathered = lax.all_gather(out_grad, "tensor", axis=1, tiled=True)
    outgoing = jnp.dot(
        placing, jnp.repeat(gathered, 2, axis=0), preferred_element_type=jnp.float32
    ).astype(jnp.bfloat16)
    arrived, arrived_scale = (
        lax.all_to_all(
            outgoing.reshape(experts, local_experts, capacity, -1),
            "expert",
            split_axis=0,
            concat_axis=2,
            tiled=True,
        ),
        lax.all_to_all(slot_scale, "expert", split_axis=0, concat_axis=2, tiled=True),
    )
    routed = arrived.reshape(local_experts, slot_count, -1)
    weight = arrived_scale.reshape(local_experts, slot_count).astype(jnp.float32)
    backprop = lax.dot_general(
        routed,
        lax.all_gather(down_weight, "dp", axis=2, tiled=True),
        (((2,), (2,)), ((0,), (0,))),
        preferred_element_type=jnp.float32,
    )
    grad_hidden = (weight[:, :, None] * backprop).astype(jnp.bfloat16)
    partial_score = jnp.sum(backprop * hidden_act.astype(jnp.float32), axis=2)
    scores = lax.psum(partial_score, "tensor")
    returned = lax.all_to_all(
        scores.reshape(local_experts, experts, capacity),
        "expert",
        split_axis=1,
        concat_axis=0,
        tiled=True,
    )
    gate_grad = (jnp.take(returned.reshape(-1), position) * kept_mask).reshape(token_count, 2)
    scaled = (weight[:, :, None] * routed.astype(jnp.float32)).astype(jnp.bfloat16)
    contract_rows = (((1,), (1,)), ((0,), (0,)))
    half_width = scaled.shape[2] // 2
    dp_index = lax.axis_index("dp")
    own_cols = lax.dynamic_slice_in_dim(scaled, dp_index * half_width, half_width, 2)
    theirs = lax.dynamic_slice_in_dim(scaled, (1 - dp_index) * half_width, half_width, 2)
    peer_hidden, peer_scaled = from_partner((hidden_act, theirs), "dp", 0)
    own_term = lax.dot_general(
        hidden_act, own_cols, contract_rows, preferred_element_type=jnp.float32
    ).astype(jnp.bfloat16)
    peer_term = lax.dot_general(
        peer_hidden, peer_scaled, contract_rows, preferred_element_type=jnp.float32
    ).astype(jnp.bfloat16)
    own_term, peer_term = lax.optimization_barrier((own_term, peer_term))
    summed = own_term.astype(jnp.float32) + peer_term.astype(jnp.float32)
    grad_down = summed.astype(jnp.bfloat16)
    return (grad_down, grad_hidden, gate_grad)


def solution(mesh):
    in_specs = (
        P(("expert", "dp"), "tensor"),
        P(("expert", "dp"), None),
        P(("expert", "dp"), None),
        P(("expert", "dp"), None),
        P("expert", "dp", "tensor"),
        P("expert", "tensor", "dp"),
    )
    out_specs = (
        P("expert", "tensor", "dp"),
        P("expert", "dp", "tensor"),
        P(("expert", "dp"), None),
    )
    return jax.shard_map(body, mesh=mesh, in_specs=in_specs, out_specs=out_specs, check_vma=False)
```

profile of v0, /device:TPU:2, one launch (start us, length us, event | category | flops | bytes accessed | tf_op | source)
XLA Modules:
  0.0 255.3 jit_solution(9706728191636282774)
XLA Ops:
  8.7 0.8 copy.37
  9.9 9.0 %reduce-window.6 = s32[32,8,128]{2,1,0:T(8,128)S(1)} reduce-window(s32[32,8,128]{2,1,0:T(8,128)S(1)} %fusion.10, s32[]{:T(128)} %constant.12.clone.1), window={size=1x1x128 pad=0_0x0_0x127_0}, to_apply=%region_0.0 | reduce-window | flops 4161536 | bytes 262148 | tf_op jit(solution)/shard_map/reduce-window
  19.9 0.9 fusion.6
  21.5 7.5 %all-to-all-start = ((bf16[16,2,36]{2,1,0:T(2,128)(2,1)}), bf16[16,2,36]{2,1,0:T(2,128)(2,1)S(1)}, u32[]{:S(2)}, u32[]{:S(2)}) async-start(bf16[16,2,36]{2,1,0:T(2,128)(2,1)} %reshape.118), calls=%async_computation | async-start | bytes 16384 | tf_op jit(solution)/shard_map/all_to_all | solution.py:48
  29.0 31.2 %all-gather.3.cloned.1.call-done = bf16[512,2048]{1,0:T(8,128)(2,1)} async-done(((bf16[512,256]{1,0:T(8,128)(2,1)}), bf16[512,2048]{1,0:T(8,128)(2,1)}) %all-gather.3.cloned.1.call-update) | async-done | bytes 2097168 | tf_op jit(solution)/shard_map/all_gather | solution.py:36
  60.2 5.4 %broadcast_in_dim.6 = bf16[512,2,2048]{2,1,0:T(2,128)(2,1)} broadcast(bf16[512,2048]{1,0:T(8,128)(2,1)} %all-gather.3.cloned.1.call-done), dimensions={0,2} | broadcast | bytes 6291456 | tf_op jit(solution)/shard_map/broadcast_in_dim | solution.py:38
  65.6 7.2 %reshape.119 = bf16[1024,2048]{1,0:T(8,128)(2,1)} reshape(bf16[512,2,2048]{2,1,0:T(2,128)(2,1)} %broadcast_in_dim.6) | data formatting | bytes 8388608 | tf_op jit(solution)/shard_map/reshape | solution.py:38
  72.8 9.5 %convolution_convert_fusion = bf16[1152,2048]{1,0:T(8,128)(2,1)} fusion(bf16[1024,2048]{1,0:T(8,128)(2,1)} %reshape.119, s32[1024]{0:T(1024)S(1)} %multiply_add_fusion), kind=kOutput, calls=%fused_computation.2 | convolution fusion | flops 4835377152 | bytes 8916992 | tf_op jit(solution)/shard_map/dot_general | solution.py:37
  82.3 7.2 %reshape.120 = bf16[16,2,36,2048]{3,2,1,0:T(8,128)(2,1)} reshape(bf16[1152,2048]{1,0:T(8,128)(2,1)} %convolution_convert_fusion) | data formatting | bytes 9437184 | tf_op jit(solution)/shard_map/reshape | solution.py:42
  89.6 9.5 %copy.44 = bf16[16,2,36,2048]{3,1,2,0:T(2,128)(2,1)} copy(bf16[16,2,36,2048]{3,2,1,0:T(8,128)(2,1)} %reshape.120) | data formatting | bytes 9437184 | tf_op jit(solution)/shard_map/reshape | solution.py:42
  99.1 7.4 %all-to-all-start.1 = ((bf16[16,2,36,2048]{3,1,2,0:T(2,128)(2,1)}), bf16[16,2,36,2048]{3,1,2,0:T(2,128)(2,1)}, u32[]{:S(2)}, u32[]{:S(2)}) async-start(bf16[16,2,36,2048]{3,1,2,0:T(2,128)(2,1)} %copy.44), calls=%async_computation.1 | async-start | bytes 9437184 | tf_op jit(solution)/shard_map/all_to_all | solution.py:41
  106.6 53.6 %all-to-all-done.1 = bf16[16,2,36,2048]{3,1,2,0:T(2,128)(2,1)} async-done(((bf16[16,2,36,2048]{3,1,2,0:T(2,128)(2,1)}), bf16[16,2,36,2048]{3,1,2,0:T(2,128)(2,1)}, u32[]{:S(2)}, u32[]{:S(2)}) %all-to-all-start.1) | async-done | bytes 4718624 | tf_op jit(solution)/shard_map/all_to_all | solution.py:41
  160.1 5.0 %multiply_convert_fusion = bf16[2,576,2048]{2,1,0:T(8,128)(2,1)S(1)} fusion(f32[2,576]{1,0:T(2,128)S(1)} %reshape.124, bf16[2,576,2048]{2,0,1:T(2,128)(2,1)} %bitcast.6), kind=kLoop, calls=%fused_computation.1 | loop fusion | flops 7077888 | bytes 9441792 | tf_op jit(solution)/shard_map/convert_element_type | solution.py:69
  165.2 2.1 copy-done
  168.1 12.3 %multiply_reduce_fusion = (f32[2,576]{1,0:T(2,128)S(1)}, bf16[2,576,896]{2,1,0:T(8,128)(2,1)}) fusion(bf16[2,576,896]{2,1,0:T(8,128)(2,1)} %param.10, f32[2,576]{1,0:T(2,128)S(1)} %reshape.124, bf16[2,896,2048]{2,1,0:T(8,128)(2,1)} %all-gather.5.cloned.1.call-done, bf16[2,576,2048]{2,0,1:T(2,128)(2,1)} %bitcast.6), kind=kOutput, calls=%fused_computation.8 | convolution fusion | flops 4233018368 | bytes 16196608 | tf_op jit(solution)/shard_map/dot_general | solution.py:52
  180.4 29.5 %psum.7 = f32[2,16,36]{2,1,0:T(8,128)S(1)} all-reduce(f32[2,16,36]{2,1,0:T(8,128)S(1)} %reshape.122), channel_id=1, replica_groups=mesh['expert'=16,'tensor'=8,'dp'=2] {'tensor'}, use_global_device_ids=true, to_apply=%region_4.5 | all-reduce | flops 1152 | bytes 9216 | tf_op jit(solution)/shard_map/psum | solution.py:60
  210.6 7.0 %all-to-all-start.2 = ((f32[2,16,36]{2,0,1:T(2,128)}), f32[2,16,36]{2,0,1:T(2,128)S(1)}, u32[]{:S(2)}, u32[]{:S(2)}) async-start(f32[2,16,36]{2,0,1:T(2,128)} %copy.48), calls=%async_computation.2 | async-start | bytes 32768 | tf_op jit(solution)/shard_map/all_to_all | solution.py:61
  217.6 7.5 %convert_bitcast_fusion.1 = bf16[2,896,1024]{1,2,0:T(8,128)(2,1)} fusion(bf16[2,576,896]{2,1,0:T(8,128)(2,1)} %param.10, bf16[2,576,2048]{2,1,0:T(8,128)(2,1)} %copy-done, s32[]{:T(128)S(6)} %select_n.28), kind=kOutput, calls=%fused_computation.11 | convolution fusion | flops 2115764224 | bytes 8093700 | tf_op jit(solution)/shard_map/dot_general | solution.py:76
  225.2 6.2 %gather_fusion = f32[1024]{0:T(1024)S(1)} fusion(f32[1152]{0:T(1024)S(1)} %reshape.123, s32[1024]{0:T(1024)S(1)} %broadcast_clamp_fusion), kind=kCustom, calls=%fused_computation | custom fusion | bytes 12288 | tf_op jit(solution)/shard_map/jit(_take)/gather | solution.py:68
  231.5 0.8 select_multiply_fusion
  232.3 1.7 copy.50
  234.0 5.8 %convert_bitcast_fusion = bf16[2,896,1024]{1,2,0:T(8,128)(2,1)S(1)} fusion(bf16[2,576,1024]{2,1,0:T(8,128)(2,1)} %collective-permute-done, bf16[2,576,896]{2,1,0:T(8,128)(2,1)} %collective-permute-done.1), kind=kOutput, calls=%fused_computation.10 | convolution fusion | flops 2115764224 | bytes 8093696 | tf_op jit(solution)/shard_map/dot_general | solution.py:79
  239.8 2.7 %add_convert_fusion = bf16[2,896,1024]{1,2,0:T(8,128)(2,1)} fusion(bf16[2,896,1024]{1,2,0:T(8,128)(2,1)S(1)} %convert_bitcast_fusion, bf16[2,896,1024]{1,2,0:T(8,128)(2,1)S(1)} %copy-done.1), kind=kLoop, calls=%fused_computation.3 | loop fusion | flops 7340032 | bytes 11010048 | tf_op jit(solution)/shard_map/convert_element_type | solution.py:84
  242.4 6.0 %copy.49 = bf16[2,896,1024]{2,1,0:T(8,128)(2,1)} copy(bf16[2,896,1024]{1,2,0:T(8,128)(2,1)} %add_convert_fusion) | data formatting | bytes 7340032
  (47 shorter events, 5.3 us)
Async XLA Ops:
  7.2 12.2 %copy-start.2 = (s32[512,2]{0,1:T(2,128)S(1)}, s32[512,2]{0,1:T(2,128)}, u32[]{:S(2)}) copy-start(s32[512,2]{0,1:T(2,128)} %param.9) | copy-start | bytes 12292
  7.2 12.3 %copy-start.3 = (f32[512,2]{0,1:T(2,128)S(1)}, f32[512,2]{0,1:T(2,128)}, u32[]{:S(2)}) copy-start(f32[512,2]{0,1:T(2,128)} %param.8) | copy-start | bytes 12292
  7.2 53.0 %all-gather.3.cloned.1.call-start = ((), (), s32[]{:S(2)}) async-start(), calls=%async_computation.3 | async-start | bytes 2359296 | tf_op jit(solution)/shard_map/all_gather | solution.py:36
  7.9 160.1 %all-gather.5.cloned.1.call-start = ((), (), s32[]{:S(2)}) async-start(), calls=%async_computation.4 | async-start | bytes 11010048 | tf_op jit(solution)/shard_map/all_gather | solution.py:54
  21.5 77.5 %all-to-all-start = ((bf16[16,2,36]{2,1,0:T(2,128)(2,1)}), bf16[16,2,36]{2,1,0:T(2,128)(2,1)S(1)}, u32[]{:S(2)}, u32[]{:S(2)}) async-start(bf16[16,2,36]{2,1,0:T(2,128)(2,1)} %reshape.118), calls=%async_computation | async-start | bytes 16384 | tf_op jit(solution)/shard_map/all_to_all | solution.py:48
  99.1 61.1 %all-to-all-start.1 = ((bf16[16,2,36,2048]{3,1,2,0:T(2,128)(2,1)}), bf16[16,2,36,2048]{3,1,2,0:T(2,128)(2,1)}, u32[]{:S(2)}, u32[]{:S(2)}) async-start(bf16[16,2,36,2048]{3,1,2,0:T(2,128)(2,1)} %copy.44), calls=%async_computation.1 | async-start | bytes 9437184 | tf_op jit(solution)/shard_map/all_to_all | solution.py:41
  106.4 127.6 %collective-permute-start.1 = (bf16[2,576,896]{2,1,0:T(8,128)(2,1)}, bf16[2,576,896]{2,1,0:T(8,128)(2,1)}, u32[]{:S(2)}, u32[]{:S(2)}) collective-permute-start(bf16[2,576,896]{2,1,0:T(8,128)(2,1)} %param.10), channel_id=1, source_target_pairs={{0,1},{1,0},{2,3},{3,2},{4,5},{5,4},{6,7},{7,6},{8,9},{9,8},{10,11... | collective-permute-start | bytes 6193160 | tf_op jit(solution)/shard_map/ppermute | solution.py:10
  165.2 2.1 copy-start
  167.5 66.5 %collective-permute-start = (bf16[2,576,1024]{2,1,0:T(8,128)(2,1)S(1)}, bf16[2,576,1024]{2,1,0:T(8,128)(2,1)}, u32[]{:S(2)}, u32[]{:S(2)}) collective-permute-start(bf16[2,576,1024]{2,1,0:T(8,128)(2,1)S(1)} %constant_dynamic-slice_fusion), channel_id=1, source_target_pairs={{0,1},{1,0},{2,3},{3,2},{4,5},{5,4},{6,7},{7,6},{8,9},{9,8},{10,11... | collective-permute-start | bytes 7077896 | tf_op jit(solution)/shard_map/ppermute | solution.py:10
  210.6 14.5 %all-to-all-start.2 = ((f32[2,16,36]{2,0,1:T(2,128)}), f32[2,16,36]{2,0,1:T(2,128)S(1)}, u32[]{:S(2)}, u32[]{:S(2)}) async-start(f32[2,16,36]{2,0,1:T(2,128)} %copy.48), calls=%async_computation.2 | async-start | bytes 32768 | tf_op jit(solution)/shard_map/all_to_all | solution.py:61
  234.0 5.8 %copy-start.1 = (bf16[2,896,1024]{1,2,0:T(8,128)(2,1)S(1)}, bf16[2,896,1024]{1,2,0:T(8,128)(2,1)}, u32[]{:S(2)}) copy-start(bf16[2,896,1024]{1,2,0:T(8,128)(2,1)} %convert_bitcast_fusion.1) | copy-start | bytes 11010052
Sparse Core Ops, SparseCore 0:
  9.7 50.4 all-gather.2
  62.0 22.2 all-gather.4
where the time goes:
time: 256 us; the launch traced here: 255 us
  waiting for transfers between devices  86.2 us (34%)
  local copies, waits for them, and re-layouts  49.5 us (19%)
  matrix products  35.9 us (14%)
  blocking collectives  29.5 us (12%)
  starting transfers between devices  22 us (9%)
  other arithmetic  17.8 us (7%)
  between operations  14.3 us (6%)
    all_to_all x1, waiting for transfers between devices, body(): lax.all_to_all(outgoing.reshape(experts, local_experts, capacity, -1), 'e...  53.6 us
    all_gather x1, waiting for transfers between devices, body(): gathered = lax.all_gather(out_grad, 'tensor', axis=1, tiled=True)  31.2 us
    psum x1, blocking collectives, body(): scores = lax.psum(partial_score, 'tensor')  29.5 us
    reshape x2, local copies, waits for them, and re-layouts, body(): outgoing.reshape(experts, local_experts, capacity, -1)  16.7 us
    dot_general x1, matrix products, body(): lax.dot_general(routed, lax.all_gather(down_weight, 'dp', axis=2, tiled=T...  12.3 us
    unnamed x13, local copies, waits for them, and re-layouts  10.9 us
    dot_general x1, matrix products, body(): jnp.dot(placing, jnp.repeat(gathered, 2, axis=0), preferred_element_type=...  9.51 us
    another operation x3, other arithmetic  9.15 us
  transfers between devices with their start and end apart: 7, of which 2 were waited for; matrix products, arithmetic and copies ran while one was open for 34% of the time, Pallas kernels for 0%

commit v1 on v0

--- a/solution.py
+++ b/solution.py
@@ -17,26 +17,29 @@
     total_experts = experts * local_experts
     slot_count = hidden_act.shape[1]
     capacity = slot_count // experts
+    places = total_experts * capacity
     chosen = expert_ids.reshape(-1)
-    onehot = (chosen[:, None] == jnp.arange(total_experts, dtype=jnp.int32)[None, :]).astype(
-        jnp.int32
-    )
-    ranking = jnp.cumsum(onehot, axis=0) - onehot
-    position = chosen * capacity + jnp.sum(ranking * onehot, axis=1)
-    placing = (
-        position[None, :] == jnp.arange(total_experts * capacity, dtype=jnp.int32)[:, None]
+    count = chosen.shape[0]
+    onehot = chosen[:, None] == jnp.arange(total_experts, dtype=jnp.int32)[None, :]
+    earlier = (
+        jnp.arange(count, dtype=jnp.int32)[:, None] > jnp.arange(count, dtype=jnp.int32)[None, :]
     ).astype(jnp.bfloat16)
-    kept_mask = keep.reshape(-1).astype(jnp.float32)
-    scale_flat = (gate_weights.reshape(-1) * kept_mask).astype(jnp.bfloat16)
+    ranking = jnp.dot(earlier, onehot.astype(jnp.bfloat16), preferred_element_type=jnp.float32)
+    slot = jnp.sum(jnp.where(onehot, ranking, 0.0), axis=1).astype(jnp.int32)
+    position = chosen * capacity + slot
+    pos2 = position.reshape(token_count, 2)
+    iota_p = jnp.arange(places, dtype=jnp.int32)[:, None]
+    pick0 = pos2[None, :, 0] == iota_p
+    pick1 = pos2[None, :, 1] == iota_p
+    placing = (pick0 | pick1).astype(jnp.bfloat16)
+    kept = keep.astype(jnp.float32)
+    scale = (gate_weights * kept).astype(jnp.bfloat16)
     slot_scale = (
-        jnp.dot(placing, scale_flat[:, None], preferred_element_type=jnp.float32)
-        .astype(jnp.bfloat16)
-        .reshape(experts, local_experts, capacity)
-    )
+        jnp.dot(pick0.astype(jnp.bfloat16), scale[:, 0], preferred_element_type=jnp.float32)
+        + jnp.dot(pick1.astype(jnp.bfloat16), scale[:, 1], preferred_element_type=jnp.float32)
+    ).astype(jnp.bfloat16).reshape(experts, local_experts, capacity)
     gathered = lax.all_gather(out_grad, "tensor", axis=1, tiled=True)
-    outgoing = jnp.dot(
-        placing, jnp.repeat(gathered, 2, axis=0), preferred_element_type=jnp.float32
-    ).astype(jnp.bfloat16)
+    outgoing = jnp.dot(placing, gathered, preferred_element_type=jnp.float32).astype(jnp.bfloat16)
     arrived, arrived_scale = (
         lax.all_to_all(
             outgoing.reshape(experts, local_experts, capacity, -1),
@@ -57,15 +60,18 @@
     )
     grad_hidden = (weight[:, :, None] * backprop).astype(jnp.bfloat16)
     partial_score = jnp.sum(backprop * hidden_act.astype(jnp.float32), axis=2)
-    scores = lax.psum(partial_score, "tensor")
+    scores = jnp.sum(lax.all_gather(partial_score, "tensor", axis=0, tiled=False), axis=0)
     returned = lax.all_to_all(
         scores.reshape(local_experts, experts, capacity),
         "expert",
         split_axis=1,
         concat_axis=0,
         tiled=True,
+    ).reshape(-1)
+    picked = jnp.sum(
+        jnp.where(position[:, None] == iota_p[None, :, 0], returned[None, :], 0.0), axis=1
     )
-    gate_grad = (jnp.take(returned.reshape(-1), position) * kept_mask).reshape(token_count, 2)
+    gate_grad = picked.reshape(token_count, 2) * kept
     scaled = (weight[:, :, None] * routed.astype(jnp.float32)).astype(jnp.bfloat16)
     contract_rows = (((1,), (1,)), ((0,), (0,)))
     half_width = scaled.shape[2] // 2

time: 256 us -> 228 us (0.89)
  local copies, waits for them, and re-layouts: 49.5 us -> 29.9 us
  other arithmetic: 17.8 us -> 8.57 us
  waiting for transfers between devices: 86.2 us -> 94.9 us
  blocking collectives: 29.5 us -> 24.7 us
  matrix products: 35.9 us -> 32.8 us
    psum x1 -> x0, blocking collectives: 29.5 us -> none  [body(): scores = lax.psum(partial_score, 'tensor')]
    all_gather x0 -> x1, blocking collectives: none -> 24.7 us  [body(): lax.all_gather(partial_score, 'tensor', axis=0, tiled=False)]
    all_gather x1, waiting for transfers between devices: 31.2 us -> 40.5 us  [body(): gathered = lax.all_gather(out_grad, 'tensor', axis=1, tiled=True)]
    another operation x3 -> x0, other arithmetic: 9.15 us -> none
    reshape x4 -> x2, local copies, waits for them, and re-layouts: 8.17 us -> 0.93 us  [the longest x1 0.72 us: body(): slot_scale = (jnp.dot(pick0.astype(jnp.bfloat16), scale[:, 0], preferred_...]
    gather x2 -> x0, local copies, waits for them, and re-layouts: 6.35 us -> none  [body(): jnp.take(returned.reshape(-1), position) * kept_mask]
    broadcast_in_dim x1, local copies, waits for them, and re-layouts: 5.4 us -> 0.1 us  [body(): jnp.where(position[:, None] == iota_p[None, :, 0], returned[None, :], 0.0)]
    dot_general x2 -> x4, matrix products: 10.4 us -> 7.33 us  [the longest x1 5.78 us: body(): jnp.dot(placing, gathered, preferred_element_type=jnp.float32)]
  transfers between devices with their start and end apart: 7 -> 7, of which waited for: 2 -> 2; matrix products, arithmetic and copies ran while one was open for 34% -> 24% of each run, Pallas kernels for 0% -> 0%
where the time goes in v1:
time: 228 us
  waiting for transfers between devices  94.9 us (42%)
  matrix products  32.8 us (14%)
  local copies, waits for them, and re-layouts  29.9 us (13%)
  blocking collectives  24.7 us (11%)
  starting transfers between devices  22.7 us (10%)
  between operations  14.3 us (6%)
  other arithmetic  8.57 us (4%)
    all_to_all x1, waiting for transfers between devices, body(): lax.all_to_all(outgoing.reshape(experts, local_experts, capacity, -1), 'e...  53 us
    all_gather x1, waiting for transfers between devices, body(): gathered = lax.all_gather(out_grad, 'tensor', axis=1, tiled=True)  40.5 us
    all_gather x1, blocking collectives, body(): lax.all_gather(partial_score, 'tensor', axis=0, tiled=False)  24.7 us
    reshape x2, local copies, waits for them, and re-layouts, body(): outgoing.reshape(experts, local_experts, capacity, -1)  17.8 us
    dot_general x1, matrix products, body(): lax.dot_general(routed, lax.all_gather(down_weight, 'dp', axis=2, tiled=T...  12.3 us
    unnamed x15, local copies, waits for them, and re-layouts  9.27 us
    all_to_all x1, starting transfers between devices, body(): lax.all_to_all(slot_scale, 'expert', split_axis=0, concat_axis=2, tiled=T...  7.48 us
    dot_general x1, matrix products, body(): lax.dot_general(hidden_act, own_cols, contract_rows, preferred_element_ty...  7.46 us
  transfers between devices with their start and end apart: 7, of which 2 were waited for; matrix products, arithmetic and copies ran while one was open for 24% of the time, Pallas kernels for 0%

profile of v1, /device:TPU:2, one launch (start us, length us, event | category | flops | bytes accessed | tf_op | source)
XLA Modules:
  0.0 227.8 jit_solution(546728603600389392)
XLA Ops:
  7.2 0.7 all-gather.5.cloned.1.call-update
  8.0 0.7 all-gather.7.cloned.1.call-update
  9.0 0.5 fusion.13
  11.1 0.5 fusion.15
  11.6 0.7 reshape.51
  12.3 7.5 %all-to-all-start = ((bf16[16,2,36]{2,1,0:T(2,128)(2,1)}), bf16[16,2,36]{2,1,0:T(2,128)(2,1)S(1)}, u32[]{:S(2)}, u32[]{:S(2)}) async-start(bf16[16,2,36]{2,1,0:T(2,128)(2,1)} %reshape.51), calls=%async_computation | async-start | bytes 16384 | tf_op jit(solution)/shard_map/all_to_all | solution.py:51
  19.8 40.5 %all-gather.5.cloned.1.call-done = bf16[512,2048]{1,0:T(8,128)(2,1)} async-done(((bf16[512,256]{1,0:T(8,128)(2,1)}), bf16[512,2048]{1,0:T(8,128)(2,1)}) %all-gather.5.cloned.1.call-update) | async-done | bytes 2097168 | tf_op jit(solution)/shard_map/all_gather | solution.py:41
  60.3 5.8 %convolution_convert_fusion = bf16[1152,2048]{1,0:T(8,128)(2,1)} fusion(bf16[512,2048]{1,0:T(8,128)(2,1)} %all-gather.5.cloned.1.call-done, s32[512]{0:T(512)S(1)} %bitcast.34, s32[512]{0:T(512)S(1)} %bitcast.36), kind=kOutput, calls=%fused_computation.1 | convolution fusion | flops 2420047872 | bytes 6819840 | tf_op jit(solution)/shard_map/dot_general | solution.py:42
  66.0 7.4 %reshape.52 = bf16[16,2,36,2048]{3,2,1,0:T(8,128)(2,1)} reshape(bf16[1152,2048]{1,0:T(8,128)(2,1)} %convolution_convert_fusion) | data formatting | bytes 9437184 | tf_op jit(solution)/shard_map/reshape | solution.py:45
  73.4 10.4 %copy.62 = bf16[16,2,36,2048]{3,1,2,0:T(2,128)(2,1)} copy(bf16[16,2,36,2048]{3,2,1,0:T(8,128)(2,1)} %reshape.52) | data formatting | bytes 9437184 | tf_op jit(solution)/shard_map/reshape | solution.py:45
  83.8 7.3 %all-to-all-start.1 = ((bf16[16,2,36,2048]{3,1,2,0:T(2,128)(2,1)}), bf16[16,2,36,2048]{3,1,2,0:T(2,128)(2,1)}, u32[]{:S(2)}, u32[]{:S(2)}) async-start(bf16[16,2,36,2048]{3,1,2,0:T(2,128)(2,1)} %copy.62), calls=%async_computation.1 | async-start | bytes 9437184 | tf_op jit(solution)/shard_map/all_to_all | solution.py:44
  91.2 53.0 %all-to-all-done.1 = bf16[16,2,36,2048]{3,1,2,0:T(2,128)(2,1)} async-done(((bf16[16,2,36,2048]{3,1,2,0:T(2,128)(2,1)}), bf16[16,2,36,2048]{3,1,2,0:T(2,128)(2,1)}, u32[]{:S(2)}, u32[]{:S(2)}) %all-to-all-start.1) | async-done | bytes 4718624 | tf_op jit(solution)/shard_map/all_to_all | solution.py:44
  144.2 5.0 %multiply_convert_fusion = bf16[2,576,2048]{2,1,0:T(8,128)(2,1)S(1)} fusion(f32[2,576]{1,0:T(2,128)S(1)} %reshape.56, bf16[2,576,2048]{2,0,1:T(2,128)(2,1)} %bitcast.6), kind=kLoop, calls=%fused_computation | loop fusion | flops 7077888 | bytes 9441792 | tf_op jit(solution)/shard_map/convert_element_type | solution.py:75
  149.3 2.1 copy-done
  152.3 12.3 %multiply_reduce_fusion = (f32[2,576]{1,0:T(2,128)S(1)}, bf16[2,576,896]{2,1,0:T(8,128)(2,1)}) fusion(bf16[2,576,896]{2,1,0:T(8,128)(2,1)} %param.10, f32[2,576]{1,0:T(2,128)S(1)} %reshape.56, bf16[2,896,2048]{2,1,0:T(8,128)(2,1)} %all-gather.7.cloned.1.call-done, bf16[2,576,2048]{2,0,1:T(2,128)(2,1)} %bitcast.6), kind=kOutput, calls=%fused_computation.9 | convolution fusion | flops 4233018368 | bytes 16196608 | tf_op jit(solution)/shard_map/dot_general | solution.py:55
  164.6 24.7 %all-gather.1 = f32[8,2,576]{2,1,0:T(2,128)S(1)} all-gather(f32[1,2,576]{2,1,0:T(2,128)S(1)} %bitcast.32), channel_id=2, replica_groups=mesh['expert'=16,'tensor'=8,'dp'=2] {'tensor'}, dimensions={0}, use_global_device_ids=true | all-gather | bytes 41472 | tf_op jit(solution)/shard_map/all_gather | solution.py:63
  189.4 0.6 copy.65
  190.0 7.2 %all-to-all-start.2 = ((f32[2,16,36]{2,0,1:T(2,128)}), f32[2,16,36]{2,0,1:T(2,128)S(1)}, u32[]{:S(2)}, u32[]{:S(2)}) async-start(f32[2,16,36]{2,0,1:T(2,128)} %copy.65), calls=%async_computation.2 | async-start | bytes 32768 | tf_op jit(solution)/shard_map/all_to_all | solution.py:64
  197.3 7.5 %convert_bitcast_fusion.1 = bf16[2,896,1024]{1,2,0:T(8,128)(2,1)} fusion(bf16[2,576,896]{2,1,0:T(8,128)(2,1)} %param.10, bf16[2,576,2048]{2,1,0:T(8,128)(2,1)} %copy-done, s32[]{:T(128)S(6)} %select_n.15), kind=kOutput, calls=%fused_computation.12 | convolution fusion | flops 2115764224 | bytes 8093700 | tf_op jit(solution)/shard_map/dot_general | solution.py:82
  204.9 0.7 select_reduce_fusion
  205.8 0.7 copy.67
  206.6 5.8 %convert_bitcast_fusion = bf16[2,896,1024]{1,2,0:T(8,128)(2,1)S(1)} fusion(bf16[2,576,1024]{2,1,0:T(8,128)(2,1)} %collective-permute-done, bf16[2,576,896]{2,1,0:T(8,128)(2,1)} %collective-permute-done.1), kind=kOutput, calls=%fused_computation.11 | convolution fusion | flops 2115764224 | bytes 8093696 | tf_op jit(solution)/shard_map/dot_general | solution.py:85
  212.3 2.7 %add_convert_fusion = bf16[2,896,1024]{1,2,0:T(8,128)(2,1)} fusion(bf16[2,896,1024]{1,2,0:T(8,128)(2,1)S(1)} %convert_bitcast_fusion, bf16[2,896,1024]{1,2,0:T(8,128)(2,1)S(1)} %copy-done.1), kind=kLoop, calls=%fused_computation.2 | loop fusion | flops 7340032 | bytes 11010048 | tf_op jit(solution)/shard_map/convert_element_type | solution.py:90
  215.0 6.0 %copy.66 = bf16[2,896,1024]{2,1,0:T(8,128)(2,1)} copy(bf16[2,896,1024]{1,2,0:T(8,128)(2,1)} %add_convert_fusion) | data formatting | bytes 7340032
  (43 shorter events, 3.3 us)
Async XLA Ops:
  7.2 1.5 copy-start.2
  7.2 2.7 %copy-start.3 = (s32[512,2]{0,1:T(2,128)S(1)}, s32[512,2]{0,1:T(2,128)}, u32[]{:S(2)}) copy-start(s32[512,2]{0,1:T(2,128)} %param.9) | copy-start | bytes 12292
  7.2 2.9 %copy-start.4 = (f32[512,2]{0,1:T(2,128)S(1)}, f32[512,2]{0,1:T(2,128)}, u32[]{:S(2)}) copy-start(f32[512,2]{0,1:T(2,128)} %param.8) | copy-start | bytes 12292
  7.2 53.1 %all-gather.5.cloned.1.call-start = ((), (), s32[]{:S(2)}) async-start(), calls=%async_computation.3 | async-start | bytes 2359296 | tf_op jit(solution)/shard_map/all_gather | solution.py:41
  7.9 144.4 %all-gather.7.cloned.1.call-start = ((), (), s32[]{:S(2)}) async-start(), calls=%async_computation.4 | async-start | bytes 11010048 | tf_op jit(solution)/shard_map/all_gather | solution.py:57
  12.3 71.5 %all-to-all-start = ((bf16[16,2,36]{2,1,0:T(2,128)(2,1)}), bf16[16,2,36]{2,1,0:T(2,128)(2,1)S(1)}, u32[]{:S(2)}, u32[]{:S(2)}) async-start(bf16[16,2,36]{2,1,0:T(2,128)(2,1)} %reshape.51), calls=%async_computation | async-start | bytes 16384 | tf_op jit(solution)/shard_map/all_to_all | solution.py:51
  83.8 60.4 %all-to-all-start.1 = ((bf16[16,2,36,2048]{3,1,2,0:T(2,128)(2,1)}), bf16[16,2,36,2048]{3,1,2,0:T(2,128)(2,1)}, u32[]{:S(2)}, u32[]{:S(2)}) async-start(bf16[16,2,36,2048]{3,1,2,0:T(2,128)(2,1)} %copy.62), calls=%async_computation.1 | async-start | bytes 9437184 | tf_op jit(solution)/shard_map/all_to_all | solution.py:44
  149.3 2.1 copy-start
  151.7 54.9 %collective-permute-start = (bf16[2,576,1024]{2,1,0:T(8,128)(2,1)S(1)}, bf16[2,576,1024]{2,1,0:T(8,128)(2,1)}, u32[]{:S(2)}, u32[]{:S(2)}) collective-permute-start(bf16[2,576,1024]{2,1,0:T(8,128)(2,1)S(1)} %constant_dynamic-slice_fusion), channel_id=1, source_target_pairs={{0,1},{1,0},{2,3},{3,2},{4,5},{5,4},{6,7},{7,6},{8,9},{9,8},{10,11... | collective-permute-start | bytes 7077896 | tf_op jit(solution)/shard_map/ppermute | solution.py:10
  151.8 54.7 %collective-permute-start.1 = (bf16[2,576,896]{2,1,0:T(8,128)(2,1)}, bf16[2,576,896]{2,1,0:T(8,128)(2,1)}, u32[]{:S(2)}, u32[]{:S(2)}) collective-permute-start(bf16[2,576,896]{2,1,0:T(8,128)(2,1)} %param.10), channel_id=1, source_target_pairs={{0,1},{1,0},{2,3},{3,2},{4,5},{5,4},{6,7},{7,6},{8,9},{9,8},{10,11... | collective-permute-start | bytes 6193160 | tf_op jit(solution)/shard_map/ppermute | solution.py:10
  190.0 14.7 %all-to-all-start.2 = ((f32[2,16,36]{2,0,1:T(2,128)}), f32[2,16,36]{2,0,1:T(2,128)S(1)}, u32[]{:S(2)}, u32[]{:S(2)}) async-start(f32[2,16,36]{2,0,1:T(2,128)} %copy.65), calls=%async_computation.2 | async-start | bytes 32768 | tf_op jit(solution)/shard_map/all_to_all | solution.py:64
  206.5 5.8 %copy-start.1 = (bf16[2,896,1024]{1,2,0:T(8,128)(2,1)S(1)}, bf16[2,896,1024]{1,2,0:T(8,128)(2,1)}, u32[]{:S(2)}) copy-start(bf16[2,896,1024]{1,2,0:T(8,128)(2,1)} %convert_bitcast_fusion.1) | copy-start | bytes 11010052
Sparse Core Ops, SparseCore 0:
  9.7 50.4 all-gather.4
  62.1 22.2 all-gather.6

commit v2 on v1

v2 whole, which is shorter than its diff:
```python
import jax
import jax.numpy as jnp
from jax import lax
from jax.sharding import PartitionSpec as P


def from_partner(value, axis, stride):
    mask = 2**stride
    pairs = [(source, source ^ mask) for source in range(lax.axis_size(axis))]
    return lax.ppermute(value, axis, pairs)


def tree_sum(value, axis):
    stride = 0
    while 2**stride < lax.axis_size(axis):
        value = value + from_partner(value, axis, stride)
        stride += 1
    return value


def body(out_grad, expert_ids, gate_weights, keep, hidden_act, down_weight):
    token_count = out_grad.shape[0]
    experts = lax.axis_size("expert")
    local_experts = hidden_act.shape[0]
    total_experts = experts * local_experts
    slot_count = hidden_act.shape[1]
    capacity = slot_count // experts
    places = total_experts * capacity
    chosen = expert_ids.reshape(-1)
    count = chosen.shape[0]
    onehot = chosen[:, None] == jnp.arange(total_experts, dtype=jnp.int32)[None, :]
    earlier = (
        jnp.arange(count, dtype=jnp.int32)[:, None] > jnp.arange(count, dtype=jnp.int32)[None, :]
    ).astype(jnp.bfloat16)
    ranking = jnp.dot(earlier, onehot.astype(jnp.bfloat16), preferred_element_type=jnp.float32)
    slot = jnp.sum(jnp.where(onehot, ranking, 0.0), axis=1).astype(jnp.int32)
    position = chosen * capacity + slot
    pos2 = position.reshape(token_count, 2)
    iota_p = jnp.arange(places, dtype=jnp.int32)[:, None]
    pick0 = pos2[None, :, 0] == iota_p
    pick1 = pos2[None, :, 1] == iota_p
    kept = keep.astype(jnp.float32)
    scale = (gate_weights * kept).astype(jnp.bfloat16)
    slot_scale = (
        jnp.dot(pick0.astype(jnp.bfloat16), scale[:, 0], preferred_element_type=jnp.float32)
        + jnp.dot(pick1.astype(jnp.bfloat16), scale[:, 1], preferred_element_type=jnp.float32)
    ).astype(jnp.bfloat16).reshape(experts, local_experts, capacity)
    arrived_scale = lax.all_to_all(slot_scale, "expert", split_axis=0, concat_axis=2, tiled=True)
    weight = arrived_scale.reshape(local_experts, slot_count).astype(jnp.float32)
    gathered = lax.all_gather(out_grad, "tensor", axis=1, tiled=True)
    full_weight = lax.all_gather(down_weight, "dp", axis=2, tiled=True)
    placing = (pick0 | pick1).astype(jnp.bfloat16).reshape(experts, local_experts, capacity, -1)
    half_width = gathered.shape[1] // 2
    dp_index = lax.axis_index("dp")
    grad_rows, scores_local, own_terms, peer_terms = [], [], [], []
    peer_hidden = from_partner(hidden_act, "dp", 0)
    for local in range(local_experts):
        outgoing = lax.dot_general(
            placing[:, local], gathered, (((2,), (0,)), ((), ())),
            preferred_element_type=jnp.float32,
        ).astype(jnp.bfloat16)
        routed = lax.all_to_all(
            outgoing, "expert", split_axis=0, concat_axis=0, tiled=True
        ).reshape(slot_count, -1)
        backprop = jnp.dot(routed, full_weight[local].T, preferred_element_type=jnp.float32)
        grad_rows.append((weight[local][:, None] * backprop).astype(jnp.bfloat16))
        scores_local.append(
            jnp.sum(backprop * hidden_act[local].astype(jnp.float32), axis=1)
        )
        scaled = (weight[local][:, None] * routed.astype(jnp.float32)).astype(jnp.bfloat16)
        own_cols = lax.dynamic_slice_in_dim(scaled, dp_index * half_width, half_width, 1)
        theirs = lax.dynamic_slice_in_dim(scaled, (1 - dp_index) * half_width, half_width, 1)
        peer_scaled = from_partner(theirs, "dp", 0)
        own_terms.append(
            jnp.dot(hidden_act[local].T, own_cols, preferred_element_type=jnp.float32).astype(
                jnp.bfloat16
            )
        )
        peer_terms.append(
            jnp.dot(peer_hidden[local].T, peer_scaled, preferred_element_type=jnp.float32).astype(
                jnp.bfloat16
            )
        )
    grad_hidden = jnp.stack(grad_rows)
    scores = tree_sum(jnp.stack(scores_local), "tensor")
    returned = lax.all_to_all(
        scores.reshape(local_experts, experts, capacity),
        "expert",
        split_axis=1,
        concat_axis=0,
        tiled=True,
    ).reshape(-1)
    picked = jnp.sum(
        jnp.where(position[:, None] == iota_p[None, :, 0], returned[None, :], 0.0), axis=1
    )
    gate_grad = picked.reshape(token_count, 2) * kept
    own_term, peer_term = lax.optimization_barrier((jnp.stack(own_terms), jnp.stack(peer_terms)))
    summed = own_term.astype(jnp.float32) + peer_term.astype(jnp.float32)
    grad_down = summed.astype(jnp.bfloat16)
    return (grad_down, grad_hidden, gate_grad)


def solution(mesh):
    in_specs = (
        P(("expert", "dp"), "tensor"),
        P(("expert", "dp"), None),
        P(("expert", "dp"), None),
        P(("expert", "dp"), None),
        P("expert", "dp", "tensor"),
        P("expert", "tensor", "dp"),
    )
    out_specs = (
        P("expert", "tensor", "dp"),
        P("expert", "dp", "tensor"),
        P(("expert", "dp"), None),
    )
    return jax.shard_map(body, mesh=mesh, in_specs=in_specs, out_specs=out_specs, check_vma=False)
```

time: 228 us -> 210 us (0.921)
  blocking collectives: 24.7 us -> 0 us
  starting transfers between devices: 22.7 us -> 34.7 us
  local copies, waits for them, and re-layouts: 29.9 us -> 21.1 us
    all_gather x1 -> x0, blocking collectives: 24.7 us -> none  [body(): lax.all_gather(partial_score, 'tensor', axis=0, tiled=False)]
    reshape x2, local copies, waits for them, and re-layouts: 17.8 us -> 4.76 us  [body(): routed = lax.all_to_all(outgoing, 'expert', split_axis=0, concat_axis=0,...]
    all_to_all x1 -> x2, starting transfers between devices: 7.27 us -> 14.3 us  [body(): lax.all_to_all(outgoing, 'expert', split_axis=0, concat_axis=0, tiled=True)]
    ppermute x2 -> x6, starting transfers between devices: 0.59 us -> 6.61 us  [from_partner(): return lax.ppermute(value, axis, pairs)]
    all_to_all x1 -> x2, waiting for transfers between devices: 53 us -> 47.2 us  [body(): lax.all_to_all(outgoing, 'expert', split_axis=0, concat_axis=0, tiled=True)]
    all_to_all x1, waiting for transfers between devices: 0.01 us -> 4.76 us  [body(): lax.all_to_all(scores.reshape(local_experts, experts, capacity), 'expert'...]
    another operation x0 -> x4, other arithmetic: none -> 4.1 us  [the longest x1 2.2 us: body(): jnp.stack(own_terms)]
    ppermute x2 -> x6, waiting for transfers between devices: 0.01 us -> 2.82 us  [from_partner(): return lax.ppermute(value, axis, pairs)]
  transfers between devices with their start and end apart: 7 -> 12, of which waited for: 2 -> 5; matrix products, arithmetic and copies ran while one was open for 24% -> 27% of each run, Pallas kernels for 0% -> 0%
where the time goes in v2:
time: 210 us; the launch traced here: 209 us
  waiting for transfers between devices  96.1 us (46%)
  starting transfers between devices  34.7 us (17%)
  matrix products  32.4 us (15%)
  local copies, waits for them, and re-layouts  21.1 us (10%)
  between operations  14.4 us (7%)
  other arithmetic  10.7 us (5%)
    all_to_all x2, waiting for transfers between devices, body(): lax.all_to_all(outgoing, 'expert', split_axis=0, concat_axis=0, tiled=True)  47.2 us
    all_gather x1, waiting for transfers between devices, body(): gathered = lax.all_gather(out_grad, 'tensor', axis=1, tiled=True)  40 us
    all_to_all x2, starting transfers between devices, body(): lax.all_to_all(outgoing, 'expert', split_axis=0, concat_axis=0, tiled=True)  14.3 us
    unnamed x33, local copies, waits for them, and re-layouts  11.5 us
    dot_general x2, matrix products, body(): jnp.dot(routed, full_weight[local].T, preferred_element_type=jnp.float32)  9.64 us
    dot_general x2, matrix products, body(): lax.dot_general(placing[:, local], gathered, (((2,), (0,)), ((), ())), pr...  9.63 us
    dot_general x2, matrix products, body(): jnp.dot(peer_hidden[local].T, peer_scaled, preferred_element_type=jnp.flo...  7.94 us
    all_to_all x1, starting transfers between devices, body(): lax.all_to_all(slot_scale, 'expert', split_axis=0, concat_axis=2, tiled=T...  7.48 us
  transfers between devices with their start and end apart: 12, of which 5 were waited for; matrix products, arithmetic and copies ran while one was open for 27% of the time, Pallas kernels for 0%

profile of v2, /device:TPU:2, one launch (start us, length us, event | category | flops | bytes accessed | tf_op | source)
XLA Modules:
  0.0 209.4 jit_solution(2179579726093566830)
XLA Ops:
  12.3 7.5 %all-to-all-start = ((bf16[16,2,36]{2,1,0:T(2,128)(2,1)}), bf16[16,2,36]{2,1,0:T(2,128)(2,1)S(1)}, u32[]{:S(2)}, u32[]{:S(2)}) async-start(bf16[16,2,36]{2,1,0:T(2,128)(2,1)} %reshape.77), calls=%async_computation | async-start | bytes 16384 | tf_op jit(solution)/shard_map/all_to_all | solution.py:48
  20.3 40.0 %all-gather.3.cloned.1.call-done = bf16[512,2048]{1,0:T(8,128)(2,1)} async-done(((bf16[512,256]{1,0:T(8,128)(2,1)}), bf16[512,2048]{1,0:T(8,128)(2,1)}) %all-gather.3.cloned.1.call-update) | async-done | bytes 2097168 | tf_op jit(solution)/shard_map/all_gather | solution.py:50
  60.2 4.7 %convolution_convert_fusion.1 = bf16[16,36,2048]{2,1,0:T(8,128)(2,1)} fusion(bf16[512,2048]{1,0:T(8,128)(2,1)} %all-gather.3.cloned.1.call-done, pred[16,2,36,512]{3,2,0,1:T(8,128)(4,1)S(1)} %compare_or_fusion), kind=kOutput, calls=%fused_computation.14 | convolution fusion | flops 1209139200 | bytes 4784128 | tf_op jit(solution)/shard_map/dot_general | solution.py:58
  64.9 7.3 %all-to-all-start.1 = ((bf16[16,36,2048]{2,1,0:T(8,128)(2,1)}), bf16[16,36,2048]{2,1,0:T(8,128)(2,1)S(1)}, u32[]{:S(2)}, u32[]{:S(2)}) async-start(bf16[16,36,2048]{2,1,0:T(8,128)(2,1)} %convolution_convert_fusion.1), calls=%async_computation.1 | async-start | bytes 5242880 | tf_op jit(solution)/shard_map/all_to_all | solution.py:62
  72.2 5.0 %convolution_convert_fusion = bf16[16,36,2048]{2,1,0:T(8,128)(2,1)} fusion(bf16[512,2048]{1,0:T(8,128)(2,1)} %all-gather.3.cloned.1.call-done, pred[16,2,36,512]{3,2,0,1:T(8,128)(4,1)S(1)} %compare_or_fusion), kind=kOutput, calls=%fused_computation.13 | convolution fusion | flops 1209139200 | bytes 4784128 | tf_op jit(solution)/shard_map/dot_general | solution.py:58
  77.1 24.8 %all-to-all-done.1 = bf16[16,36,2048]{2,1,0:T(8,128)(2,1)S(1)} async-done(((bf16[16,36,2048]{2,1,0:T(8,128)(2,1)}), bf16[16,36,2048]{2,1,0:T(8,128)(2,1)S(1)}, u32[]{:S(2)}, u32[]{:S(2)}) %all-to-all-start.1) | async-done | bytes 2359328 | tf_op jit(solution)/shard_map/all_to_all | solution.py:62
  101.9 7.1 %all-to-all-start.2 = ((bf16[16,36,2048]{2,1,0:T(8,128)(2,1)}), bf16[16,36,2048]{2,1,0:T(8,128)(2,1)}, u32[]{:S(2)}, u32[]{:S(2)}) async-start(bf16[16,36,2048]{2,1,0:T(8,128)(2,1)} %convolution_convert_fusion), calls=%async_computation.2 | async-start | bytes 5242880 | tf_op jit(solution)/shard_map/all_to_all | solution.py:62
  109.3 2.1 %reshape.78 = bf16[576,2048]{1,0:T(8,128)(2,1)} reshape(bf16[16,36,2048]{2,1,0:T(8,128)(2,1)S(1)} %all-to-all-done.1) | data formatting | bytes 4718592 | tf_op jit(solution)/shard_map/reshape | solution.py:64
  111.4 2.1 %multiply_convert_fusion.1 = bf16[576,2048]{1,0:T(8,128)(2,1)S(1)} fusion(bf16[576,2048]{1,0:T(8,128)(2,1)} %reshape.78, f32[576]{0:T(1024)S(1)} %mul.74), kind=kLoop, calls=%fused_computation.4 | loop fusion | flops 3538944 | bytes 4720896 | tf_op jit(solution)/shard_map/convert_element_type | solution.py:70
  116.5 22.4 %all-to-all-done.2 = bf16[16,36,2048]{2,1,0:T(8,128)(2,1)} async-done(((bf16[16,36,2048]{2,1,0:T(8,128)(2,1)}), bf16[16,36,2048]{2,1,0:T(8,128)(2,1)}, u32[]{:S(2)}, u32[]{:S(2)}) %all-to-all-start.2) | async-done | bytes 2359328 | tf_op jit(solution)/shard_map/all_to_all | solution.py:62
  138.9 2.7 %reshape.79 = bf16[576,2048]{1,0:T(8,128)(2,1)S(1)} reshape(bf16[16,36,2048]{2,1,0:T(8,128)(2,1)} %all-to-all-done.2) | data formatting | bytes 4718592 | tf_op jit(solution)/shard_map/reshape | solution.py:64
  145.3 1.8 convert_bitcast_fusion.3
  147.1 1.8 convert_bitcast_fusion.2
  148.9 2.2 %pad_maximum_fusion = bf16[2,896,1024]{1,2,0:T(8,128)(2,1)} fusion(bf16[1,896,1024]{1,2,0:T(8,128)(2,1)S(1)} %convert_bitcast_fusion.2, bf16[1,896,1024]{1,2,0:T(8,128)(2,1)S(1)} %convert_bitcast_fusion.3), kind=kLoop, calls=%fused_computation.11 | loop fusion | flops 1835008 | bytes 7340032 | tf_op jit(solution)/shard_map/stack | solution.py:97
  151.1 4.6 %convert_bitcast_fusion.1 = bf16[1,896,1024]{1,2,0:T(8,128)(2,1)} fusion(bf16[576,1024]{1,0:T(8,128)(2,1)} %collective-permute-done, bf16[2,576,896]{2,1,0:T(8,128)(2,1)} %collective-permute-done.1), kind=kOutput, calls=%fused_computation.28 | convolution fusion | flops 1057882112 | bytes 4046848 | tf_op jit(solution)/shard_map/dot_general | solution.py:80
  155.8 5.5 %fusion.1 = f32[576,896]{1,0:T(8,128)S(1)} fusion(bf16[576,2048]{1,0:T(8,128)(2,1)} %copy-done.2, bf16[2,896,2048]{2,1,0:T(8,128)(2,1)} %all-gather.5.cloned.1.call-done), kind=kOutput, calls=%fused_computation.8 | convolution fusion | flops 2113929216 | bytes 8093696 | tf_op jit(solution)/shard_map/dot_general | solution.py:65
  161.9 4.1 %multiply_reduce_fusion.1 = (f32[576]{0:T(1024)S(1)}, f32[576]{0:T(1024)S(1)}, bf16[1,576,896]{2,1,0:T(8,128)(2,1)}, bf16[1,576,896]{2,1,0:T(8,128)(2,1)}) fusion(bf16[2,576,896]{2,1,0:T(8,128)(2,1)S(1)} %copy-done.13, f32[576,896]{1,0:T(8,128)S(1)} %fusion.1, f32[576]{0:T(1024)S(1)} %mul.78, f32[576]{0:T(1024)S(1)} %mul.74, ...), kind=kOutput, calls=%fused_computation.24 | convolution fusion | flops 2119089152 | bytes 12235264 | tf_op jit(solution)/shard_map/dot_general | solution.py:65
  167.4 3.4 %convert_bitcast_fusion = bf16[1,896,1024]{1,2,0:T(8,128)(2,1)S(1)} fusion(bf16[576,1024]{1,0:T(8,128)(2,1)} %collective-permute-done.2, bf16[2,576,896]{2,1,0:T(8,128)(2,1)} %collective-permute-done.1), kind=kOutput, calls=%fused_computation.27 | convolution fusion | flops 1057882112 | bytes 4046848 | tf_op jit(solution)/shard_map/dot_general | solution.py:80
  172.6 2.8 %collective-permute-done.4 = f32[2,576]{1,0:T(2,128)S(1)} collective-permute-done((f32[2,576]{1,0:T(2,128)S(1)}, f32[2,576]{1,0:T(2,128)S(1)}, u32[]{:S(2)}, u32[]{:S(2)}) %collective-permute-start.4) | collective-permute-done | bytes 4640 | tf_op jit(solution)/shard_map/ppermute | solution.py:10
  175.4 3.4 %collective-permute-start.5 = (f32[2,576]{1,0:T(2,128)S(1)}, f32[2,576]{1,0:T(2,128)S(1)}, u32[]{:S(2)}, u32[]{:S(2)}) collective-permute-start(f32[2,576]{1,0:T(2,128)S(1)} %fusion.32), channel_id=1, source_target_pairs={{0,8},{2,10},{4,12},{6,14},{8,0},{10,2},{12,4},{14,6},{1,9},{3,11}... | collective-permute-start | bytes 13832 | tf_op jit(solution)/shard_map/ppermute | solution.py:10
  178.8 2.7 %add_convert_fusion = bf16[2,896,1024]{1,2,0:T(8,128)(2,1)} fusion(bf16[2,896,1024]{1,2,0:T(8,128)(2,1)S(1)} %pad_maximum_fusion.1, bf16[2,896,1024]{1,2,0:T(8,128)(2,1)S(1)} %copy-done), kind=kLoop, calls=%fused_computation | loop fusion | flops 7340032 | bytes 11010048 | tf_op jit(solution)/shard_map/convert_element_type | solution.py:99
  181.4 6.1 %copy.46 = bf16[2,896,1024]{2,1,0:T(8,128)(2,1)} copy(bf16[2,896,1024]{1,2,0:T(8,128)(2,1)} %add_convert_fusion) | data formatting | bytes 7340032
  188.3 6.2 %all-to-all-start.3 = ((f32[2,16,36]{2,0,1:T(2,128)}), f32[2,16,36]{2,0,1:T(2,128)S(1)}, u32[]{:S(2)}, u32[]{:S(2)}) async-start(f32[2,16,36]{2,0,1:T(2,128)} %copy.45), calls=%async_computation.3 | async-start | bytes 32768 | tf_op jit(solution)/shard_map/all_to_all | solution.py:86
  196.0 4.8 %all-to-all-done.3 = f32[2,16,36]{2,0,1:T(2,128)S(1)} async-done(((f32[2,16,36]{2,0,1:T(2,128)}), f32[2,16,36]{2,0,1:T(2,128)S(1)}, u32[]{:S(2)}, u32[]{:S(2)}) %all-to-all-start.3) | async-done | bytes 4640 | tf_op jit(solution)/shard_map/all_to_all | solution.py:86
  (87 shorter events, 20.2 us)
Async XLA Ops:
  7.2 1.5 copy-start.8
  7.2 53.1 %all-gather.3.cloned.1.call-start = ((), (), s32[]{:S(2)}) async-start(), calls=%async_computation.4 | async-start | bytes 2359296 | tf_op jit(solution)/shard_map/all_gather | solution.py:50
  7.9 2.0 copy-start.9
  7.9 2.2 %copy-start.10 = (f32[512,2]{0,1:T(2,128)S(1)}, f32[512,2]{0,1:T(2,128)}, u32[]{:S(2)}) copy-start(f32[512,2]{0,1:T(2,128)} %param.8) | copy-start | bytes 12292
  7.9 147.8 %all-gather.5.cloned.1.call-start = ((), (), s32[]{:S(2)}) async-start(), calls=%async_computation.5 | async-start | bytes 11010048 | tf_op jit(solution)/shard_map/all_gather | solution.py:51
  12.3 52.6 %all-to-all-start = ((bf16[16,2,36]{2,1,0:T(2,128)(2,1)}), bf16[16,2,36]{2,1,0:T(2,128)(2,1)S(1)}, u32[]{:S(2)}, u32[]{:S(2)}) async-start(bf16[16,2,36]{2,1,0:T(2,128)(2,1)} %reshape.77), calls=%async_computation | async-start | bytes 16384 | tf_op jit(solution)/shard_map/all_to_all | solution.py:48
  64.9 37.0 %all-to-all-start.1 = ((bf16[16,36,2048]{2,1,0:T(8,128)(2,1)}), bf16[16,36,2048]{2,1,0:T(8,128)(2,1)S(1)}, u32[]{:S(2)}, u32[]{:S(2)}) async-start(bf16[16,36,2048]{2,1,0:T(8,128)(2,1)} %convolution_convert_fusion.1), calls=%async_computation.1 | async-start | bytes 5242880 | tf_op jit(solution)/shard_map/all_to_all | solution.py:62
  101.9 37.0 %all-to-all-start.2 = ((bf16[16,36,2048]{2,1,0:T(8,128)(2,1)}), bf16[16,36,2048]{2,1,0:T(8,128)(2,1)}, u32[]{:S(2)}, u32[]{:S(2)}) async-start(bf16[16,36,2048]{2,1,0:T(8,128)(2,1)} %convolution_convert_fusion), calls=%async_computation.2 | async-start | bytes 5242880 | tf_op jit(solution)/shard_map/all_to_all | solution.py:62
  109.0 42.2 %collective-permute-start.1 = (bf16[2,576,896]{2,1,0:T(8,128)(2,1)}, bf16[2,576,896]{2,1,0:T(8,128)(2,1)}, u32[]{:S(2)}, u32[]{:S(2)}) collective-permute-start(bf16[2,576,896]{2,1,0:T(8,128)(2,1)} %param.10), channel_id=1, source_target_pairs={{0,1},{1,0},{2,3},{3,2},{4,5},{5,4},{6,7},{7,6},{8,9},{9,8},{10,11... | collective-permute-start | bytes 6193160 | tf_op jit(solution)/shard_map/ppermute | solution.py:10
  116.0 35.1 %collective-permute-start = (bf16[576,1024]{1,0:T(8,128)(2,1)}, bf16[576,1024]{1,0:T(8,128)(2,1)}, u32[]{:S(2)}, u32[]{:S(2)}) collective-permute-start(bf16[576,1024]{1,0:T(8,128)(2,1)} %constant_dynamic-slice_fusion.1), channel_id=1, source_target_pairs={{0,1},{1,0},{2,3},{3,2},{4,5},{5,4},{6,7},{7,6},{8,9},{9,8},{10,11... | collective-permute-start | bytes 3538952 | tf_op jit(solution)/shard_map/ppermute | solution.py:10
  141.6 2.6 %copy-start.12 = (bf16[2,576,896]{2,1,0:T(8,128)(2,1)S(1)}, bf16[2,576,896]{2,1,0:T(8,128)(2,1)}, u32[]{:S(2)}) copy-start(bf16[2,576,896]{2,1,0:T(8,128)(2,1)} %param.10) | copy-start | bytes 6193156
  143.1 2.3 %copy-start.4 = (bf16[576,2048]{1,0:T(8,128)(2,1)S(1)}, bf16[576,2048]{1,0:T(8,128)(2,1)}, u32[]{:S(2)}) copy-start(bf16[576,2048]{1,0:T(8,128)(2,1)} %copy-done.3) | copy-start | bytes 7077892
  144.2 23.2 %collective-permute-start.2 = (bf16[576,1024]{1,0:T(8,128)(2,1)}, bf16[576,1024]{1,0:T(8,128)(2,1)}, u32[]{:S(2)}, u32[]{:S(2)}) collective-permute-start(bf16[576,1024]{1,0:T(8,128)(2,1)} %constant_dynamic-slice_fusion), channel_id=1, source_target_pairs={{0,1},{1,0},{2,3},{3,2},{4,5},{5,4},{6,7},{7,6},{8,9},{9,8},{10,11... | collective-permute-start | bytes 3538952 | tf_op jit(solution)/shard_map/ppermute | solution.py:10
  155.7 5.5 %copy-start.1 = (bf16[576,2048]{1,0:T(8,128)(2,1)S(1)}, bf16[576,2048]{1,0:T(8,128)(2,1)}, u32[]{:S(2)}) copy-start(bf16[576,2048]{1,0:T(8,128)(2,1)} %reshape.78) | copy-start | bytes 7077892
  155.7 5.6 %copy-start.11 = (bf16[2,896,2048]{2,1,0:T(8,128)(2,1)S(1)}, bf16[2,896,2048]{2,1,0:T(8,128)(2,1)}, u32[]{:S(2)}) copy-start(bf16[2,896,2048]{2,1,0:T(8,128)(2,1)} %all-gather.5.cloned.1.call-done) | copy-start | bytes 22020100
  155.7 6.2 %copy-start.13 = (bf16[2,576,896]{2,1,0:T(8,128)(2,1)S(1)}, bf16[2,576,896]{2,1,0:T(8,128)(2,1)}, u32[]{:S(2)}) copy-start(bf16[2,576,896]{2,1,0:T(8,128)(2,1)} %param.10) | copy-start | bytes 6193156
  166.0 6.2 %copy-start.5 = (bf16[1,896,1024]{1,2,0:T(8,128)(2,1)S(1)}, bf16[1,896,1024]{1,2,0:T(8,128)(2,1)}, u32[]{:S(2)}) copy-start(bf16[1,896,1024]{1,2,0:T(8,128)(2,1)} %convert_bitcast_fusion.1) | copy-start | bytes 5505028
  166.0 4.7 %collective-permute-start.3 = (f32[2,576]{1,0:T(2,128)S(1)}, f32[2,576]{1,0:T(2,128)S(1)}, u32[]{:S(2)}, u32[]{:S(2)}) collective-permute-start(f32[2,576]{1,0:T(2,128)S(1)} %pad_maximum_fusion.3), channel_id=1, source_target_pairs={{0,2},{2,0},{4,6},{6,4},{8,10},{10,8},{12,14},{14,12},{1,3},{3,1},... | collective-permute-start | bytes 13832 | tf_op jit(solution)/shard_map/ppermute | solution.py:10
  170.8 8.0 %copy-start = (bf16[2,896,1024]{1,2,0:T(8,128)(2,1)S(1)}, bf16[2,896,1024]{1,2,0:T(8,128)(2,1)}, u32[]{:S(2)}) copy-start(bf16[2,896,1024]{1,2,0:T(8,128)(2,1)} %pad_maximum_fusion) | copy-start | bytes 11010052
  170.8 4.6 %collective-permute-start.4 = (f32[2,576]{1,0:T(2,128)S(1)}, f32[2,576]{1,0:T(2,128)S(1)}, u32[]{:S(2)}, u32[]{:S(2)}) collective-permute-start(f32[2,576]{1,0:T(2,128)S(1)} %fusion.24), channel_id=1, source_target_pairs={{0,4},{2,6},{4,0},{6,2},{8,12},{10,14},{12,8},{14,10},{1,5},{3,7},... | collective-permute-start | bytes 13832 | tf_op jit(solution)/shard_map/ppermute | solution.py:10
  175.4 12.2 %collective-permute-start.5 = (f32[2,576]{1,0:T(2,128)S(1)}, f32[2,576]{1,0:T(2,128)S(1)}, u32[]{:S(2)}, u32[]{:S(2)}) collective-permute-start(f32[2,576]{1,0:T(2,128)S(1)} %fusion.32), channel_id=1, source_target_pairs={{0,8},{2,10},{4,12},{6,14},{8,0},{10,2},{12,4},{14,6},{1,9},{3,11}... | collective-permute-start | bytes 13832 | tf_op jit(solution)/shard_map/ppermute | solution.py:10
  181.4 13.0 %copy-start.6 = (bf16[1,576,896]{2,1,0:T(8,128)(2,1)S(1)}, bf16[1,576,896]{2,1,0:T(8,128)(2,1)}, u32[]{:S(2)}) copy-start(bf16[1,576,896]{2,1,0:T(8,128)(2,1)} %get-tuple-element.31) | copy-start | bytes 3096580
  181.4 13.0 %copy-start.7 = (bf16[1,576,896]{2,1,0:T(8,128)(2,1)S(1)}, bf16[1,576,896]{2,1,0:T(8,128)(2,1)}, u32[]{:S(2)}) copy-start(bf16[1,576,896]{2,1,0:T(8,128)(2,1)} %get-tuple-element.32) | copy-start | bytes 3096580
  188.3 12.5 %all-to-all-start.3 = ((f32[2,16,36]{2,0,1:T(2,128)}), f32[2,16,36]{2,0,1:T(2,128)S(1)}, u32[]{:S(2)}, u32[]{:S(2)}) async-start(f32[2,16,36]{2,0,1:T(2,128)} %copy.45), calls=%async_computation.3 | async-start | bytes 32768 | tf_op jit(solution)/shard_map/all_to_all | solution.py:86
  (2 other events, 2.9 us)
Sparse Core Ops, SparseCore 0:
  9.7 50.4 all-gather.2
  62.0 22.2 all-gather.4

commit v3 on v2

--- a/solution.py
+++ b/solution.py
@@ -17,6 +17,26 @@
         stride += 1
     return value
 
+
+def ring_gather(value, axis):
+    size = lax.axis_size(axis)
+    index = lax.axis_index(axis)
+    right = [(source, (source + 1) % size) for source in range(size)]
+    left = [(source, (source - 1) % size) for source in range(size)]
+    gathered = jnp.zeros((size,) + value.shape, value.dtype)
+    gathered = lax.dynamic_update_index_in_dim(gathered, value, index, 0)
+    going_right = going_left = value
+    for step in range(1, size // 2 + 1):
+        going_right = lax.ppermute(going_right, axis, right)
+        gathered = lax.dynamic_update_index_in_dim(
+            gathered, going_right, (index + size - step) % size, 0
+        )
+        if step < size - size // 2:
+            going_left = lax.ppermute(going_left, axis, left)
+            gathered = lax.dynamic_update_index_in_dim(
+                gathered, going_left, (index + step) % size, 0
+            )
+    return gathered
 
 def body(out_grad, expert_ids, gate_weights, keep, hidden_act, down_weight):
     token_count = out_grad.shape[0]
@@ -47,18 +67,18 @@
     ).astype(jnp.bfloat16).reshape(experts, local_experts, capacity)
     arrived_scale = lax.all_to_all(slot_scale, "expert", split_axis=0, concat_axis=2, tiled=True)
     weight = arrived_scale.reshape(local_experts, slot_count).astype(jnp.float32)
-    gathered = lax.all_gather(out_grad, "tensor", axis=1, tiled=True)
+    gathered = ring_gather(out_grad, "tensor")
     full_weight = lax.all_gather(down_weight, "dp", axis=2, tiled=True)
     placing = (pick0 | pick1).astype(jnp.bfloat16).reshape(experts, local_experts, capacity, -1)
-    half_width = gathered.shape[1] // 2
+    half_width = gathered.shape[0] * gathered.shape[2] // 2
     dp_index = lax.axis_index("dp")
     grad_rows, scores_local, own_terms, peer_terms = [], [], [], []
     peer_hidden = from_partner(hidden_act, "dp", 0)
     for local in range(local_experts):
         outgoing = lax.dot_general(
-            placing[:, local], gathered, (((2,), (0,)), ((), ())),
+            placing[:, local], gathered, (((2,), (1,)), ((), ())),
             preferred_element_type=jnp.float32,
-        ).astype(jnp.bfloat16)
+        ).astype(jnp.bfloat16).reshape(experts, capacity, -1)
         routed = lax.all_to_all(
             outgoing, "expert", split_axis=0, concat_axis=0, tiled=True
         ).reshape(slot_count, -1)

time: 210 us -> 202 us (0.962)
  waiting for transfers between devices: 96.1 us -> 66.8 us
  local copies, waits for them, and re-layouts: 21.1 us -> 33.6 us
  starting transfers between devices: 34.7 us -> 47.1 us
  matrix products: 32.4 us -> 27.6 us
    all_gather x1 -> x0, waiting for transfers between devices: 40 us -> none  [body(): gathered = lax.all_gather(out_grad, 'tensor', axis=1, tiled=True)]
    ppermute x0 -> x7, waiting for transfers between devices: none -> 16.1 us  [the longest x4 16.1 us: ring_gather(): going_right = lax.ppermute(going_right, axis, right)]
    ppermute x0 -> x7, starting transfers between devices: none -> 12.6 us  [the longest x3 10.5 us: ring_gather(): going_left = lax.ppermute(going_left, axis, left)]
    reshape x0 -> x4, local copies, waits for them, and re-layouts: none -> 9.85 us  [body(): outgoing = lax.dot_general(placing[:, local], gathered, (((2,), (1,)), ((...]
    dot_general x2, matrix products: 9.63 us -> 4.63 us  [body(): lax.dot_general(placing[:, local], gathered, (((2,), (1,)), ((), ())), pr...]
    all_to_all x2, waiting for transfers between devices: 47.2 us -> 43.1 us  [body(): lax.all_to_all(outgoing, 'expert', split_axis=0, concat_axis=0, tiled=True)]
    unnamed x33 -> x41, local copies, waits for them, and re-layouts: 11.5 us -> 12.8 us
  transfers between devices with their start and end apart: 12 -> 18, of which waited for: 5 -> 8; matrix products, arithmetic and copies ran while one was open for 27% -> 32% of each run, Pallas kernels for 0% -> 0%
where the time goes in v3:
time: 202 us; the launch traced here: 201 us
  waiting for transfers between devices  66.8 us (33%)
  starting transfers between devices  47.1 us (23%)
  local copies, waits for them, and re-layouts  33.6 us (17%)
  matrix products  27.6 us (14%)
  between operations  14.7 us (7%)
  other arithmetic  11.4 us (6%)
    all_to_all x2, waiting for transfers between devices, body(): lax.all_to_all(outgoing, 'expert', split_axis=0, concat_axis=0, tiled=True)  43.1 us
    ppermute x4, waiting for transfers between devices, ring_gather(): going_right = lax.ppermute(going_right, axis, right)  16.1 us
    all_to_all x2, starting transfers between devices, body(): lax.all_to_all(outgoing, 'expert', split_axis=0, concat_axis=0, tiled=True)  14.6 us
    unnamed x41, local copies, waits for them, and re-layouts  12.8 us
    ppermute x3, starting transfers between devices, ring_gather(): going_left = lax.ppermute(going_left, axis, left)  10.5 us
    reshape x4, local copies, waits for them, and re-layouts, body(): outgoing = lax.dot_general(placing[:, local], gathered, (((2,), (1,)), ((...  9.85 us
    dot_general x2, matrix products, body(): jnp.dot(routed, full_weight[local].T, preferred_element_type=jnp.float32)  9.66 us
    dot_general x2, matrix products, body(): jnp.dot(peer_hidden[local].T, peer_scaled, preferred_element_type=jnp.flo...  8.11 us
  transfers between devices with their start and end apart: 18, of which 8 were waited for; matrix products, arithmetic and copies ran while one was open for 32% of the time, Pallas kernels for 0%

profile of v3, /device:TPU:2, one launch (start us, length us, event | category | flops | bytes accessed | tf_op | source)
XLA Modules:
  0.0 201.2 jit_solution(7725304929216622920)
XLA Ops:
  9.2 4.0 %collective-permute-start.1 = (bf16[512,256]{1,0:T(8,128)(2,1)}, bf16[512,256]{1,0:T(8,128)(2,1)S(1)}, u32[]{:S(2)}, u32[]{:S(2)}) collective-permute-start(bf16[512,256]{1,0:T(8,128)(2,1)} %param.6), channel_id=1, source_target_pairs={{0,14},{2,0},{4,2},{6,4},{8,6},{10,8},{12,10},{14,12},{1,15},{3,1}... | collective-permute-start | bytes 786440 | tf_op jit(solution)/shard_map/ppermute | solution.py:35
  16.9 7.5 %all-to-all-start = ((bf16[16,2,36]{2,1,0:T(2,128)(2,1)}), bf16[16,2,36]{2,1,0:T(2,128)(2,1)S(1)}, u32[]{:S(2)}, u32[]{:S(2)}) async-start(bf16[16,2,36]{2,1,0:T(2,128)(2,1)} %reshape.83), calls=%async_computation | async-start | bytes 16384 | tf_op jit(solution)/shard_map/all_to_all | solution.py:68
  26.0 3.2 %collective-permute-start.3 = (bf16[512,256]{1,0:T(8,128)(2,1)S(1)}, bf16[512,256]{1,0:T(8,128)(2,1)S(1)}, u32[]{:S(2)}, u32[]{:S(2)}) collective-permute-start(bf16[512,256]{1,0:T(8,128)(2,1)S(1)} %collective-permute-done.1), channel_id=1, source_target_pairs={{0,14},{2,0},{4,2},{6,4},{8,6},{10,8},{12,10},{14,12},{1,15},{3,1}... | collective-permute-start | bytes 786440 | tf_op jit(solution)/shard_map/ppermute | solution.py:35
  30.3 4.3 %collective-permute-done.2 = bf16[512,256]{1,0:T(8,128)(2,1)S(1)} collective-permute-done((bf16[512,256]{1,0:T(8,128)(2,1)}, bf16[512,256]{1,0:T(8,128)(2,1)S(1)}, u32[]{:S(2)}, u32[]{:S(2)}) %collective-permute-start.2) | collective-permute-done | bytes 262176 | tf_op jit(solution)/shard_map/ppermute | solution.py:30
  34.6 3.2 %collective-permute-start.5 = (bf16[512,256]{1,0:T(8,128)(2,1)S(1)}, bf16[512,256]{1,0:T(8,128)(2,1)S(1)}, u32[]{:S(2)}, u32[]{:S(2)}) collective-permute-start(bf16[512,256]{1,0:T(8,128)(2,1)S(1)} %collective-permute-done.3), channel_id=1, source_target_pairs={{0,14},{2,0},{4,2},{6,4},{8,6},{10,8},{12,10},{14,12},{1,15},{3,1}... | collective-permute-start | bytes 786440 | tf_op jit(solution)/shard_map/ppermute | solution.py:35
  37.9 4.3 %collective-permute-done.4 = bf16[512,256]{1,0:T(8,128)(2,1)S(1)} collective-permute-done((bf16[512,256]{1,0:T(8,128)(2,1)S(1)}, bf16[512,256]{1,0:T(8,128)(2,1)S(1)}, u32[]{:S(2)}, u32[]{:S(2)}) %collective-permute-start.4) | collective-permute-done | bytes 262176 | tf_op jit(solution)/shard_map/ppermute | solution.py:30
  42.3 7.5 %collective-permute-done.6 = bf16[512,256]{1,0:T(8,128)(2,1)S(1)} collective-permute-done((bf16[512,256]{1,0:T(8,128)(2,1)S(1)}, bf16[512,256]{1,0:T(8,128)(2,1)S(1)}, u32[]{:S(2)}, u32[]{:S(2)}) %collective-permute-start.6) | collective-permute-done | bytes 262176 | tf_op jit(solution)/shard_map/ppermute | solution.py:30
  53.3 2.7 %reshape.100 = bf16[16,36,2048]{2,1,0:T(8,128)(2,1)} reshape(bf16[16,36,8,256]{3,2,1,0:T(8,128)(2,1)S(1)} %copy.70) | data formatting | bytes 4718592 | tf_op jit(solution)/shard_map/reshape | solution.py:81
  56.0 7.2 %all-to-all-start.1 = ((bf16[16,36,2048]{2,1,0:T(8,128)(2,1)}), bf16[16,36,2048]{2,1,0:T(8,128)(2,1)S(1)}, u32[]{:S(2)}, u32[]{:S(2)}) async-start(bf16[16,36,2048]{2,1,0:T(8,128)(2,1)} %reshape.100), calls=%async_computation.1 | async-start | bytes 5242880 | tf_op jit(solution)/shard_map/all_to_all | solution.py:82
  63.3 3.1 %fusion.12 = bf16[16,36,8,256]{3,1,2,0:T(8,128)(2,1)S(1)} fusion(bf16[8,512,256]{2,1,0:T(8,128)(2,1)} %copy-done.5, pred[16,2,36,512]{3,2,0,1:T(8,128)(4,1)S(1)} %compare_or_fusion), kind=kOutput, calls=%fused_computation.23 | convolution fusion | flops 1209139200 | bytes 4784128 | tf_op jit(solution)/shard_map/dot_general | solution.py:78
  68.4 4.5 %reshape.101 = bf16[16,36,2048]{2,1,0:T(8,128)(2,1)} reshape(bf16[16,36,8,256]{3,2,1,0:T(8,128)(2,1)} %copy.71) | data formatting | bytes 4718592 | tf_op jit(solution)/shard_map/reshape | solution.py:81
  72.9 20.1 %all-to-all-done.1 = bf16[16,36,2048]{2,1,0:T(8,128)(2,1)S(1)} async-done(((bf16[16,36,2048]{2,1,0:T(8,128)(2,1)}), bf16[16,36,2048]{2,1,0:T(8,128)(2,1)S(1)}, u32[]{:S(2)}, u32[]{:S(2)}) %all-to-all-start.1) | async-done | bytes 2359328 | tf_op jit(solution)/shard_map/all_to_all | solution.py:82
  93.0 7.4 %all-to-all-start.2 = ((bf16[16,36,2048]{2,1,0:T(8,128)(2,1)}), bf16[16,36,2048]{2,1,0:T(8,128)(2,1)}, u32[]{:S(2)}, u32[]{:S(2)}) async-start(bf16[16,36,2048]{2,1,0:T(8,128)(2,1)} %reshape.101), calls=%async_computation.2 | async-start | bytes 5242880 | tf_op jit(solution)/shard_map/all_to_all | solution.py:82
  107.9 23.0 %all-to-all-done.2 = bf16[16,36,2048]{2,1,0:T(8,128)(2,1)} async-done(((bf16[16,36,2048]{2,1,0:T(8,128)(2,1)}), bf16[16,36,2048]{2,1,0:T(8,128)(2,1)}, u32[]{:S(2)}, u32[]{:S(2)}) %all-to-all-start.2) | async-done | bytes 2359328 | tf_op jit(solution)/shard_map/all_to_all | solution.py:82
  143.1 4.6 %convert_bitcast_fusion.1 = bf16[1,896,1024]{1,2,0:T(8,128)(2,1)} fusion(bf16[576,1024]{1,0:T(8,128)(2,1)} %collective-permute-done.7, bf16[2,576,896]{2,1,0:T(8,128)(2,1)} %collective-permute-done.8), kind=kOutput, calls=%fused_computation.30 | convolution fusion | flops 1057882112 | bytes 4046848 | tf_op jit(solution)/shard_map/dot_general | solution.py:100
  147.8 5.5 %fusion.1 = f32[576,896]{1,0:T(8,128)S(1)} fusion(bf16[576,2048]{1,0:T(8,128)(2,1)} %copy-done.2, bf16[2,896,2048]{2,1,0:T(8,128)(2,1)} %all-gather.2.cloned.1.call-done), kind=kOutput, calls=%fused_computation.8 | convolution fusion | flops 2113929216 | bytes 8093696 | tf_op jit(solution)/shard_map/dot_general | solution.py:85
  153.9 4.1 %multiply_reduce_fusion.1 = (f32[576]{0:T(1024)S(1)}, f32[576]{0:T(1024)S(1)}, bf16[1,576,896]{2,1,0:T(8,128)(2,1)}, bf16[1,576,896]{2,1,0:T(8,128)(2,1)}) fusion(bf16[2,576,896]{2,1,0:T(8,128)(2,1)S(1)} %copy-done.17, f32[576,896]{1,0:T(8,128)S(1)} %fusion.1, f32[576]{0:T(1024)S(1)} %mul.78, f32[576]{0:T(1024)S(1)} %mul.74, ...), kind=kOutput, calls=%fused_computation.26 | convolution fusion | flops 2119089152 | bytes 12235264 | tf_op jit(solution)/shard_map/dot_general | solution.py:85
  158.4 3.5 %convert_bitcast_fusion = bf16[1,896,1024]{1,2,0:T(8,128)(2,1)S(1)} fusion(bf16[576,1024]{1,0:T(8,128)(2,1)} %collective-permute-done.9, bf16[2,576,896]{2,1,0:T(8,128)(2,1)} %collective-permute-done.8), kind=kOutput, calls=%fused_computation.29 | convolution fusion | flops 1057882112 | bytes 4046848 | tf_op jit(solution)/shard_map/dot_general | solution.py:100
  163.9 2.8 %collective-permute-done.11 = f32[2,576]{1,0:T(2,128)S(1)} collective-permute-done((f32[2,576]{1,0:T(2,128)S(1)}, f32[2,576]{1,0:T(2,128)S(1)}, u32[]{:S(2)}, u32[]{:S(2)}) %collective-permute-start.11) | collective-permute-done | bytes 4640 | tf_op jit(solution)/shard_map/ppermute | solution.py:10
  166.6 3.5 %collective-permute-start.12 = (f32[2,576]{1,0:T(2,128)S(1)}, f32[2,576]{1,0:T(2,128)S(1)}, u32[]{:S(2)}, u32[]{:S(2)}) collective-permute-start(f32[2,576]{1,0:T(2,128)S(1)} %fusion.40), channel_id=1, source_target_pairs={{0,8},{2,10},{4,12},{6,14},{8,0},{10,2},{12,4},{14,6},{1,9},{3,11}... | collective-permute-start | bytes 13832 | tf_op jit(solution)/shard_map/ppermute | solution.py:10
  170.2 2.7 %add_convert_fusion = bf16[2,896,1024]{1,2,0:T(8,128)(2,1)} fusion(bf16[2,896,1024]{1,2,0:T(8,128)(2,1)S(1)} %pad_maximum_fusion.1, bf16[2,896,1024]{1,2,0:T(8,128)(2,1)S(1)} %copy-done), kind=kLoop, calls=%fused_computation | loop fusion | flops 7340032 | bytes 11010048 | tf_op jit(solution)/shard_map/convert_element_type | solution.py:119
  172.9 6.1 %copy.66 = bf16[2,896,1024]{2,1,0:T(8,128)(2,1)} copy(bf16[2,896,1024]{1,2,0:T(8,128)(2,1)} %add_convert_fusion) | data formatting | bytes 7340032
  179.7 6.6 %all-to-all-start.3 = ((f32[2,16,36]{2,0,1:T(2,128)}), f32[2,16,36]{2,0,1:T(2,128)S(1)}, u32[]{:S(2)}, u32[]{:S(2)}) async-start(f32[2,16,36]{2,0,1:T(2,128)} %copy.65), calls=%async_computation.3 | async-start | bytes 32768 | tf_op jit(solution)/shard_map/all_to_all | solution.py:106
  187.8 4.8 %all-to-all-done.3 = f32[2,16,36]{2,0,1:T(2,128)S(1)} async-done(((f32[2,16,36]{2,0,1:T(2,128)}), f32[2,16,36]{2,0,1:T(2,128)S(1)}, u32[]{:S(2)}, u32[]{:S(2)}) %all-to-all-start.3) | async-done | bytes 4640 | tf_op jit(solution)/shard_map/all_to_all | solution.py:106
  (119 shorter events, 40.2 us)
Async XLA Ops:
  7.2 140.6 %all-gather.2.cloned.1.call-start = ((), (), s32[]{:S(2)}) async-start(), calls=%async_computation.4 | async-start | bytes 11010048 | tf_op jit(solution)/shard_map/all_gather | solution.py:71
  7.2 18.7 %collective-permute-start = (bf16[512,256]{1,0:T(8,128)(2,1)}, bf16[512,256]{1,0:T(8,128)(2,1)}, u32[]{:S(2)}, u32[]{:S(2)}) collective-permute-start(bf16[512,256]{1,0:T(8,128)(2,1)} %param.6), channel_id=1, source_target_pairs={{0,2},{2,4},{4,6},{6,8},{8,10},{10,12},{12,14},{14,0},{1,3},{3,5},... | collective-permute-start | bytes 786440 | tf_op jit(solution)/shard_map/ppermute | solution.py:30
  9.2 16.8 %collective-permute-start.1 = (bf16[512,256]{1,0:T(8,128)(2,1)}, bf16[512,256]{1,0:T(8,128)(2,1)S(1)}, u32[]{:S(2)}, u32[]{:S(2)}) collective-permute-start(bf16[512,256]{1,0:T(8,128)(2,1)} %param.6), channel_id=1, source_target_pairs={{0,14},{2,0},{4,2},{6,4},{8,6},{10,8},{12,10},{14,12},{1,15},{3,1}... | collective-permute-start | bytes 786440 | tf_op jit(solution)/shard_map/ppermute | solution.py:35
  14.5 10.0 %copy-start.12 = (s32[512,1]{0,1:T(1,128)}, s32[512,1]{0,1:T(1,128)S(1)}, u32[]{:S(2)}) copy-start(s32[512,1]{0,1:T(1,128)S(1)} %get-tuple-element.34) | copy-start | bytes 6148
  14.9 9.7 %copy-start.9 = (bf16[512,256]{1,0:T(8,128)(2,1)S(1)}, bf16[512,256]{1,0:T(8,128)(2,1)}, u32[]{:S(2)}) copy-start(bf16[512,256]{1,0:T(8,128)(2,1)} %param.6) | copy-start | bytes 786436
  16.9 39.1 %all-to-all-start = ((bf16[16,2,36]{2,1,0:T(2,128)(2,1)}), bf16[16,2,36]{2,1,0:T(2,128)(2,1)S(1)}, u32[]{:S(2)}, u32[]{:S(2)}) async-start(bf16[16,2,36]{2,1,0:T(2,128)(2,1)} %reshape.83), calls=%async_computation | async-start | bytes 16384 | tf_op jit(solution)/shard_map/all_to_all | solution.py:68
  25.9 8.7 %collective-permute-start.2 = (bf16[512,256]{1,0:T(8,128)(2,1)}, bf16[512,256]{1,0:T(8,128)(2,1)S(1)}, u32[]{:S(2)}, u32[]{:S(2)}) collective-permute-start(bf16[512,256]{1,0:T(8,128)(2,1)} %collective-permute-done), channel_id=1, source_target_pairs={{0,2},{2,4},{4,6},{6,8},{8,10},{10,12},{12,14},{14,0},{1,3},{3,5},... | collective-permute-start | bytes 786440 | tf_op jit(solution)/shard_map/ppermute | solution.py:30
  26.0 8.6 %collective-permute-start.3 = (bf16[512,256]{1,0:T(8,128)(2,1)S(1)}, bf16[512,256]{1,0:T(8,128)(2,1)S(1)}, u32[]{:S(2)}, u32[]{:S(2)}) collective-permute-start(bf16[512,256]{1,0:T(8,128)(2,1)S(1)} %collective-permute-done.1), channel_id=1, source_target_pairs={{0,14},{2,0},{4,2},{6,4},{8,6},{10,8},{12,10},{14,12},{1,15},{3,1}... | collective-permute-start | bytes 786440 | tf_op jit(solution)/shard_map/ppermute | solution.py:35
  34.6 7.6 %collective-permute-start.4 = (bf16[512,256]{1,0:T(8,128)(2,1)S(1)}, bf16[512,256]{1,0:T(8,128)(2,1)S(1)}, u32[]{:S(2)}, u32[]{:S(2)}) collective-permute-start(bf16[512,256]{1,0:T(8,128)(2,1)S(1)} %collective-permute-done.2), channel_id=1, source_target_pairs={{0,2},{2,4},{4,6},{6,8},{8,10},{10,12},{12,14},{14,0},{1,3},{3,5},... | collective-permute-start | bytes 786440 | tf_op jit(solution)/shard_map/ppermute | solution.py:30
  34.6 7.6 %collective-permute-start.5 = (bf16[512,256]{1,0:T(8,128)(2,1)S(1)}, bf16[512,256]{1,0:T(8,128)(2,1)S(1)}, u32[]{:S(2)}, u32[]{:S(2)}) collective-permute-start(bf16[512,256]{1,0:T(8,128)(2,1)S(1)} %collective-permute-done.3), channel_id=1, source_target_pairs={{0,14},{2,0},{4,2},{6,4},{8,6},{10,8},{12,10},{14,12},{1,15},{3,1}... | collective-permute-start | bytes 786440 | tf_op jit(solution)/shard_map/ppermute | solution.py:35
  42.2 7.6 %collective-permute-start.6 = (bf16[512,256]{1,0:T(8,128)(2,1)S(1)}, bf16[512,256]{1,0:T(8,128)(2,1)S(1)}, u32[]{:S(2)}, u32[]{:S(2)}) collective-permute-start(bf16[512,256]{1,0:T(8,128)(2,1)S(1)} %collective-permute-done.4), channel_id=1, source_target_pairs={{0,2},{2,4},{4,6},{6,8},{8,10},{10,12},{12,14},{14,0},{1,3},{3,5},... | collective-permute-start | bytes 786440 | tf_op jit(solution)/shard_map/ppermute | solution.py:30
  56.0 36.9 %all-to-all-start.1 = ((bf16[16,36,2048]{2,1,0:T(8,128)(2,1)}), bf16[16,36,2048]{2,1,0:T(8,128)(2,1)S(1)}, u32[]{:S(2)}, u32[]{:S(2)}) async-start(bf16[16,36,2048]{2,1,0:T(8,128)(2,1)} %reshape.100), calls=%async_computation.1 | async-start | bytes 5242880 | tf_op jit(solution)/shard_map/all_to_all | solution.py:82
  93.0 37.9 %all-to-all-start.2 = ((bf16[16,36,2048]{2,1,0:T(8,128)(2,1)}), bf16[16,36,2048]{2,1,0:T(8,128)(2,1)}, u32[]{:S(2)}, u32[]{:S(2)}) async-start(bf16[16,36,2048]{2,1,0:T(8,128)(2,1)} %reshape.101), calls=%async_computation.2 | async-start | bytes 5242880 | tf_op jit(solution)/shard_map/all_to_all | solution.py:82
  100.4 42.8 %collective-permute-start.8 = (bf16[2,576,896]{2,1,0:T(8,128)(2,1)}, bf16[2,576,896]{2,1,0:T(8,128)(2,1)}, u32[]{:S(2)}, u32[]{:S(2)}) collective-permute-start(bf16[2,576,896]{2,1,0:T(8,128)(2,1)} %param.10), channel_id=1, source_target_pairs={{0,1},{1,0},{2,3},{3,2},{4,5},{5,4},{6,7},{7,6},{8,9},{9,8},{10,11... | collective-permute-start | bytes 6193160 | tf_op jit(solution)/shard_map/ppermute | solution.py:10
  107.4 35.7 %collective-permute-start.7 = (bf16[576,1024]{1,0:T(8,128)(2,1)}, bf16[576,1024]{1,0:T(8,128)(2,1)}, u32[]{:S(2)}, u32[]{:S(2)}) collective-permute-start(bf16[576,1024]{1,0:T(8,128)(2,1)} %constant_dynamic-slice_fusion.1), channel_id=1, source_target_pairs={{0,1},{1,0},{2,3},{3,2},{4,5},{5,4},{6,7},{7,6},{8,9},{9,8},{10,11... | collective-permute-start | bytes 3538952 | tf_op jit(solution)/shard_map/ppermute | solution.py:10
  136.2 22.2 %collective-permute-start.9 = (bf16[576,1024]{1,0:T(8,128)(2,1)}, bf16[576,1024]{1,0:T(8,128)(2,1)}, u32[]{:S(2)}, u32[]{:S(2)}) collective-permute-start(bf16[576,1024]{1,0:T(8,128)(2,1)} %constant_dynamic-slice_fusion), channel_id=1, source_target_pairs={{0,1},{1,0},{2,3},{3,2},{4,5},{5,4},{6,7},{7,6},{8,9},{9,8},{10,11... | collective-permute-start | bytes 3538952 | tf_op jit(solution)/shard_map/ppermute | solution.py:10
  147.7 6.2 %copy-start.17 = (bf16[2,576,896]{2,1,0:T(8,128)(2,1)S(1)}, bf16[2,576,896]{2,1,0:T(8,128)(2,1)}, u32[]{:S(2)}) copy-start(bf16[2,576,896]{2,1,0:T(8,128)(2,1)} %param.10) | copy-start | bytes 6193156
  158.1 3.9 %collective-permute-start.10 = (f32[2,576]{1,0:T(2,128)S(1)}, f32[2,576]{1,0:T(2,128)S(1)}, u32[]{:S(2)}, u32[]{:S(2)}) collective-permute-start(f32[2,576]{1,0:T(2,128)S(1)} %pad_maximum_fusion.3), channel_id=1, source_target_pairs={{0,2},{2,0},{4,6},{6,4},{8,10},{10,8},{12,14},{14,12},{1,3},{3,1},... | collective-permute-start | bytes 13832 | tf_op jit(solution)/shard_map/ppermute | solution.py:10
  162.0 8.2 %copy-start = (bf16[2,896,1024]{1,2,0:T(8,128)(2,1)S(1)}, bf16[2,896,1024]{1,2,0:T(8,128)(2,1)}, u32[]{:S(2)}) copy-start(bf16[2,896,1024]{1,2,0:T(8,128)(2,1)} %pad_maximum_fusion) | copy-start | bytes 11010052
  162.0 4.6 %collective-permute-start.11 = (f32[2,576]{1,0:T(2,128)S(1)}, f32[2,576]{1,0:T(2,128)S(1)}, u32[]{:S(2)}, u32[]{:S(2)}) collective-permute-start(f32[2,576]{1,0:T(2,128)S(1)} %fusion.32), channel_id=1, source_target_pairs={{0,4},{2,6},{4,0},{6,2},{8,12},{10,14},{12,8},{14,10},{1,5},{3,7},... | collective-permute-start | bytes 13832 | tf_op jit(solution)/shard_map/ppermute | solution.py:10
  166.6 12.4 %collective-permute-start.12 = (f32[2,576]{1,0:T(2,128)S(1)}, f32[2,576]{1,0:T(2,128)S(1)}, u32[]{:S(2)}, u32[]{:S(2)}) collective-permute-start(f32[2,576]{1,0:T(2,128)S(1)} %fusion.40), channel_id=1, source_target_pairs={{0,8},{2,10},{4,12},{6,14},{8,0},{10,2},{12,4},{14,6},{1,9},{3,11}... | collective-permute-start | bytes 13832 | tf_op jit(solution)/shard_map/ppermute | solution.py:10
  172.8 13.5 %copy-start.7 = (bf16[1,576,896]{2,1,0:T(8,128)(2,1)S(1)}, bf16[1,576,896]{2,1,0:T(8,128)(2,1)}, u32[]{:S(2)}) copy-start(bf16[1,576,896]{2,1,0:T(8,128)(2,1)} %get-tuple-element.31) | copy-start | bytes 3096580
  172.9 13.5 %copy-start.8 = (bf16[1,576,896]{2,1,0:T(8,128)(2,1)S(1)}, bf16[1,576,896]{2,1,0:T(8,128)(2,1)}, u32[]{:S(2)}) copy-start(bf16[1,576,896]{2,1,0:T(8,128)(2,1)} %get-tuple-element.32) | copy-start | bytes 3096580
  179.7 12.9 %all-to-all-start.3 = ((f32[2,16,36]{2,0,1:T(2,128)}), f32[2,16,36]{2,0,1:T(2,128)S(1)}, u32[]{:S(2)}, u32[]{:S(2)}) async-start(f32[2,16,36]{2,0,1:T(2,128)} %copy.65), calls=%async_computation.3 | async-start | bytes 32768 | tf_op jit(solution)/shard_map/all_to_all | solution.py:106
  (12 other events, 35.6 us)
Sparse Core Ops, SparseCore 0:
  13.4 23.8 all-gather.1

commit v4 on v3

--- a/solution.py
+++ b/solution.py
@@ -23,18 +23,19 @@
     index = lax.axis_index(axis)
     right = [(source, (source + 1) % size) for source in range(size)]
     left = [(source, (source - 1) % size) for source in range(size)]
-    gathered = jnp.zeros((size,) + value.shape, value.dtype)
-    gathered = lax.dynamic_update_index_in_dim(gathered, value, index, 0)
+    width = value.shape[1]
+    gathered = jnp.zeros((value.shape[0], size * width), value.dtype)
+    gathered = lax.dynamic_update_slice_in_dim(gathered, value, index * width, 1)
     going_right = going_left = value
     for step in range(1, size // 2 + 1):
         going_right = lax.ppermute(going_right, axis, right)
-        gathered = lax.dynamic_update_index_in_dim(
-            gathered, going_right, (index + size - step) % size, 0
+        gathered = lax.dynamic_update_slice_in_dim(
+            gathered, going_right, (index + size - step) % size * width, 1
         )
         if step < size - size // 2:
             going_left = lax.ppermute(going_left, axis, left)
-            gathered = lax.dynamic_update_index_in_dim(
-                gathered, going_left, (index + step) % size, 0
+            gathered = lax.dynamic_update_slice_in_dim(
+                gathered, going_left, (index + step) % size * width, 1
             )
     return gathered
 
@@ -70,18 +71,20 @@
     gathered = ring_gather(out_grad, "tensor")
     full_weight = lax.all_gather(down_weight, "dp", axis=2, tiled=True)
     placing = (pick0 | pick1).astype(jnp.bfloat16).reshape(experts, local_experts, capacity, -1)
-    half_width = gathered.shape[0] * gathered.shape[2] // 2
+    half_width = gathered.shape[1] // 2
     dp_index = lax.axis_index("dp")
     grad_rows, scores_local, own_terms, peer_terms = [], [], [], []
     peer_hidden = from_partner(hidden_act, "dp", 0)
+    outgoing = lax.dot_general(
+        placing.reshape(experts, local_experts * capacity, -1), gathered,
+        (((2,), (0,)), ((), ())),
+        preferred_element_type=jnp.float32,
+    ).astype(jnp.bfloat16)
+    arrived = lax.all_to_all(outgoing, "expert", split_axis=0, concat_axis=0, tiled=True)
+    routed_all = arrived.reshape(experts, local_experts, capacity, -1).transpose(1, 0, 2, 3)
+    routed_all = routed_all.reshape(local_experts, slot_count, -1)
     for local in range(local_experts):
-        outgoing = lax.dot_general(
-            placing[:, local], gathered, (((2,), (1,)), ((), ())),
-            preferred_element_type=jnp.float32,
-        ).astype(jnp.bfloat16).reshape(experts, capacity, -1)
-        routed = lax.all_to_all(
-            outgoing, "expert", split_axis=0, concat_axis=0, tiled=True
-        ).reshape(slot_count, -1)
+        routed = routed_all[local]
         backprop = jnp.dot(routed, full_weight[local].T, preferred_element_type=jnp.float32)
         grad_rows.append((weight[local][:, None] * backprop).astype(jnp.bfloat16))
         scores_local.append(

time: 202 us -> 204 us (level)
  waiting for transfers between devices: 66.8 us -> 79.1 us
  starting transfers between devices: 47.1 us -> 39.2 us
  local copies, waits for them, and re-layouts: 33.6 us -> 29.1 us
  matrix products: 27.6 us -> 30.8 us
    reshape x6 -> x0, local copies, waits for them, and re-layouts: 14.6 us -> none  [the longest x4 9.85 us: body(): outgoing = lax.dot_general(placing[:, local], gathered, (((2,), (1,)), ((...]
    all_to_all x2 -> x1, waiting for transfers between devices: 43.1 us -> 55.7 us  [body(): lax.all_to_all(outgoing, 'expert', split_axis=0, concat_axis=0, tiled=True)]
    ppermute x4, waiting for transfers between devices: 16.1 us -> 6.65 us  [ring_gather(): going_right = lax.ppermute(going_right, axis, right)]
    ppermute x3, waiting for transfers between devices: 0.01 us -> 7.75 us  [ring_gather(): going_left = lax.ppermute(going_left, axis, left)]
    all_to_all x2 -> x1, starting transfers between devices: 14.6 us -> 7.23 us  [body(): lax.all_to_all(outgoing, 'expert', split_axis=0, concat_axis=0, tiled=True)]
    slice x0 -> x3, local copies, waits for them, and re-layouts: none -> 6.05 us  [body(): routed = routed_all[local]]
    all_to_all x0 -> x1, local copies, waits for them, and re-layouts: none -> 4.92 us  [body(): lax.all_to_all(outgoing, 'expert', split_axis=0, concat_axis=0, tiled=True)]
    squeeze x0 -> x2, local copies, waits for them, and re-layouts: none -> 4.3 us  [body(): routed = routed_all[local]]
  transfers between devices with their start and end apart: 18 -> 17, of which waited for: 8 -> 8; matrix products, arithmetic and copies ran while one was open for 32% -> 33% of each run, Pallas kernels for 0% -> 0%
where the time goes in v4:
time: 204 us; the launch traced here: 203 us
  waiting for transfers between devices  79.1 us (39%)
  starting transfers between devices  39.2 us (19%)
  matrix products  30.8 us (15%)
  local copies, waits for them, and re-layouts  29.1 us (14%)
  between operations  14.5 us (7%)
  other arithmetic  10.2 us (5%)
    all_to_all x1, waiting for transfers between devices, body(): lax.all_to_all(outgoing, 'expert', split_axis=0, concat_axis=0, tiled=True)  55.7 us
    dot_general x2, matrix products, body(): jnp.dot(routed, full_weight[local].T, preferred_element_type=jnp.float32)  11.1 us
    ppermute x3, starting transfers between devices, ring_gather(): going_left = lax.ppermute(going_left, axis, left)  11 us
    unnamed x27, local copies, waits for them, and re-layouts  9.46 us
    dot_general x2, matrix products, body(): jnp.dot(peer_hidden[local].T, peer_scaled, preferred_element_type=jnp.flo...  7.78 us
    ppermute x3, waiting for transfers between devices, ring_gather(): going_left = lax.ppermute(going_left, axis, left)  7.75 us
    all_to_all x1, starting transfers between devices, body(): lax.all_to_all(slot_scale, 'expert', split_axis=0, concat_axis=2, tiled=T...  7.48 us
    all_to_all x1, starting transfers between devices, body(): lax.all_to_all(scores.reshape(local_experts, experts, capacity), 'expert'...  7.26 us
  transfers between devices with their start and end apart: 17, of which 8 were waited for; matrix products, arithmetic and copies ran while one was open for 33% of the time, Pallas kernels for 0%

profile of v4, /device:TPU:2, one launch (start us, length us, event | category | flops | bytes accessed | tf_op | source)
XLA Modules:
  0.0 202.9 jit_solution(7984233271964864671)
XLA Ops:
  9.2 4.0 %collective-permute-start.1 = (bf16[512,256]{1,0:T(8,128)(2,1)}, bf16[512,256]{1,0:T(8,128)(2,1)S(1)}, u32[]{:S(2)}, u32[]{:S(2)}) collective-permute-start(bf16[512,256]{1,0:T(8,128)(2,1)} %param.6), channel_id=1, source_target_pairs={{0,14},{2,0},{4,2},{6,4},{8,6},{10,8},{12,10},{14,12},{1,15},{3,1}... | collective-permute-start | bytes 786440 | tf_op jit(solution)/shard_map/ppermute | solution.py:36
  16.8 2.9 %collective-permute-done = bf16[512,256]{1,0:T(8,128)(2,1)S(1)} collective-permute-done((bf16[512,256]{1,0:T(8,128)(2,1)}, bf16[512,256]{1,0:T(8,128)(2,1)S(1)}, u32[]{:S(2)}, u32[]{:S(2)}) %collective-permute-start) | collective-permute-done | bytes 262176 | tf_op jit(solution)/shard_map/ppermute | solution.py:31
  20.4 7.5 %all-to-all-start = ((bf16[16,2,36]{2,1,0:T(2,128)(2,1)}), bf16[16,2,36]{2,1,0:T(2,128)(2,1)S(1)}, u32[]{:S(2)}, u32[]{:S(2)}) async-start(bf16[16,2,36]{2,1,0:T(2,128)(2,1)} %reshape.74), calls=%async_computation | async-start | bytes 16384 | tf_op jit(solution)/shard_map/all_to_all | solution.py:69
  28.2 3.3 %collective-permute-start.3 = (bf16[512,256]{1,0:T(8,128)(2,1)S(1)}, bf16[512,256]{1,0:T(8,128)(2,1)S(1)}, u32[]{:S(2)}, u32[]{:S(2)}) collective-permute-start(bf16[512,256]{1,0:T(8,128)(2,1)S(1)} %collective-permute-done.1), channel_id=1, source_target_pairs={{0,14},{2,0},{4,2},{6,4},{8,6},{10,8},{12,10},{14,12},{1,15},{3,1}... | collective-permute-start | bytes 786440 | tf_op jit(solution)/shard_map/ppermute | solution.py:36
  31.6 4.1 %collective-permute-done.3 = bf16[512,256]{1,0:T(8,128)(2,1)S(1)} collective-permute-done((bf16[512,256]{1,0:T(8,128)(2,1)S(1)}, bf16[512,256]{1,0:T(8,128)(2,1)S(1)}, u32[]{:S(2)}, u32[]{:S(2)}) %collective-permute-start.3) | collective-permute-done | bytes 262176 | tf_op jit(solution)/shard_map/ppermute | solution.py:36
  35.6 3.7 %collective-permute-start.5 = (bf16[512,256]{1,0:T(8,128)(2,1)S(1)}, bf16[512,256]{1,0:T(8,128)(2,1)S(1)}, u32[]{:S(2)}, u32[]{:S(2)}) collective-permute-start(bf16[512,256]{1,0:T(8,128)(2,1)S(1)} %collective-permute-done.3), channel_id=1, source_target_pairs={{0,14},{2,0},{4,2},{6,4},{8,6},{10,8},{12,10},{14,12},{1,15},{3,1}... | collective-permute-start | bytes 786440 | tf_op jit(solution)/shard_map/ppermute | solution.py:36
  39.5 3.7 %collective-permute-done.5 = bf16[512,256]{1,0:T(8,128)(2,1)S(1)} collective-permute-done((bf16[512,256]{1,0:T(8,128)(2,1)S(1)}, bf16[512,256]{1,0:T(8,128)(2,1)S(1)}, u32[]{:S(2)}, u32[]{:S(2)}) %collective-permute-start.5) | collective-permute-done | bytes 262176 | tf_op jit(solution)/shard_map/ppermute | solution.py:36
  43.2 3.8 %collective-permute-done.6 = bf16[512,256]{1,0:T(8,128)(2,1)S(1)} collective-permute-done((bf16[512,256]{1,0:T(8,128)(2,1)S(1)}, bf16[512,256]{1,0:T(8,128)(2,1)S(1)}, u32[]{:S(2)}, u32[]{:S(2)}) %collective-permute-start.6) | collective-permute-done | bytes 262176 | tf_op jit(solution)/shard_map/ppermute | solution.py:31
  47.0 4.3 %convolution_convert_fusion = bf16[16,72,2048]{2,1,0:T(8,128)(2,1)} fusion(bf16[512,2048]{1,0:T(8,128)(2,1)S(1)} %constant_dynamic-update-slice_fusion, s32[512]{0:T(512)S(1)} %bitcast.71, s32[16,72]{1,0:T(8,128)S(1)} %multiply_add_fusion, s32[512]{0:T(512)S(1)} %bitcast.69), kind=kOutput, calls=%fused_computation.7 | convolution fusion | flops 2420047872 | bytes 6824448 | tf_op jit(solution)/shard_map/dot_general | solution.py:78
  51.3 7.2 %all-to-all-start.1 = ((bf16[16,72,2048]{2,1,0:T(8,128)(2,1)}), bf16[16,72,2048]{2,1,0:T(8,128)(2,1)}, u32[]{:S(2)}, u32[]{:S(2)}) async-start(bf16[16,72,2048]{2,1,0:T(8,128)(2,1)} %convolution_convert_fusion), calls=%async_computation.1 | async-start | bytes 9437184 | tf_op jit(solution)/shard_map/all_to_all | solution.py:83
  59.8 55.7 %all-to-all-done.1 = bf16[16,72,2048]{2,1,0:T(8,128)(2,1)} async-done(((bf16[16,72,2048]{2,1,0:T(8,128)(2,1)}), bf16[16,72,2048]{2,1,0:T(8,128)(2,1)}, u32[]{:S(2)}, u32[]{:S(2)}) %all-to-all-start.1) | async-done | bytes 4718624 | tf_op jit(solution)/shard_map/all_to_all | solution.py:83
  115.6 4.9 %copy.57 = bf16[16,72,2048]{2,0,1:T(8,128)(2,1)S(1)} copy(bf16[16,72,2048]{2,1,0:T(8,128)(2,1)} %all-to-all-done.1) | data formatting | bytes 9437184 | tf_op jit(solution)/shard_map/all_to_all | solution.py:83
  125.7 3.0 %copy.58 = bf16[1,16,36,2048]{3,2,1,0:T(8,128)(2,1)S(1)} copy(bf16[1,16,36,2048]{3,1,2,0:T(8,128)(2,1)} %get-tuple-element.31) | data formatting | bytes 4718592 | tf_op jit(solution)/shard_map/slice | solution.py:87
  136.2 3.0 %convert_bitcast_fusion.3 = bf16[1,896,1024]{1,2,0:T(8,128)(2,1)S(1)} fusion(bf16[576,2048]{1,0:T(8,128)(2,1)S(1)} %multiply_convert_fusion.1, s32[]{:T(128)S(6)} %select_n.87, bf16[2,576,896]{2,1,0:T(8,128)(2,1)} %param.10), kind=kOutput, calls=%fused_computation.30 | convolution fusion | flops 1057882112 | bytes 4046852 | tf_op jit(solution)/shard_map/dot_general | solution.py:98
  139.2 3.0 %convert_bitcast_fusion.2 = bf16[1,896,1024]{1,2,0:T(8,128)(2,1)S(1)} fusion(bf16[576,2048]{1,0:T(8,128)(2,1)S(1)} %multiply_convert_fusion, s32[]{:T(128)S(6)} %select_n.87, bf16[2,576,896]{2,1,0:T(8,128)(2,1)} %param.10), kind=kOutput, calls=%fused_computation.29 | convolution fusion | flops 1057882112 | bytes 4046852 | tf_op jit(solution)/shard_map/dot_general | solution.py:98
  144.5 4.3 %convert_bitcast_fusion.1 = bf16[1,896,1024]{1,2,0:T(8,128)(2,1)} fusion(bf16[576,1024]{1,0:T(8,128)(2,1)S(1)} %collective-permute-done.7, bf16[2,576,896]{2,1,0:T(8,128)(2,1)} %collective-permute-done.8), kind=kOutput, calls=%fused_computation.28 | convolution fusion | flops 1057882112 | bytes 4046848 | tf_op jit(solution)/shard_map/dot_general | solution.py:103
  148.8 5.5 %fusion.1 = f32[576,896]{1,0:T(8,128)S(1)} fusion(bf16[576,2048]{1,0:T(8,128)(2,1)} %squeeze.36, bf16[2,896,2048]{2,1,0:T(8,128)(2,1)} %all-gather.2.cloned.1.call-done), kind=kOutput, calls=%fused_computation.9 | convolution fusion | flops 2113929216 | bytes 8093696 | tf_op jit(solution)/shard_map/dot_general | solution.py:88
  154.3 5.6 %multiply_reduce_fusion.1 = (f32[576]{0:T(1024)S(1)}, f32[576]{0:T(1024)S(1)}, bf16[1,576,896]{2,1,0:T(8,128)(2,1)}, bf16[1,576,896]{2,1,0:T(8,128)(2,1)}) fusion(bf16[2,576,896]{2,1,0:T(8,128)(2,1)} %param.10, f32[576,896]{1,0:T(8,128)S(1)} %fusion.1, f32[576]{0:T(1024)S(1)} %mul.110, f32[576]{0:T(1024)S(1)} %mul.98, bf16[576,2048]{1,0:T(8,128)(2,1)S(1)} %copy-done.1, ...), kind=kOutput, calls=%fused_computation.24 | convolution fusion | flops 2119089152 | bytes 12235264 | tf_op jit(solution)/shard_map/dot_general | solution.py:88
  160.3 3.5 %convert_bitcast_fusion = bf16[1,896,1024]{1,2,0:T(8,128)(2,1)S(1)} fusion(bf16[576,1024]{1,0:T(8,128)(2,1)} %collective-permute-done.9, bf16[2,576,896]{2,1,0:T(8,128)(2,1)} %collective-permute-done.8), kind=kOutput, calls=%fused_computation.27 | convolution fusion | flops 1057882112 | bytes 4046848 | tf_op jit(solution)/shard_map/dot_general | solution.py:103
  165.0 3.6 %collective-permute-done.11 = f32[2,576]{1,0:T(2,128)S(1)} collective-permute-done((f32[2,576]{1,0:T(2,128)S(1)}, f32[2,576]{1,0:T(2,128)S(1)}, u32[]{:S(2)}, u32[]{:S(2)}) %collective-permute-start.11) | collective-permute-done | bytes 4640 | tf_op jit(solution)/shard_map/ppermute | solution.py:10
  168.6 2.7 %collective-permute-start.12 = (f32[2,576]{1,0:T(2,128)S(1)}, f32[2,576]{1,0:T(2,128)S(1)}, u32[]{:S(2)}, u32[]{:S(2)}) collective-permute-start(f32[2,576]{1,0:T(2,128)S(1)} %fusion.38), channel_id=1, source_target_pairs={{0,8},{2,10},{4,12},{6,14},{8,0},{10,2},{12,4},{14,6},{1,9},{3,11}... | collective-permute-start | bytes 13832 | tf_op jit(solution)/shard_map/ppermute | solution.py:10
  173.9 6.1 %copy.61 = bf16[2,896,1024]{2,1,0:T(8,128)(2,1)} copy(bf16[2,896,1024]{1,2,0:T(8,128)(2,1)} %add_convert_fusion) | data formatting | bytes 7340032
  180.8 7.3 %all-to-all-start.2 = ((f32[2,16,36]{2,0,1:T(2,128)}), f32[2,16,36]{2,0,1:T(2,128)S(1)}, u32[]{:S(2)}, u32[]{:S(2)}) async-start(f32[2,16,36]{2,0,1:T(2,128)} %copy.60), calls=%async_computation.2 | async-start | bytes 32768 | tf_op jit(solution)/shard_map/all_to_all | solution.py:109
  189.5 4.7 %all-to-all-done.2 = f32[2,16,36]{2,0,1:T(2,128)S(1)} async-done(((f32[2,16,36]{2,0,1:T(2,128)}), f32[2,16,36]{2,0,1:T(2,128)S(1)}, u32[]{:S(2)}, u32[]{:S(2)}) %all-to-all-start.2) | async-done | bytes 4640 | tf_op jit(solution)/shard_map/all_to_all | solution.py:109
  (101 shorter events, 31.1 us)
Async XLA Ops:
  7.2 7.9 %copy-start.7 = (s32[512,2]{0,1:T(2,128)S(1)}, s32[512,2]{0,1:T(2,128)}, u32[]{:S(2)}) copy-start(s32[512,2]{0,1:T(2,128)} %param.7) | copy-start | bytes 12292
  7.2 8.0 %copy-start.8 = (s32[512,2]{0,1:T(2,128)S(1)}, s32[512,2]{0,1:T(2,128)}, u32[]{:S(2)}) copy-start(s32[512,2]{0,1:T(2,128)} %param.9) | copy-start | bytes 12292
  7.2 8.1 %copy-start.9 = (f32[512,2]{0,1:T(2,128)S(1)}, f32[512,2]{0,1:T(2,128)}, u32[]{:S(2)}) copy-start(f32[512,2]{0,1:T(2,128)} %param.8) | copy-start | bytes 12292
  7.2 12.5 %collective-permute-start = (bf16[512,256]{1,0:T(8,128)(2,1)}, bf16[512,256]{1,0:T(8,128)(2,1)S(1)}, u32[]{:S(2)}, u32[]{:S(2)}) collective-permute-start(bf16[512,256]{1,0:T(8,128)(2,1)} %param.6), channel_id=1, source_target_pairs={{0,2},{2,4},{4,6},{6,8},{8,10},{10,12},{12,14},{14,0},{1,3},{3,5},... | collective-permute-start | bytes 786440 | tf_op jit(solution)/shard_map/ppermute | solution.py:31
  9.2 19.0 %collective-permute-start.1 = (bf16[512,256]{1,0:T(8,128)(2,1)}, bf16[512,256]{1,0:T(8,128)(2,1)S(1)}, u32[]{:S(2)}, u32[]{:S(2)}) collective-permute-start(bf16[512,256]{1,0:T(8,128)(2,1)} %param.6), channel_id=1, source_target_pairs={{0,14},{2,0},{4,2},{6,4},{8,6},{10,8},{12,10},{14,12},{1,15},{3,1}... | collective-permute-start | bytes 786440 | tf_op jit(solution)/shard_map/ppermute | solution.py:36
  15.5 12.6 %copy-start.6 = (bf16[512,256]{1,0:T(8,128)(2,1)S(1)}, bf16[512,256]{1,0:T(8,128)(2,1)}, u32[]{:S(2)}) copy-start(bf16[512,256]{1,0:T(8,128)(2,1)} %param.6) | copy-start | bytes 786436
  19.6 11.8 %collective-permute-start.2 = (bf16[512,256]{1,0:T(8,128)(2,1)S(1)}, bf16[512,256]{1,0:T(8,128)(2,1)S(1)}, u32[]{:S(2)}, u32[]{:S(2)}) collective-permute-start(bf16[512,256]{1,0:T(8,128)(2,1)S(1)} %collective-permute-done), channel_id=1, source_target_pairs={{0,2},{2,4},{4,6},{6,8},{8,10},{10,12},{12,14},{14,0},{1,3},{3,5},... | collective-permute-start | bytes 786440 | tf_op jit(solution)/shard_map/ppermute | solution.py:31
  20.4 31.0 %all-to-all-start = ((bf16[16,2,36]{2,1,0:T(2,128)(2,1)}), bf16[16,2,36]{2,1,0:T(2,128)(2,1)S(1)}, u32[]{:S(2)}, u32[]{:S(2)}) async-start(bf16[16,2,36]{2,1,0:T(2,128)(2,1)} %reshape.74), calls=%async_computation | async-start | bytes 16384 | tf_op jit(solution)/shard_map/all_to_all | solution.py:69
  28.2 7.5 %collective-permute-start.3 = (bf16[512,256]{1,0:T(8,128)(2,1)S(1)}, bf16[512,256]{1,0:T(8,128)(2,1)S(1)}, u32[]{:S(2)}, u32[]{:S(2)}) collective-permute-start(bf16[512,256]{1,0:T(8,128)(2,1)S(1)} %collective-permute-done.1), channel_id=1, source_target_pairs={{0,14},{2,0},{4,2},{6,4},{8,6},{10,8},{12,10},{14,12},{1,15},{3,1}... | collective-permute-start | bytes 786440 | tf_op jit(solution)/shard_map/ppermute | solution.py:36
  31.5 7.9 %collective-permute-start.4 = (bf16[512,256]{1,0:T(8,128)(2,1)S(1)}, bf16[512,256]{1,0:T(8,128)(2,1)S(1)}, u32[]{:S(2)}, u32[]{:S(2)}) collective-permute-start(bf16[512,256]{1,0:T(8,128)(2,1)S(1)} %collective-permute-done.2), channel_id=1, source_target_pairs={{0,2},{2,4},{4,6},{6,8},{8,10},{10,12},{12,14},{14,0},{1,3},{3,5},... | collective-permute-start | bytes 786440 | tf_op jit(solution)/shard_map/ppermute | solution.py:31
  35.6 7.6 %collective-permute-start.5 = (bf16[512,256]{1,0:T(8,128)(2,1)S(1)}, bf16[512,256]{1,0:T(8,128)(2,1)S(1)}, u32[]{:S(2)}, u32[]{:S(2)}) collective-permute-start(bf16[512,256]{1,0:T(8,128)(2,1)S(1)} %collective-permute-done.3), channel_id=1, source_target_pairs={{0,14},{2,0},{4,2},{6,4},{8,6},{10,8},{12,10},{14,12},{1,15},{3,1}... | collective-permute-start | bytes 786440 | tf_op jit(solution)/shard_map/ppermute | solution.py:36
  39.4 7.7 %collective-permute-start.6 = (bf16[512,256]{1,0:T(8,128)(2,1)S(1)}, bf16[512,256]{1,0:T(8,128)(2,1)S(1)}, u32[]{:S(2)}, u32[]{:S(2)}) collective-permute-start(bf16[512,256]{1,0:T(8,128)(2,1)S(1)} %collective-permute-done.4), channel_id=1, source_target_pairs={{0,2},{2,4},{4,6},{6,8},{8,10},{10,12},{12,14},{14,0},{1,3},{3,5},... | collective-permute-start | bytes 786440 | tf_op jit(solution)/shard_map/ppermute | solution.py:31
  51.3 64.2 %all-to-all-start.1 = ((bf16[16,72,2048]{2,1,0:T(8,128)(2,1)}), bf16[16,72,2048]{2,1,0:T(8,128)(2,1)}, u32[]{:S(2)}, u32[]{:S(2)}) async-start(bf16[16,72,2048]{2,1,0:T(8,128)(2,1)} %convolution_convert_fusion), calls=%async_computation.1 | async-start | bytes 9437184 | tf_op jit(solution)/shard_map/all_to_all | solution.py:83
  58.6 90.2 %all-gather.2.cloned.1.call-start = ((), (), s32[]{:S(2)}) async-start(), calls=%async_computation.3 | async-start | bytes 11010048 | tf_op jit(solution)/shard_map/all_gather | solution.py:72
  59.3 85.2 %collective-permute-start.8 = (bf16[2,576,896]{2,1,0:T(8,128)(2,1)}, bf16[2,576,896]{2,1,0:T(8,128)(2,1)}, u32[]{:S(2)}, u32[]{:S(2)}) collective-permute-start(bf16[2,576,896]{2,1,0:T(8,128)(2,1)} %param.10), channel_id=1, source_target_pairs={{0,1},{1,0},{2,3},{3,2},{4,5},{5,4},{6,7},{7,6},{8,9},{9,8},{10,11... | collective-permute-start | bytes 6193160 | tf_op jit(solution)/shard_map/ppermute | solution.py:10
  133.1 11.4 %collective-permute-start.7 = (bf16[576,1024]{1,0:T(8,128)(2,1)S(1)}, bf16[576,1024]{1,0:T(8,128)(2,1)S(1)}, u32[]{:S(2)}, u32[]{:S(2)}) collective-permute-start(bf16[576,1024]{1,0:T(8,128)(2,1)S(1)} %constant_dynamic-slice_fusion.1), channel_id=1, source_target_pairs={{0,1},{1,0},{2,3},{3,2},{4,5},{5,4},{6,7},{7,6},{8,9},{9,8},{10,11... | collective-permute-start | bytes 3538952 | tf_op jit(solution)/shard_map/ppermute | solution.py:10
  136.2 24.1 %collective-permute-start.9 = (bf16[576,1024]{1,0:T(8,128)(2,1)}, bf16[576,1024]{1,0:T(8,128)(2,1)}, u32[]{:S(2)}, u32[]{:S(2)}) collective-permute-start(bf16[576,1024]{1,0:T(8,128)(2,1)} %constant_dynamic-slice_fusion), channel_id=1, source_target_pairs={{0,1},{1,0},{2,3},{3,2},{4,5},{5,4},{6,7},{7,6},{8,9},{9,8},{10,11... | collective-permute-start | bytes 3538952 | tf_op jit(solution)/shard_map/ppermute | solution.py:10
  160.0 4.0 %collective-permute-start.10 = (f32[2,576]{1,0:T(2,128)S(1)}, f32[2,576]{1,0:T(2,128)S(1)}, u32[]{:S(2)}, u32[]{:S(2)}) collective-permute-start(f32[2,576]{1,0:T(2,128)S(1)} %pad_maximum_fusion.3), channel_id=1, source_target_pairs={{0,2},{2,0},{4,6},{6,4},{8,10},{10,8},{12,14},{14,12},{1,3},{3,1},... | collective-permute-start | bytes 13832 | tf_op jit(solution)/shard_map/ppermute | solution.py:10
  163.9 7.3 %copy-start = (bf16[2,896,1024]{1,2,0:T(8,128)(2,1)S(1)}, bf16[2,896,1024]{1,2,0:T(8,128)(2,1)}, u32[]{:S(2)}) copy-start(bf16[2,896,1024]{1,2,0:T(8,128)(2,1)} %pad_maximum_fusion) | copy-start | bytes 11010052
  164.0 4.6 %collective-permute-start.11 = (f32[2,576]{1,0:T(2,128)S(1)}, f32[2,576]{1,0:T(2,128)S(1)}, u32[]{:S(2)}, u32[]{:S(2)}) collective-permute-start(f32[2,576]{1,0:T(2,128)S(1)} %fusion.29), channel_id=1, source_target_pairs={{0,4},{2,6},{4,0},{6,2},{8,12},{10,14},{12,8},{14,10},{1,5},{3,7},... | collective-permute-start | bytes 13832 | tf_op jit(solution)/shard_map/ppermute | solution.py:10
  168.6 11.5 %collective-permute-start.12 = (f32[2,576]{1,0:T(2,128)S(1)}, f32[2,576]{1,0:T(2,128)S(1)}, u32[]{:S(2)}, u32[]{:S(2)}) collective-permute-start(f32[2,576]{1,0:T(2,128)S(1)} %fusion.38), channel_id=1, source_target_pairs={{0,8},{2,10},{4,12},{6,14},{8,0},{10,2},{12,4},{14,6},{1,9},{3,11}... | collective-permute-start | bytes 13832 | tf_op jit(solution)/shard_map/ppermute | solution.py:10
  173.9 14.1 %copy-start.4 = (bf16[1,576,896]{2,1,0:T(8,128)(2,1)S(1)}, bf16[1,576,896]{2,1,0:T(8,128)(2,1)}, u32[]{:S(2)}) copy-start(bf16[1,576,896]{2,1,0:T(8,128)(2,1)} %get-tuple-element.33) | copy-start | bytes 3096580
  173.9 14.1 %copy-start.5 = (bf16[1,576,896]{2,1,0:T(8,128)(2,1)S(1)}, bf16[1,576,896]{2,1,0:T(8,128)(2,1)}, u32[]{:S(2)}) copy-start(bf16[1,576,896]{2,1,0:T(8,128)(2,1)} %get-tuple-element.34) | copy-start | bytes 3096580
  180.8 13.5 %all-to-all-start.2 = ((f32[2,16,36]{2,0,1:T(2,128)}), f32[2,16,36]{2,0,1:T(2,128)S(1)}, u32[]{:S(2)}, u32[]{:S(2)}) async-start(f32[2,16,36]{2,0,1:T(2,128)} %copy.60), calls=%async_computation.2 | async-start | bytes 32768 | tf_op jit(solution)/shard_map/all_to_all | solution.py:109
  (4 other events, 17.5 us)
Sparse Core Ops, SparseCore 0:
  61.2 23.1 all-gather.1

commit v5 on v4

--- a/solution.py
+++ b/solution.py
@@ -75,16 +75,14 @@
     dp_index = lax.axis_index("dp")
     grad_rows, scores_local, own_terms, peer_terms = [], [], [], []
     peer_hidden = from_partner(hidden_act, "dp", 0)
-    outgoing = lax.dot_general(
-        placing.reshape(experts, local_experts * capacity, -1), gathered,
-        (((2,), (0,)), ((), ())),
-        preferred_element_type=jnp.float32,
-    ).astype(jnp.bfloat16)
-    arrived = lax.all_to_all(outgoing, "expert", split_axis=0, concat_axis=0, tiled=True)
-    routed_all = arrived.reshape(experts, local_experts, capacity, -1).transpose(1, 0, 2, 3)
-    routed_all = routed_all.reshape(local_experts, slot_count, -1)
     for local in range(local_experts):
-        routed = routed_all[local]
+        outgoing = lax.dot_general(
+            placing[:, local], gathered, (((2,), (0,)), ((), ())),
+            preferred_element_type=jnp.float32,
+        ).astype(jnp.bfloat16)
+        routed = lax.all_to_all(
+            outgoing, "expert", split_axis=0, concat_axis=0, tiled=True
+        ).reshape(slot_count, -1)
         backprop = jnp.dot(routed, full_weight[local].T, preferred_element_type=jnp.float32)
         grad_rows.append((weight[local][:, None] * backprop).astype(jnp.bfloat16))
         scores_local.append(

time: 204 us -> 198 us (0.971)
  waiting for transfers between devices: 79.1 us -> 69.1 us
  starting transfers between devices: 39.2 us -> 47.3 us
  local copies, waits for them, and re-layouts: 29.1 us -> 24.5 us
    ppermute x3, waiting for transfers between devices: 7.75 us -> 0.01 us  [ring_gather(): going_left = lax.ppermute(going_left, axis, left)]
    all_to_all x1 -> x2, waiting for transfers between devices: 55.7 us -> 48 us  [body(): lax.all_to_all(outgoing, 'expert', split_axis=0, concat_axis=0, tiled=True)]
    all_to_all x1 -> x2, starting transfers between devices: 7.23 us -> 14.9 us  [body(): lax.all_to_all(outgoing, 'expert', split_axis=0, concat_axis=0, tiled=True)]
    ppermute x4, waiting for transfers between devices: 6.65 us -> 13.5 us  [ring_gather(): going_right = lax.ppermute(going_right, axis, right)]
    slice x3 -> x0, local copies, waits for them, and re-layouts: 6.05 us -> none  [body(): routed = routed_all[local]]
    all_to_all x1 -> x0, local copies, waits for them, and re-layouts: 4.92 us -> none  [body(): lax.all_to_all(outgoing, 'expert', split_axis=0, concat_axis=0, tiled=True)]
    reshape x0 -> x2, local copies, waits for them, and re-layouts: none -> 4.77 us  [body(): routed = lax.all_to_all(outgoing, 'expert', split_axis=0, concat_axis=0,...]
    squeeze x2 -> x0, local copies, waits for them, and re-layouts: 4.3 us -> none  [body(): routed = routed_all[local]]
  transfers between devices with their start and end apart: 17 -> 18, of which waited for: 8 -> 8; matrix products, arithmetic and copies ran while one was open for 33% -> 30% of each run, Pallas kernels for 0% -> 0%
where the time goes in v5:
time: 198 us; the launch traced here: 197 us
  waiting for transfers between devices  69.1 us (35%)
  starting transfers between devices  47.3 us (24%)
  matrix products  30.6 us (15%)
  local copies, waits for them, and re-layouts  24.5 us (12%)
  between operations  14.7 us (7%)
  other arithmetic  10.7 us (5%)
    all_to_all x2, waiting for transfers between devices, body(): lax.all_to_all(outgoing, 'expert', split_axis=0, concat_axis=0, tiled=True)  48 us
    all_to_all x2, starting transfers between devices, body(): lax.all_to_all(outgoing, 'expert', split_axis=0, concat_axis=0, tiled=True)  14.9 us
    ppermute x4, waiting for transfers between devices, ring_gather(): going_right = lax.ppermute(going_right, axis, right)  13.5 us
    unnamed x37, local copies, waits for them, and re-layouts  11.5 us
    ppermute x3, starting transfers between devices, ring_gather(): going_left = lax.ppermute(going_left, axis, left)  10.6 us
    dot_general x2, matrix products, body(): jnp.dot(routed, full_weight[local].T, preferred_element_type=jnp.float32)  9.62 us
    dot_general x2, matrix products, body(): jnp.dot(peer_hidden[local].T, peer_scaled, preferred_element_type=jnp.flo...  8.11 us
    dot_general x2, matrix products, body(): lax.dot_general(placing[:, local], gathered, (((2,), (0,)), ((), ())), pr...  7.68 us
  transfers between devices with their start and end apart: 18, of which 8 were waited for; matrix products, arithmetic and copies ran while one was open for 30% of the time, Pallas kernels for 0%

profile of v5, /device:TPU:2, one launch (start us, length us, event | category | flops | bytes accessed | tf_op | source)
XLA Modules:
  0.0 196.8 jit_solution(16240865488243934380)
XLA Ops:
  9.2 4.0 %collective-permute-start.1 = (bf16[512,256]{1,0:T(8,128)(2,1)}, bf16[512,256]{1,0:T(8,128)(2,1)S(1)}, u32[]{:S(2)}, u32[]{:S(2)}) collective-permute-start(bf16[512,256]{1,0:T(8,128)(2,1)} %param.6), channel_id=1, source_target_pairs={{0,14},{2,0},{4,2},{6,4},{8,6},{10,8},{12,10},{14,12},{1,15},{3,1}... | collective-permute-start | bytes 786440 | tf_op jit(solution)/shard_map/ppermute | solution.py:36
  16.9 7.5 %all-to-all-start = ((bf16[16,2,36]{2,1,0:T(2,128)(2,1)}), bf16[16,2,36]{2,1,0:T(2,128)(2,1)S(1)}, u32[]{:S(2)}, u32[]{:S(2)}) async-start(bf16[16,2,36]{2,1,0:T(2,128)(2,1)} %reshape.77), calls=%async_computation | async-start | bytes 16384 | tf_op jit(solution)/shard_map/all_to_all | solution.py:69
  25.0 3.3 %collective-permute-start.3 = (bf16[512,256]{1,0:T(8,128)(2,1)S(1)}, bf16[512,256]{1,0:T(8,128)(2,1)}, u32[]{:S(2)}, u32[]{:S(2)}) collective-permute-start(bf16[512,256]{1,0:T(8,128)(2,1)S(1)} %collective-permute-done.1), channel_id=1, source_target_pairs={{0,14},{2,0},{4,2},{6,4},{8,6},{10,8},{12,10},{14,12},{1,15},{3,1}... | collective-permute-start | bytes 786440 | tf_op jit(solution)/shard_map/ppermute | solution.py:36
  28.7 4.5 %collective-permute-done.2 = bf16[512,256]{1,0:T(8,128)(2,1)} collective-permute-done((bf16[512,256]{1,0:T(8,128)(2,1)}, bf16[512,256]{1,0:T(8,128)(2,1)}, u32[]{:S(2)}, u32[]{:S(2)}) %collective-permute-start.2) | collective-permute-done | bytes 262176 | tf_op jit(solution)/shard_map/ppermute | solution.py:31
  34.3 3.3 %collective-permute-start.5 = (bf16[512,256]{1,0:T(8,128)(2,1)}, bf16[512,256]{1,0:T(8,128)(2,1)S(1)}, u32[]{:S(2)}, u32[]{:S(2)}) collective-permute-start(bf16[512,256]{1,0:T(8,128)(2,1)} %collective-permute-done.3), channel_id=1, source_target_pairs={{0,14},{2,0},{4,2},{6,4},{8,6},{10,8},{12,10},{14,12},{1,15},{3,1}... | collective-permute-start | bytes 786440 | tf_op jit(solution)/shard_map/ppermute | solution.py:36
  38.5 2.5 %collective-permute-done.4 = bf16[512,256]{1,0:T(8,128)(2,1)S(1)} collective-permute-done((bf16[512,256]{1,0:T(8,128)(2,1)}, bf16[512,256]{1,0:T(8,128)(2,1)S(1)}, u32[]{:S(2)}, u32[]{:S(2)}) %collective-permute-start.4) | collective-permute-done | bytes 262176 | tf_op jit(solution)/shard_map/ppermute | solution.py:31
  42.1 6.5 %collective-permute-done.6 = bf16[512,256]{1,0:T(8,128)(2,1)S(1)} collective-permute-done((bf16[512,256]{1,0:T(8,128)(2,1)S(1)}, bf16[512,256]{1,0:T(8,128)(2,1)S(1)}, u32[]{:S(2)}, u32[]{:S(2)}) %collective-permute-start.6) | collective-permute-done | bytes 262176 | tf_op jit(solution)/shard_map/ppermute | solution.py:31
  48.6 3.1 %convolution_convert_fusion.1 = bf16[16,36,2048]{2,1,0:T(8,128)(2,1)} fusion(bf16[512,2048]{1,0:T(8,128)(2,1)S(1)} %constant_dynamic-update-slice_fusion, pred[16,2,36,512]{3,2,0,1:T(8,128)(4,1)S(1)} %compare_or_fusion), kind=kOutput, calls=%fused_computation.14 | convolution fusion | flops 1209139200 | bytes 4784128 | tf_op jit(solution)/shard_map/dot_general | solution.py:79
  51.7 7.2 %all-to-all-start.1 = ((bf16[16,36,2048]{2,1,0:T(8,128)(2,1)}), bf16[16,36,2048]{2,1,0:T(8,128)(2,1)S(1)}, u32[]{:S(2)}, u32[]{:S(2)}) async-start(bf16[16,36,2048]{2,1,0:T(8,128)(2,1)} %convolution_convert_fusion.1), calls=%async_computation.1 | async-start | bytes 5242880 | tf_op jit(solution)/shard_map/all_to_all | solution.py:83
  59.0 4.6 %convolution_convert_fusion = bf16[16,36,2048]{2,1,0:T(8,128)(2,1)} fusion(bf16[512,2048]{1,0:T(8,128)(2,1)} %copy-done.5, pred[16,2,36,512]{3,2,0,1:T(8,128)(4,1)S(1)} %compare_or_fusion), kind=kOutput, calls=%fused_computation.13 | convolution fusion | flops 1209139200 | bytes 4784128 | tf_op jit(solution)/shard_map/dot_general | solution.py:79
  63.6 25.1 %all-to-all-done.1 = bf16[16,36,2048]{2,1,0:T(8,128)(2,1)S(1)} async-done(((bf16[16,36,2048]{2,1,0:T(8,128)(2,1)}), bf16[16,36,2048]{2,1,0:T(8,128)(2,1)S(1)}, u32[]{:S(2)}, u32[]{:S(2)}) %all-to-all-start.1) | async-done | bytes 2359328 | tf_op jit(solution)/shard_map/all_to_all | solution.py:83
  88.6 7.6 %all-to-all-start.2 = ((bf16[16,36,2048]{2,1,0:T(8,128)(2,1)}), bf16[16,36,2048]{2,1,0:T(8,128)(2,1)}, u32[]{:S(2)}, u32[]{:S(2)}) async-start(bf16[16,36,2048]{2,1,0:T(8,128)(2,1)} %convolution_convert_fusion), calls=%async_computation.2 | async-start | bytes 5242880 | tf_op jit(solution)/shard_map/all_to_all | solution.py:83
  103.8 22.9 %all-to-all-done.2 = bf16[16,36,2048]{2,1,0:T(8,128)(2,1)} async-done(((bf16[16,36,2048]{2,1,0:T(8,128)(2,1)}), bf16[16,36,2048]{2,1,0:T(8,128)(2,1)}, u32[]{:S(2)}, u32[]{:S(2)}) %all-to-all-start.2) | async-done | bytes 2359328 | tf_op jit(solution)/shard_map/all_to_all | solution.py:83
  126.7 2.7 %reshape.79 = bf16[576,2048]{1,0:T(8,128)(2,1)S(1)} reshape(bf16[16,36,2048]{2,1,0:T(8,128)(2,1)} %all-to-all-done.2) | data formatting | bytes 4718592 | tf_op jit(solution)/shard_map/reshape | solution.py:85
  138.9 4.6 %convert_bitcast_fusion.1 = bf16[1,896,1024]{1,2,0:T(8,128)(2,1)} fusion(bf16[576,1024]{1,0:T(8,128)(2,1)} %collective-permute-done.7, bf16[2,576,896]{2,1,0:T(8,128)(2,1)} %collective-permute-done.8), kind=kOutput, calls=%fused_computation.28 | convolution fusion | flops 1057882112 | bytes 4046848 | tf_op jit(solution)/shard_map/dot_general | solution.py:101
  143.5 5.5 %fusion.1 = f32[576,896]{1,0:T(8,128)S(1)} fusion(bf16[576,2048]{1,0:T(8,128)(2,1)} %copy-done.2, bf16[2,896,2048]{2,1,0:T(8,128)(2,1)} %all-gather.2.cloned.1.call-done), kind=kOutput, calls=%fused_computation.8 | convolution fusion | flops 2113929216 | bytes 8093696 | tf_op jit(solution)/shard_map/dot_general | solution.py:86
  149.7 4.1 %multiply_reduce_fusion.1 = (f32[576]{0:T(1024)S(1)}, f32[576]{0:T(1024)S(1)}, bf16[1,576,896]{2,1,0:T(8,128)(2,1)}, bf16[1,576,896]{2,1,0:T(8,128)(2,1)}) fusion(bf16[2,576,896]{2,1,0:T(8,128)(2,1)S(1)} %copy-done.15, f32[576,896]{1,0:T(8,128)S(1)} %fusion.1, f32[576]{0:T(1024)S(1)} %mul.110, f32[576]{0:T(1024)S(1)} %mul.98, ...), kind=kOutput, calls=%fused_computation.24 | convolution fusion | flops 2119089152 | bytes 12235264 | tf_op jit(solution)/shard_map/dot_general | solution.py:86
  154.2 3.5 %convert_bitcast_fusion = bf16[1,896,1024]{1,2,0:T(8,128)(2,1)S(1)} fusion(bf16[576,1024]{1,0:T(8,128)(2,1)} %collective-permute-done.9, bf16[2,576,896]{2,1,0:T(8,128)(2,1)} %collective-permute-done.8), kind=kOutput, calls=%fused_computation.27 | convolution fusion | flops 1057882112 | bytes 4046848 | tf_op jit(solution)/shard_map/dot_general | solution.py:101
  159.6 2.7 %collective-permute-done.11 = f32[2,576]{1,0:T(2,128)S(1)} collective-permute-done((f32[2,576]{1,0:T(2,128)S(1)}, f32[2,576]{1,0:T(2,128)S(1)}, u32[]{:S(2)}, u32[]{:S(2)}) %collective-permute-start.11) | collective-permute-done | bytes 4640 | tf_op jit(solution)/shard_map/ppermute | solution.py:10
  162.4 3.6 %collective-permute-start.12 = (f32[2,576]{1,0:T(2,128)S(1)}, f32[2,576]{1,0:T(2,128)S(1)}, u32[]{:S(2)}, u32[]{:S(2)}) collective-permute-start(f32[2,576]{1,0:T(2,128)S(1)} %fusion.32), channel_id=1, source_target_pairs={{0,8},{2,10},{4,12},{6,14},{8,0},{10,2},{12,4},{14,6},{1,9},{3,11}... | collective-permute-start | bytes 13832 | tf_op jit(solution)/shard_map/ppermute | solution.py:10
  166.0 2.7 %add_convert_fusion = bf16[2,896,1024]{1,2,0:T(8,128)(2,1)} fusion(bf16[2,896,1024]{1,2,0:T(8,128)(2,1)S(1)} %pad_maximum_fusion.1, bf16[2,896,1024]{1,2,0:T(8,128)(2,1)S(1)} %copy-done), kind=kLoop, calls=%fused_computation | loop fusion | flops 7340032 | bytes 11010048 | tf_op jit(solution)/shard_map/convert_element_type | solution.py:120
  168.7 6.1 %copy.46 = bf16[2,896,1024]{2,1,0:T(8,128)(2,1)} copy(bf16[2,896,1024]{1,2,0:T(8,128)(2,1)} %add_convert_fusion) | data formatting | bytes 7340032
  175.6 6.3 %all-to-all-start.3 = ((f32[2,16,36]{2,0,1:T(2,128)}), f32[2,16,36]{2,0,1:T(2,128)S(1)}, u32[]{:S(2)}, u32[]{:S(2)}) async-start(f32[2,16,36]{2,0,1:T(2,128)} %copy.45), calls=%async_computation.3 | async-start | bytes 32768 | tf_op jit(solution)/shard_map/all_to_all | solution.py:107
  183.4 4.8 %all-to-all-done.3 = f32[2,16,36]{2,0,1:T(2,128)S(1)} async-done(((f32[2,16,36]{2,0,1:T(2,128)}), f32[2,16,36]{2,0,1:T(2,128)S(1)}, u32[]{:S(2)}, u32[]{:S(2)}) %all-to-all-start.3) | async-done | bytes 4640 | tf_op jit(solution)/shard_map/all_to_all | solution.py:107
  (111 shorter events, 33.3 us)
Async XLA Ops:
  7.2 6.1 %copy-start.10 = (s32[512,2]{0,1:T(2,128)S(1)}, s32[512,2]{0,1:T(2,128)}, u32[]{:S(2)}) copy-start(s32[512,2]{0,1:T(2,128)} %param.7) | copy-start | bytes 12292
  7.2 136.4 %all-gather.2.cloned.1.call-start = ((), (), s32[]{:S(2)}) async-start(), calls=%async_computation.4 | async-start | bytes 11010048 | tf_op jit(solution)/shard_map/all_gather | solution.py:72
  7.2 17.2 %collective-permute-start = (bf16[512,256]{1,0:T(8,128)(2,1)}, bf16[512,256]{1,0:T(8,128)(2,1)}, u32[]{:S(2)}, u32[]{:S(2)}) collective-permute-start(bf16[512,256]{1,0:T(8,128)(2,1)} %param.6), channel_id=1, source_target_pairs={{0,2},{2,4},{4,6},{6,8},{8,10},{10,12},{12,14},{14,0},{1,3},{3,5},... | collective-permute-start | bytes 786440 | tf_op jit(solution)/shard_map/ppermute | solution.py:31
  9.2 15.8 %collective-permute-start.1 = (bf16[512,256]{1,0:T(8,128)(2,1)}, bf16[512,256]{1,0:T(8,128)(2,1)S(1)}, u32[]{:S(2)}, u32[]{:S(2)}) collective-permute-start(bf16[512,256]{1,0:T(8,128)(2,1)} %param.6), channel_id=1, source_target_pairs={{0,14},{2,0},{4,2},{6,4},{8,6},{10,8},{12,10},{14,12},{1,15},{3,1}... | collective-permute-start | bytes 786440 | tf_op jit(solution)/shard_map/ppermute | solution.py:36
  15.1 13.4 %copy-start.9 = (bf16[512,256]{1,0:T(8,128)(2,1)S(1)}, bf16[512,256]{1,0:T(8,128)(2,1)}, u32[]{:S(2)}) copy-start(bf16[512,256]{1,0:T(8,128)(2,1)} %param.6) | copy-start | bytes 786436
  16.9 34.8 %all-to-all-start = ((bf16[16,2,36]{2,1,0:T(2,128)(2,1)}), bf16[16,2,36]{2,1,0:T(2,128)(2,1)S(1)}, u32[]{:S(2)}, u32[]{:S(2)}) async-start(bf16[16,2,36]{2,1,0:T(2,128)(2,1)} %reshape.77), calls=%async_computation | async-start | bytes 16384 | tf_op jit(solution)/shard_map/all_to_all | solution.py:69
  24.4 8.8 %collective-permute-start.2 = (bf16[512,256]{1,0:T(8,128)(2,1)}, bf16[512,256]{1,0:T(8,128)(2,1)}, u32[]{:S(2)}, u32[]{:S(2)}) collective-permute-start(bf16[512,256]{1,0:T(8,128)(2,1)} %collective-permute-done), channel_id=1, source_target_pairs={{0,2},{2,4},{4,6},{6,8},{8,10},{10,12},{12,14},{14,0},{1,3},{3,5},... | collective-permute-start | bytes 786440 | tf_op jit(solution)/shard_map/ppermute | solution.py:31
  25.0 9.2 %collective-permute-start.3 = (bf16[512,256]{1,0:T(8,128)(2,1)S(1)}, bf16[512,256]{1,0:T(8,128)(2,1)}, u32[]{:S(2)}, u32[]{:S(2)}) collective-permute-start(bf16[512,256]{1,0:T(8,128)(2,1)S(1)} %collective-permute-done.1), channel_id=1, source_target_pairs={{0,14},{2,0},{4,2},{6,4},{8,6},{10,8},{12,10},{14,12},{1,15},{3,1}... | collective-permute-start | bytes 786440 | tf_op jit(solution)/shard_map/ppermute | solution.py:36
  33.2 7.8 %collective-permute-start.4 = (bf16[512,256]{1,0:T(8,128)(2,1)}, bf16[512,256]{1,0:T(8,128)(2,1)S(1)}, u32[]{:S(2)}, u32[]{:S(2)}) collective-permute-start(bf16[512,256]{1,0:T(8,128)(2,1)} %collective-permute-done.2), channel_id=1, source_target_pairs={{0,2},{2,4},{4,6},{6,8},{8,10},{10,12},{12,14},{14,0},{1,3},{3,5},... | collective-permute-start | bytes 786440 | tf_op jit(solution)/shard_map/ppermute | solution.py:31
  34.3 7.8 %collective-permute-start.5 = (bf16[512,256]{1,0:T(8,128)(2,1)}, bf16[512,256]{1,0:T(8,128)(2,1)S(1)}, u32[]{:S(2)}, u32[]{:S(2)}) collective-permute-start(bf16[512,256]{1,0:T(8,128)(2,1)} %collective-permute-done.3), channel_id=1, source_target_pairs={{0,14},{2,0},{4,2},{6,4},{8,6},{10,8},{12,10},{14,12},{1,15},{3,1}... | collective-permute-start | bytes 786440 | tf_op jit(solution)/shard_map/ppermute | solution.py:36
  41.0 7.6 %collective-permute-start.6 = (bf16[512,256]{1,0:T(8,128)(2,1)S(1)}, bf16[512,256]{1,0:T(8,128)(2,1)S(1)}, u32[]{:S(2)}, u32[]{:S(2)}) collective-permute-start(bf16[512,256]{1,0:T(8,128)(2,1)S(1)} %collective-permute-done.4), channel_id=1, source_target_pairs={{0,2},{2,4},{4,6},{6,8},{8,10},{10,12},{12,14},{14,0},{1,3},{3,5},... | collective-permute-start | bytes 786440 | tf_op jit(solution)/shard_map/ppermute | solution.py:31
  51.7 36.9 %all-to-all-start.1 = ((bf16[16,36,2048]{2,1,0:T(8,128)(2,1)}), bf16[16,36,2048]{2,1,0:T(8,128)(2,1)S(1)}, u32[]{:S(2)}, u32[]{:S(2)}) async-start(bf16[16,36,2048]{2,1,0:T(8,128)(2,1)} %convolution_convert_fusion.1), calls=%async_computation.1 | async-start | bytes 5242880 | tf_op jit(solution)/shard_map/all_to_all | solution.py:83
  88.6 38.1 %all-to-all-start.2 = ((bf16[16,36,2048]{2,1,0:T(8,128)(2,1)}), bf16[16,36,2048]{2,1,0:T(8,128)(2,1)}, u32[]{:S(2)}, u32[]{:S(2)}) async-start(bf16[16,36,2048]{2,1,0:T(8,128)(2,1)} %convolution_convert_fusion), calls=%async_computation.2 | async-start | bytes 5242880 | tf_op jit(solution)/shard_map/all_to_all | solution.py:83
  96.3 42.7 %collective-permute-start.8 = (bf16[2,576,896]{2,1,0:T(8,128)(2,1)}, bf16[2,576,896]{2,1,0:T(8,128)(2,1)}, u32[]{:S(2)}, u32[]{:S(2)}) collective-permute-start(bf16[2,576,896]{2,1,0:T(8,128)(2,1)} %param.10), channel_id=1, source_target_pairs={{0,1},{1,0},{2,3},{3,2},{4,5},{5,4},{6,7},{7,6},{8,9},{9,8},{10,11... | collective-permute-start | bytes 6193160 | tf_op jit(solution)/shard_map/ppermute | solution.py:10
  103.3 35.6 %collective-permute-start.7 = (bf16[576,1024]{1,0:T(8,128)(2,1)}, bf16[576,1024]{1,0:T(8,128)(2,1)}, u32[]{:S(2)}, u32[]{:S(2)}) collective-permute-start(bf16[576,1024]{1,0:T(8,128)(2,1)} %constant_dynamic-slice_fusion.1), channel_id=1, source_target_pairs={{0,1},{1,0},{2,3},{3,2},{4,5},{5,4},{6,7},{7,6},{8,9},{9,8},{10,11... | collective-permute-start | bytes 3538952 | tf_op jit(solution)/shard_map/ppermute | solution.py:10
  132.0 22.2 %collective-permute-start.9 = (bf16[576,1024]{1,0:T(8,128)(2,1)}, bf16[576,1024]{1,0:T(8,128)(2,1)}, u32[]{:S(2)}, u32[]{:S(2)}) collective-permute-start(bf16[576,1024]{1,0:T(8,128)(2,1)} %constant_dynamic-slice_fusion), channel_id=1, source_target_pairs={{0,1},{1,0},{2,3},{3,2},{4,5},{5,4},{6,7},{7,6},{8,9},{9,8},{10,11... | collective-permute-start | bytes 3538952 | tf_op jit(solution)/shard_map/ppermute | solution.py:10
  143.5 6.2 %copy-start.15 = (bf16[2,576,896]{2,1,0:T(8,128)(2,1)S(1)}, bf16[2,576,896]{2,1,0:T(8,128)(2,1)}, u32[]{:S(2)}) copy-start(bf16[2,576,896]{2,1,0:T(8,128)(2,1)} %param.10) | copy-start | bytes 6193156
  153.8 3.9 %collective-permute-start.10 = (f32[2,576]{1,0:T(2,128)S(1)}, f32[2,576]{1,0:T(2,128)S(1)}, u32[]{:S(2)}, u32[]{:S(2)}) collective-permute-start(f32[2,576]{1,0:T(2,128)S(1)} %pad_maximum_fusion.3), channel_id=1, source_target_pairs={{0,2},{2,0},{4,6},{6,4},{8,10},{10,8},{12,14},{14,12},{1,3},{3,1},... | collective-permute-start | bytes 13832 | tf_op jit(solution)/shard_map/ppermute | solution.py:10
  157.8 8.3 %copy-start = (bf16[2,896,1024]{1,2,0:T(8,128)(2,1)S(1)}, bf16[2,896,1024]{1,2,0:T(8,128)(2,1)}, u32[]{:S(2)}) copy-start(bf16[2,896,1024]{1,2,0:T(8,128)(2,1)} %pad_maximum_fusion) | copy-start | bytes 11010052
  157.8 4.6 %collective-permute-start.11 = (f32[2,576]{1,0:T(2,128)S(1)}, f32[2,576]{1,0:T(2,128)S(1)}, u32[]{:S(2)}, u32[]{:S(2)}) collective-permute-start(f32[2,576]{1,0:T(2,128)S(1)} %fusion.24), channel_id=1, source_target_pairs={{0,4},{2,6},{4,0},{6,2},{8,12},{10,14},{12,8},{14,10},{1,5},{3,7},... | collective-permute-start | bytes 13832 | tf_op jit(solution)/shard_map/ppermute | solution.py:10
  162.4 12.5 %collective-permute-start.12 = (f32[2,576]{1,0:T(2,128)S(1)}, f32[2,576]{1,0:T(2,128)S(1)}, u32[]{:S(2)}, u32[]{:S(2)}) collective-permute-start(f32[2,576]{1,0:T(2,128)S(1)} %fusion.32), channel_id=1, source_target_pairs={{0,8},{2,10},{4,12},{6,14},{8,0},{10,2},{12,4},{14,6},{1,9},{3,11}... | collective-permute-start | bytes 13832 | tf_op jit(solution)/shard_map/ppermute | solution.py:10
  168.7 13.2 %copy-start.7 = (bf16[1,576,896]{2,1,0:T(8,128)(2,1)S(1)}, bf16[1,576,896]{2,1,0:T(8,128)(2,1)}, u32[]{:S(2)}) copy-start(bf16[1,576,896]{2,1,0:T(8,128)(2,1)} %get-tuple-element.31) | copy-start | bytes 3096580
  168.7 13.2 %copy-start.8 = (bf16[1,576,896]{2,1,0:T(8,128)(2,1)S(1)}, bf16[1,576,896]{2,1,0:T(8,128)(2,1)}, u32[]{:S(2)}) copy-start(bf16[1,576,896]{2,1,0:T(8,128)(2,1)} %get-tuple-element.32) | copy-start | bytes 3096580
  175.6 12.6 %all-to-all-start.3 = ((f32[2,16,36]{2,0,1:T(2,128)}), f32[2,16,36]{2,0,1:T(2,128)S(1)}, u32[]{:S(2)}, u32[]{:S(2)}) async-start(f32[2,16,36]{2,0,1:T(2,128)} %copy.45), calls=%async_computation.3 | async-start | bytes 32768 | tf_op jit(solution)/shard_map/all_to_all | solution.py:107
  (10 other events, 30.1 us)
Sparse Core Ops, SparseCore 0:
  13.4 23.8 all-gather.1

commit v6 on v5

--- a/solution.py
+++ b/solution.py
@@ -103,13 +103,16 @@
             )
         )
     grad_hidden = jnp.stack(grad_rows)
-    scores = tree_sum(jnp.stack(scores_local), "tensor")
+    tensor_size = lax.axis_size("tensor")
+    partial = jnp.stack(scores_local).reshape(local_experts, experts, capacity).transpose(1, 0, 2)
+    outgoing_scores = jnp.broadcast_to(
+        partial[:, None], (experts, tensor_size, local_experts, capacity)
+    ).reshape(experts * tensor_size, local_experts, capacity)
     returned = lax.all_to_all(
-        scores.reshape(local_experts, experts, capacity),
-        "expert",
-        split_axis=1,
-        concat_axis=0,
-        tiled=True,
+        outgoing_scores, ("expert", "tensor"), split_axis=0, concat_axis=0, tiled=True
+    )
+    returned = jnp.sum(
+        returned.reshape(experts, tensor_size, local_experts, capacity), axis=1
     ).reshape(-1)
     picked = jnp.sum(
         jnp.where(position[:, None] == iota_p[None, :, 0], returned[None, :], 0.0), axis=1

time: 198 us -> 198 us (level)
  starting transfers between devices: 47.3 us -> 45 us
    ppermute x6 -> x3, starting transfers between devices: 5.92 us -> 0.49 us  [from_partner(): return lax.ppermute(value, axis, pairs)]
    all_to_all x1, waiting for transfers between devices: 4.76 us -> 8.78 us  [body(): lax.all_to_all(outgoing_scores, ('expert', 'tensor'), split_axis=0, conca...]
    all_to_all x1, starting transfers between devices: 6.29 us -> 9.48 us  [body(): lax.all_to_all(outgoing_scores, ('expert', 'tensor'), split_axis=0, conca...]
    ppermute x6 -> x3, waiting for transfers between devices: 2.82 us -> 0.01 us  [from_partner(): return lax.ppermute(value, axis, pairs)]
    unnamed x37 -> x31, local copies, waits for them, and re-layouts: 11.5 us -> 11.5 us
  transfers between devices with their start and end apart: 18 -> 15, of which waited for: 8 -> 6; matrix products, arithmetic and copies ran while one was open for 30% -> 25% of each run, Pallas kernels for 0% -> 0%
where the time goes in v6:
time: 198 us; the launch traced here: 196 us
  waiting for transfers between devices  70.2 us (35%)
  starting transfers between devices  45 us (23%)
  matrix products  30.6 us (15%)
  local copies, waits for them, and re-layouts  24.8 us (13%)
  between operations  14.7 us (7%)
  other arithmetic  10.4 us (5%)
    all_to_all x2, waiting for transfers between devices, body(): lax.all_to_all(outgoing, 'expert', split_axis=0, concat_axis=0, tiled=True)  47.2 us
    all_to_all x2, starting transfers between devices, body(): lax.all_to_all(outgoing, 'expert', split_axis=0, concat_axis=0, tiled=True)  14.8 us
    ppermute x4, waiting for transfers between devices, ring_gather(): going_right = lax.ppermute(going_right, axis, right)  13.5 us
    unnamed x31, local copies, waits for them, and re-layouts  11.5 us
    ppermute x3, starting transfers between devices, ring_gather(): going_left = lax.ppermute(going_left, axis, left)  10.6 us
    dot_general x2, matrix products, body(): jnp.dot(routed, full_weight[local].T, preferred_element_type=jnp.float32)  9.64 us
    all_to_all x1, starting transfers between devices, body(): lax.all_to_all(outgoing_scores, ('expert', 'tensor'), split_axis=0, conca...  9.48 us
    all_to_all x1, waiting for transfers between devices, body(): lax.all_to_all(outgoing_scores, ('expert', 'tensor'), split_axis=0, conca...  8.78 us
  transfers between devices with their start and end apart: 15, of which 6 were waited for; matrix products, arithmetic and copies ran while one was open for 25% of the time, Pallas kernels for 0%

profile of v6, /device:TPU:2, one launch (start us, length us, event | category | flops | bytes accessed | tf_op | source)
XLA Modules:
  0.0 195.7 jit_solution(5335552436030907526)
XLA Ops:
  9.2 4.0 %collective-permute-start.1 = (bf16[512,256]{1,0:T(8,128)(2,1)}, bf16[512,256]{1,0:T(8,128)(2,1)S(1)}, u32[]{:S(2)}, u32[]{:S(2)}) collective-permute-start(bf16[512,256]{1,0:T(8,128)(2,1)} %param.6), channel_id=1, source_target_pairs={{0,14},{2,0},{4,2},{6,4},{8,6},{10,8},{12,10},{14,12},{1,15},{3,1}... | collective-permute-start | bytes 786440 | tf_op jit(solution)/shard_map/ppermute | solution.py:36
  17.5 7.5 %all-to-all-start = ((bf16[16,2,36]{2,1,0:T(2,128)(2,1)}), bf16[16,2,36]{2,1,0:T(2,128)(2,1)S(1)}, u32[]{:S(2)}, u32[]{:S(2)}) async-start(bf16[16,2,36]{2,1,0:T(2,128)(2,1)} %reshape.85), calls=%async_computation | async-start | bytes 16384 | tf_op jit(solution)/shard_map/all_to_all | solution.py:69
  25.6 3.3 %collective-permute-start.3 = (bf16[512,256]{1,0:T(8,128)(2,1)S(1)}, bf16[512,256]{1,0:T(8,128)(2,1)}, u32[]{:S(2)}, u32[]{:S(2)}) collective-permute-start(bf16[512,256]{1,0:T(8,128)(2,1)S(1)} %collective-permute-done.1), channel_id=1, source_target_pairs={{0,14},{2,0},{4,2},{6,4},{8,6},{10,8},{12,10},{14,12},{1,15},{3,1}... | collective-permute-start | bytes 786440 | tf_op jit(solution)/shard_map/ppermute | solution.py:36
  29.3 4.5 %collective-permute-done.2 = bf16[512,256]{1,0:T(8,128)(2,1)} collective-permute-done((bf16[512,256]{1,0:T(8,128)(2,1)}, bf16[512,256]{1,0:T(8,128)(2,1)}, u32[]{:S(2)}, u32[]{:S(2)}) %collective-permute-start.2) | collective-permute-done | bytes 262176 | tf_op jit(solution)/shard_map/ppermute | solution.py:31
  34.9 3.3 %collective-permute-start.5 = (bf16[512,256]{1,0:T(8,128)(2,1)}, bf16[512,256]{1,0:T(8,128)(2,1)S(1)}, u32[]{:S(2)}, u32[]{:S(2)}) collective-permute-start(bf16[512,256]{1,0:T(8,128)(2,1)} %collective-permute-done.3), channel_id=1, source_target_pairs={{0,14},{2,0},{4,2},{6,4},{8,6},{10,8},{12,10},{14,12},{1,15},{3,1}... | collective-permute-start | bytes 786440 | tf_op jit(solution)/shard_map/ppermute | solution.py:36
  39.1 2.5 %collective-permute-done.4 = bf16[512,256]{1,0:T(8,128)(2,1)S(1)} collective-permute-done((bf16[512,256]{1,0:T(8,128)(2,1)}, bf16[512,256]{1,0:T(8,128)(2,1)S(1)}, u32[]{:S(2)}, u32[]{:S(2)}) %collective-permute-start.4) | collective-permute-done | bytes 262176 | tf_op jit(solution)/shard_map/ppermute | solution.py:31
  42.7 6.5 %collective-permute-done.6 = bf16[512,256]{1,0:T(8,128)(2,1)S(1)} collective-permute-done((bf16[512,256]{1,0:T(8,128)(2,1)S(1)}, bf16[512,256]{1,0:T(8,128)(2,1)S(1)}, u32[]{:S(2)}, u32[]{:S(2)}) %collective-permute-start.6) | collective-permute-done | bytes 262176 | tf_op jit(solution)/shard_map/ppermute | solution.py:31
  49.2 3.1 %convolution_convert_fusion.1 = bf16[16,36,2048]{2,1,0:T(8,128)(2,1)} fusion(bf16[512,2048]{1,0:T(8,128)(2,1)S(1)} %constant_dynamic-update-slice_fusion, pred[16,2,36,512]{3,2,0,1:T(8,128)(4,1)S(1)} %compare_or_fusion), kind=kOutput, calls=%fused_computation.14 | convolution fusion | flops 1209139200 | bytes 4784128 | tf_op jit(solution)/shard_map/dot_general | solution.py:79
  52.3 7.2 %all-to-all-start.1 = ((bf16[16,36,2048]{2,1,0:T(8,128)(2,1)}), bf16[16,36,2048]{2,1,0:T(8,128)(2,1)S(1)}, u32[]{:S(2)}, u32[]{:S(2)}) async-start(bf16[16,36,2048]{2,1,0:T(8,128)(2,1)} %convolution_convert_fusion.1), calls=%async_computation.1 | async-start | bytes 5242880 | tf_op jit(solution)/shard_map/all_to_all | solution.py:83
  60.3 4.6 %convolution_convert_fusion = bf16[16,36,2048]{2,1,0:T(8,128)(2,1)} fusion(bf16[512,2048]{1,0:T(8,128)(2,1)} %copy-done.5, pred[16,2,36,512]{3,2,0,1:T(8,128)(4,1)S(1)} %compare_or_fusion), kind=kOutput, calls=%fused_computation.13 | convolution fusion | flops 1209139200 | bytes 4784128 | tf_op jit(solution)/shard_map/dot_general | solution.py:79
  64.9 24.3 %all-to-all-done.1 = bf16[16,36,2048]{2,1,0:T(8,128)(2,1)S(1)} async-done(((bf16[16,36,2048]{2,1,0:T(8,128)(2,1)}), bf16[16,36,2048]{2,1,0:T(8,128)(2,1)S(1)}, u32[]{:S(2)}, u32[]{:S(2)}) %all-to-all-start.1) | async-done | bytes 2359328 | tf_op jit(solution)/shard_map/all_to_all | solution.py:83
  89.3 7.6 %all-to-all-start.2 = ((bf16[16,36,2048]{2,1,0:T(8,128)(2,1)}), bf16[16,36,2048]{2,1,0:T(8,128)(2,1)}, u32[]{:S(2)}, u32[]{:S(2)}) async-start(bf16[16,36,2048]{2,1,0:T(8,128)(2,1)} %convolution_convert_fusion), calls=%async_computation.2 | async-start | bytes 5242880 | tf_op jit(solution)/shard_map/all_to_all | solution.py:83
  104.4 22.9 %all-to-all-done.2 = bf16[16,36,2048]{2,1,0:T(8,128)(2,1)} async-done(((bf16[16,36,2048]{2,1,0:T(8,128)(2,1)}), bf16[16,36,2048]{2,1,0:T(8,128)(2,1)}, u32[]{:S(2)}, u32[]{:S(2)}) %all-to-all-start.2) | async-done | bytes 2359328 | tf_op jit(solution)/shard_map/all_to_all | solution.py:83
  127.3 2.7 %reshape.87 = bf16[576,2048]{1,0:T(8,128)(2,1)S(1)} reshape(bf16[16,36,2048]{2,1,0:T(8,128)(2,1)} %all-to-all-done.2) | data formatting | bytes 4718592 | tf_op jit(solution)/shard_map/reshape | solution.py:85
  133.3 3.5 %convert_bitcast_fusion.3 = bf16[1,896,1024]{1,2,0:T(8,128)(2,1)S(1)} fusion(bf16[576,2048]{1,0:T(8,128)(2,1)} %copy-done.2, s32[]{:T(128)S(6)} %select_n.87, bf16[2,576,896]{2,1,0:T(8,128)(2,1)} %param.10), kind=kOutput, calls=%fused_computation.30 | convolution fusion | flops 1057882112 | bytes 4046852 | tf_op jit(solution)/shard_map/dot_general | solution.py:96
  139.1 3.4 %convert_bitcast_fusion.1 = bf16[1,896,1024]{1,2,0:T(8,128)(2,1)S(1)} fusion(bf16[576,1024]{1,0:T(8,128)(2,1)} %collective-permute-done.7, bf16[2,576,896]{2,1,0:T(8,128)(2,1)} %collective-permute-done.8), kind=kOutput, calls=%fused_computation.28 | convolution fusion | flops 1057882112 | bytes 4046848 | tf_op jit(solution)/shard_map/dot_general | solution.py:101
  142.4 3.0 %convert_bitcast_fusion = bf16[1,896,1024]{1,2,0:T(8,128)(2,1)S(1)} fusion(bf16[576,1024]{1,0:T(8,128)(2,1)S(1)} %collective-permute-done.9, bf16[2,576,896]{2,1,0:T(8,128)(2,1)} %collective-permute-done.8), kind=kOutput, calls=%fused_computation.27 | convolution fusion | flops 1057882112 | bytes 4046848 | tf_op jit(solution)/shard_map/dot_general | solution.py:101
  145.8 2.7 %add_convert_fusion = bf16[2,896,1024]{1,2,0:T(8,128)(2,1)} fusion(bf16[2,896,1024]{1,2,0:T(8,128)(2,1)S(1)} %pad_maximum_fusion.1, bf16[2,896,1024]{1,2,0:T(8,128)(2,1)S(1)} %pad_maximum_fusion), kind=kLoop, calls=%fused_computation | loop fusion | flops 7340032 | bytes 11010048 | tf_op jit(solution)/shard_map/convert_element_type | solution.py:123
  148.5 6.0 %copy.58 = bf16[2,896,1024]{2,1,0:T(8,128)(2,1)} copy(bf16[2,896,1024]{1,2,0:T(8,128)(2,1)} %add_convert_fusion) | data formatting | bytes 7340032
  154.5 5.5 %fusion.1 = f32[576,896]{1,0:T(8,128)S(1)} fusion(bf16[576,2048]{1,0:T(8,128)(2,1)} %copy-done.1, bf16[2,896,2048]{2,1,0:T(8,128)(2,1)} %all-gather.2.cloned.1.call-done), kind=kOutput, calls=%fused_computation.8 | convolution fusion | flops 2113929216 | bytes 8093696 | tf_op jit(solution)/shard_map/dot_general | solution.py:86
  160.6 4.1 %multiply_reduce_fusion.1 = (f32[576]{0:T(1024)S(1)}, f32[576]{0:T(1024)S(1)}, bf16[1,576,896]{2,1,0:T(8,128)(2,1)}, bf16[1,576,896]{2,1,0:T(8,128)(2,1)}) fusion(bf16[2,576,896]{2,1,0:T(8,128)(2,1)S(1)} %copy-done.12, f32[576,896]{1,0:T(8,128)S(1)} %fusion.1, f32[576]{0:T(1024)S(1)} %mul.110, f32[576]{0:T(1024)S(1)} %mul.98, ...), kind=kOutput, calls=%fused_computation.24 | convolution fusion | flops 2119089152 | bytes 12235264 | tf_op jit(solution)/shard_map/dot_general | solution.py:86
  165.6 9.5 %all-to-all-start.3 = ((f32[128,2,36]{2,1,0:T(2,128)}), f32[128,2,36]{2,1,0:T(2,128)S(1)}, u32[]{:S(2)}, u32[]{:S(2)}) async-start(f32[128,2,36]{2,1,0:T(2,128)} %bitcast.25), calls=%async_computation.3 | async-start | bytes 262144 | tf_op jit(solution)/shard_map/all_to_all | solution.py:111
  175.1 3.0 %pad_maximum_fusion.2 = bf16[2,576,896]{2,1,0:T(8,128)(2,1)} fusion(bf16[1,576,896]{2,1,0:T(8,128)(2,1)} %get-tuple-element.34, bf16[1,576,896]{2,1,0:T(8,128)(2,1)} %get-tuple-element.35), kind=kLoop, calls=%fused_computation.22 | loop fusion | flops 1032192 | bytes 4128768 | tf_op jit(solution)/shard_map/stack | solution.py:105
  178.2 8.8 %all-to-all-done.3 = f32[128,2,36]{2,1,0:T(2,128)S(1)} async-done(((f32[128,2,36]{2,1,0:T(2,128)}), f32[128,2,36]{2,1,0:T(2,128)S(1)}, u32[]{:S(2)}, u32[]{:S(2)}) %all-to-all-start.3) | async-done | bytes 36896 | tf_op jit(solution)/shard_map/all_to_all | solution.py:111
  (96 shorter events, 27.5 us)
Async XLA Ops:
  7.2 7.9 %copy-start.7 = (s32[512,2]{0,1:T(2,128)S(1)}, s32[512,2]{0,1:T(2,128)}, u32[]{:S(2)}) copy-start(s32[512,2]{0,1:T(2,128)} %param.7) | copy-start | bytes 12292
  7.2 8.0 %copy-start.8 = (s32[512,2]{0,1:T(2,128)S(1)}, s32[512,2]{0,1:T(2,128)}, u32[]{:S(2)}) copy-start(s32[512,2]{0,1:T(2,128)} %param.9) | copy-start | bytes 12292
  7.2 8.1 %copy-start.9 = (f32[512,2]{0,1:T(2,128)S(1)}, f32[512,2]{0,1:T(2,128)}, u32[]{:S(2)}) copy-start(f32[512,2]{0,1:T(2,128)} %param.8) | copy-start | bytes 12292
  7.2 17.8 %collective-permute-start = (bf16[512,256]{1,0:T(8,128)(2,1)}, bf16[512,256]{1,0:T(8,128)(2,1)}, u32[]{:S(2)}, u32[]{:S(2)}) collective-permute-start(bf16[512,256]{1,0:T(8,128)(2,1)} %param.6), channel_id=1, source_target_pairs={{0,2},{2,4},{4,6},{6,8},{8,10},{10,12},{12,14},{14,0},{1,3},{3,5},... | collective-permute-start | bytes 786440 | tf_op jit(solution)/shard_map/ppermute | solution.py:31
  9.2 16.4 %collective-permute-start.1 = (bf16[512,256]{1,0:T(8,128)(2,1)}, bf16[512,256]{1,0:T(8,128)(2,1)S(1)}, u32[]{:S(2)}, u32[]{:S(2)}) collective-permute-start(bf16[512,256]{1,0:T(8,128)(2,1)} %param.6), channel_id=1, source_target_pairs={{0,14},{2,0},{4,2},{6,4},{8,6},{10,8},{12,10},{14,12},{1,15},{3,1}... | collective-permute-start | bytes 786440 | tf_op jit(solution)/shard_map/ppermute | solution.py:36
  15.7 13.4 %copy-start.6 = (bf16[512,256]{1,0:T(8,128)(2,1)S(1)}, bf16[512,256]{1,0:T(8,128)(2,1)}, u32[]{:S(2)}) copy-start(bf16[512,256]{1,0:T(8,128)(2,1)} %param.6) | copy-start | bytes 786436
  17.5 34.8 %all-to-all-start = ((bf16[16,2,36]{2,1,0:T(2,128)(2,1)}), bf16[16,2,36]{2,1,0:T(2,128)(2,1)S(1)}, u32[]{:S(2)}, u32[]{:S(2)}) async-start(bf16[16,2,36]{2,1,0:T(2,128)(2,1)} %reshape.85), calls=%async_computation | async-start | bytes 16384 | tf_op jit(solution)/shard_map/all_to_all | solution.py:69
  25.0 8.8 %collective-permute-start.2 = (bf16[512,256]{1,0:T(8,128)(2,1)}, bf16[512,256]{1,0:T(8,128)(2,1)}, u32[]{:S(2)}, u32[]{:S(2)}) collective-permute-start(bf16[512,256]{1,0:T(8,128)(2,1)} %collective-permute-done), channel_id=1, source_target_pairs={{0,2},{2,4},{4,6},{6,8},{8,10},{10,12},{12,14},{14,0},{1,3},{3,5},... | collective-permute-start | bytes 786440 | tf_op jit(solution)/shard_map/ppermute | solution.py:31
  25.6 9.2 %collective-permute-start.3 = (bf16[512,256]{1,0:T(8,128)(2,1)S(1)}, bf16[512,256]{1,0:T(8,128)(2,1)}, u32[]{:S(2)}, u32[]{:S(2)}) collective-permute-start(bf16[512,256]{1,0:T(8,128)(2,1)S(1)} %collective-permute-done.1), channel_id=1, source_target_pairs={{0,14},{2,0},{4,2},{6,4},{8,6},{10,8},{12,10},{14,12},{1,15},{3,1}... | collective-permute-start | bytes 786440 | tf_op jit(solution)/shard_map/ppermute | solution.py:36
  33.8 7.8 %collective-permute-start.4 = (bf16[512,256]{1,0:T(8,128)(2,1)}, bf16[512,256]{1,0:T(8,128)(2,1)S(1)}, u32[]{:S(2)}, u32[]{:S(2)}) collective-permute-start(bf16[512,256]{1,0:T(8,128)(2,1)} %collective-permute-done.2), channel_id=1, source_target_pairs={{0,2},{2,4},{4,6},{6,8},{8,10},{10,12},{12,14},{14,0},{1,3},{3,5},... | collective-permute-start | bytes 786440 | tf_op jit(solution)/shard_map/ppermute | solution.py:31
  34.9 7.8 %collective-permute-start.5 = (bf16[512,256]{1,0:T(8,128)(2,1)}, bf16[512,256]{1,0:T(8,128)(2,1)S(1)}, u32[]{:S(2)}, u32[]{:S(2)}) collective-permute-start(bf16[512,256]{1,0:T(8,128)(2,1)} %collective-permute-done.3), channel_id=1, source_target_pairs={{0,14},{2,0},{4,2},{6,4},{8,6},{10,8},{12,10},{14,12},{1,15},{3,1}... | collective-permute-start | bytes 786440 | tf_op jit(solution)/shard_map/ppermute | solution.py:36
  41.6 7.6 %collective-permute-start.6 = (bf16[512,256]{1,0:T(8,128)(2,1)S(1)}, bf16[512,256]{1,0:T(8,128)(2,1)S(1)}, u32[]{:S(2)}, u32[]{:S(2)}) collective-permute-start(bf16[512,256]{1,0:T(8,128)(2,1)S(1)} %collective-permute-done.4), channel_id=1, source_target_pairs={{0,2},{2,4},{4,6},{6,8},{8,10},{10,12},{12,14},{14,0},{1,3},{3,5},... | collective-permute-start | bytes 786440 | tf_op jit(solution)/shard_map/ppermute | solution.py:31
  52.3 36.9 %all-to-all-start.1 = ((bf16[16,36,2048]{2,1,0:T(8,128)(2,1)}), bf16[16,36,2048]{2,1,0:T(8,128)(2,1)S(1)}, u32[]{:S(2)}, u32[]{:S(2)}) async-start(bf16[16,36,2048]{2,1,0:T(8,128)(2,1)} %convolution_convert_fusion.1), calls=%async_computation.1 | async-start | bytes 5242880 | tf_op jit(solution)/shard_map/all_to_all | solution.py:83
  59.6 94.9 %all-gather.2.cloned.1.call-start = ((), (), s32[]{:S(2)}) async-start(), calls=%async_computation.4 | async-start | bytes 11010048 | tf_op jit(solution)/shard_map/all_gather | solution.py:72
  89.3 38.0 %all-to-all-start.2 = ((bf16[16,36,2048]{2,1,0:T(8,128)(2,1)}), bf16[16,36,2048]{2,1,0:T(8,128)(2,1)}, u32[]{:S(2)}, u32[]{:S(2)}) async-start(bf16[16,36,2048]{2,1,0:T(8,128)(2,1)} %convolution_convert_fusion), calls=%async_computation.2 | async-start | bytes 5242880 | tf_op jit(solution)/shard_map/all_to_all | solution.py:83
  96.9 42.2 %collective-permute-start.8 = (bf16[2,576,896]{2,1,0:T(8,128)(2,1)}, bf16[2,576,896]{2,1,0:T(8,128)(2,1)}, u32[]{:S(2)}, u32[]{:S(2)}) collective-permute-start(bf16[2,576,896]{2,1,0:T(8,128)(2,1)} %param.10), channel_id=1, source_target_pairs={{0,1},{1,0},{2,3},{3,2},{4,5},{5,4},{6,7},{7,6},{8,9},{9,8},{10,11... | collective-permute-start | bytes 6193160 | tf_op jit(solution)/shard_map/ppermute | solution.py:10
  103.9 35.1 %collective-permute-start.7 = (bf16[576,1024]{1,0:T(8,128)(2,1)}, bf16[576,1024]{1,0:T(8,128)(2,1)}, u32[]{:S(2)}, u32[]{:S(2)}) collective-permute-start(bf16[576,1024]{1,0:T(8,128)(2,1)} %constant_dynamic-slice_fusion.1), channel_id=1, source_target_pairs={{0,1},{1,0},{2,3},{3,2},{4,5},{5,4},{6,7},{7,6},{8,9},{9,8},{10,11... | collective-permute-start | bytes 3538952 | tf_op jit(solution)/shard_map/ppermute | solution.py:10
  133.3 9.1 %collective-permute-start.9 = (bf16[576,1024]{1,0:T(8,128)(2,1)}, bf16[576,1024]{1,0:T(8,128)(2,1)S(1)}, u32[]{:S(2)}, u32[]{:S(2)}) collective-permute-start(bf16[576,1024]{1,0:T(8,128)(2,1)} %constant_dynamic-slice_fusion), channel_id=1, source_target_pairs={{0,1},{1,0},{2,3},{3,2},{4,5},{5,4},{6,7},{7,6},{8,9},{9,8},{10,11... | collective-permute-start | bytes 3538952 | tf_op jit(solution)/shard_map/ppermute | solution.py:10
  133.3 3.5 %copy-start.4 = (bf16[576,2048]{1,0:T(8,128)(2,1)S(1)}, bf16[576,2048]{1,0:T(8,128)(2,1)}, u32[]{:S(2)}) copy-start(bf16[576,2048]{1,0:T(8,128)(2,1)} %copy-done.3) | copy-start | bytes 7077892
  133.3 3.5 %copy-start.11 = (bf16[2,576,896]{2,1,0:T(8,128)(2,1)S(1)}, bf16[2,576,896]{2,1,0:T(8,128)(2,1)}, u32[]{:S(2)}) copy-start(bf16[2,576,896]{2,1,0:T(8,128)(2,1)} %param.10) | copy-start | bytes 6193156
  154.5 5.5 %copy-start = (bf16[576,2048]{1,0:T(8,128)(2,1)S(1)}, bf16[576,2048]{1,0:T(8,128)(2,1)}, u32[]{:S(2)}) copy-start(bf16[576,2048]{1,0:T(8,128)(2,1)} %reshape.86) | copy-start | bytes 7077892
  154.5 5.6 %copy-start.10 = (bf16[2,896,2048]{2,1,0:T(8,128)(2,1)S(1)}, bf16[2,896,2048]{2,1,0:T(8,128)(2,1)}, u32[]{:S(2)}) copy-start(bf16[2,896,2048]{2,1,0:T(8,128)(2,1)} %all-gather.2.cloned.1.call-done) | copy-start | bytes 22020100
  154.5 6.2 %copy-start.12 = (bf16[2,576,896]{2,1,0:T(8,128)(2,1)S(1)}, bf16[2,576,896]{2,1,0:T(8,128)(2,1)}, u32[]{:S(2)}) copy-start(bf16[2,576,896]{2,1,0:T(8,128)(2,1)} %param.10) | copy-start | bytes 6193156
  165.6 21.3 %all-to-all-start.3 = ((f32[128,2,36]{2,1,0:T(2,128)}), f32[128,2,36]{2,1,0:T(2,128)S(1)}, u32[]{:S(2)}, u32[]{:S(2)}) async-start(f32[128,2,36]{2,1,0:T(2,128)} %bitcast.25), calls=%async_computation.3 | async-start | bytes 262144 | tf_op jit(solution)/shard_map/all_to_all | solution.py:111
  (4 other events, 7.8 us)
Sparse Core Ops, SparseCore 0:
  62.2 23.3 all-gather.1

commit v7 on v6

--- a/solution.py
+++ b/solution.py
@@ -92,22 +92,24 @@
         own_cols = lax.dynamic_slice_in_dim(scaled, dp_index * half_width, half_width, 1)
         theirs = lax.dynamic_slice_in_dim(scaled, (1 - dp_index) * half_width, half_width, 1)
         peer_scaled = from_partner(theirs, "dp", 0)
-        own_terms.append(
-            jnp.dot(hidden_act[local].T, own_cols, preferred_element_type=jnp.float32).astype(
-                jnp.bfloat16
-            )
-        )
-        peer_terms.append(
-            jnp.dot(peer_hidden[local].T, peer_scaled, preferred_element_type=jnp.float32).astype(
-                jnp.bfloat16
-            )
-        )
+        own_terms.append(own_cols)
+        peer_terms.append(peer_scaled)
     grad_hidden = jnp.stack(grad_rows)
     tensor_size = lax.axis_size("tensor")
     partial = jnp.stack(scores_local).reshape(local_experts, experts, capacity).transpose(1, 0, 2)
     outgoing_scores = jnp.broadcast_to(
         partial[:, None], (experts, tensor_size, local_experts, capacity)
     ).reshape(experts * tensor_size, local_experts, capacity)
+    outgoing_scores, term_hidden, term_peer = lax.optimization_barrier(
+        (outgoing_scores, hidden_act, peer_hidden)
+    )
+    for local in range(local_experts):
+        own_terms[local] = jnp.dot(
+            term_hidden[local].T, own_terms[local], preferred_element_type=jnp.float32
+        ).astype(jnp.bfloat16)
+        peer_terms[local] = jnp.dot(
+            term_peer[local].T, peer_terms[local], preferred_element_type=jnp.float32
+        ).astype(jnp.bfloat16)
     returned = lax.all_to_all(
         outgoing_scores, ("expert", "tensor"), split_axis=0, concat_axis=0, tiled=True
     )

time: 198 us -> 191 us (0.965)
  local copies, waits for them, and re-layouts: 24.8 us -> 18 us
  other arithmetic: 10.4 us -> 16.7 us
  waiting for transfers between devices: 70.2 us -> 64.5 us
    unnamed x31 -> x34, local copies, waits for them, and re-layouts: 11.5 us -> 4.69 us
    all_to_all x1, waiting for transfers between devices: 8.78 us -> 3.01 us  [body(): lax.all_to_all(outgoing_scores, ('expert', 'tensor'), split_axis=0, conca...]
    convert_element_type x1, other arithmetic: 2.66 us -> 6.98 us  [body(): grad_down = summed.astype(jnp.bfloat16)]
  transfers between devices with their start and end apart: 15 -> 15, of which waited for: 6 -> 6; matrix products, arithmetic and copies ran while one was open for 25% -> 28% of each run, Pallas kernels for 0% -> 0%
where the time goes in v7:
time: 191 us; the launch traced here: 189 us
  waiting for transfers between devices  64.5 us (34%)
  starting transfers between devices  45 us (24%)
  matrix products  30.3 us (16%)
  local copies, waits for them, and re-layouts  18 us (9%)
  other arithmetic  16.7 us (9%)
  between operations  14.7 us (8%)
    all_to_all x2, waiting for transfers between devices, body(): lax.all_to_all(outgoing, 'expert', split_axis=0, concat_axis=0, tiled=True)  48 us
    all_to_all x2, starting transfers between devices, body(): lax.all_to_all(outgoing, 'expert', split_axis=0, concat_axis=0, tiled=True)  14.8 us
    ppermute x4, waiting for transfers between devices, ring_gather(): going_right = lax.ppermute(going_right, axis, right)  13.5 us
    ppermute x3, starting transfers between devices, ring_gather(): going_left = lax.ppermute(going_left, axis, left)  10.6 us
    dot_general x2, matrix products, body(): jnp.dot(routed, full_weight[local].T, preferred_element_type=jnp.float32)  9.68 us
    all_to_all x1, starting transfers between devices, body(): lax.all_to_all(outgoing_scores, ('expert', 'tensor'), split_axis=0, conca...  9.48 us
    dot_general x2, matrix products, body(): lax.dot_general(placing[:, local], gathered, (((2,), (0,)), ((), ())), pr...  7.68 us
    all_to_all x1, starting transfers between devices, body(): lax.all_to_all(slot_scale, 'expert', split_axis=0, concat_axis=2, tiled=T...  7.48 us
  transfers between devices with their start and end apart: 15, of which 6 were waited for; matrix products, arithmetic and copies ran while one was open for 28% of the time, Pallas kernels for 0%

profile of v7, /device:TPU:2, one launch (start us, length us, event | category | flops | bytes accessed | tf_op | source)
XLA Modules:
  0.0 189.3 jit_solution(5310522387306363654)
XLA Ops:
  9.2 4.0 %collective-permute-start.1 = (bf16[512,256]{1,0:T(8,128)(2,1)}, bf16[512,256]{1,0:T(8,128)(2,1)S(1)}, u32[]{:S(2)}, u32[]{:S(2)}) collective-permute-start(bf16[512,256]{1,0:T(8,128)(2,1)} %param.6), channel_id=1, source_target_pairs={{0,14},{2,0},{4,2},{6,4},{8,6},{10,8},{12,10},{14,12},{1,15},{3,1}... | collective-permute-start | bytes 786440 | tf_op jit(solution)/shard_map/ppermute | solution.py:36
  16.9 7.5 %all-to-all-start.2 = ((bf16[16,2,36]{2,1,0:T(2,128)(2,1)}), bf16[16,2,36]{2,1,0:T(2,128)(2,1)S(1)}, u32[]{:S(2)}, u32[]{:S(2)}) async-start(bf16[16,2,36]{2,1,0:T(2,128)(2,1)} %reshape.92), calls=%async_computation.2 | async-start | bytes 16384 | tf_op jit(solution)/shard_map/all_to_all | solution.py:69
  25.0 3.3 %collective-permute-start.3 = (bf16[512,256]{1,0:T(8,128)(2,1)S(1)}, bf16[512,256]{1,0:T(8,128)(2,1)}, u32[]{:S(2)}, u32[]{:S(2)}) collective-permute-start(bf16[512,256]{1,0:T(8,128)(2,1)S(1)} %collective-permute-done.1), channel_id=1, source_target_pairs={{0,14},{2,0},{4,2},{6,4},{8,6},{10,8},{12,10},{14,12},{1,15},{3,1}... | collective-permute-start | bytes 786440 | tf_op jit(solution)/shard_map/ppermute | solution.py:36
  28.7 4.5 %collective-permute-done.2 = bf16[512,256]{1,0:T(8,128)(2,1)} collective-permute-done((bf16[512,256]{1,0:T(8,128)(2,1)}, bf16[512,256]{1,0:T(8,128)(2,1)}, u32[]{:S(2)}, u32[]{:S(2)}) %collective-permute-start.2) | collective-permute-done | bytes 262176 | tf_op jit(solution)/shard_map/ppermute | solution.py:31
  34.3 3.3 %collective-permute-start.5 = (bf16[512,256]{1,0:T(8,128)(2,1)}, bf16[512,256]{1,0:T(8,128)(2,1)S(1)}, u32[]{:S(2)}, u32[]{:S(2)}) collective-permute-start(bf16[512,256]{1,0:T(8,128)(2,1)} %collective-permute-done.3), channel_id=1, source_target_pairs={{0,14},{2,0},{4,2},{6,4},{8,6},{10,8},{12,10},{14,12},{1,15},{3,1}... | collective-permute-start | bytes 786440 | tf_op jit(solution)/shard_map/ppermute | solution.py:36
  38.5 2.5 %collective-permute-done.4 = bf16[512,256]{1,0:T(8,128)(2,1)S(1)} collective-permute-done((bf16[512,256]{1,0:T(8,128)(2,1)}, bf16[512,256]{1,0:T(8,128)(2,1)S(1)}, u32[]{:S(2)}, u32[]{:S(2)}) %collective-permute-start.4) | collective-permute-done | bytes 262176 | tf_op jit(solution)/shard_map/ppermute | solution.py:31
  42.1 6.5 %collective-permute-done.6 = bf16[512,256]{1,0:T(8,128)(2,1)S(1)} collective-permute-done((bf16[512,256]{1,0:T(8,128)(2,1)S(1)}, bf16[512,256]{1,0:T(8,128)(2,1)S(1)}, u32[]{:S(2)}, u32[]{:S(2)}) %collective-permute-start.6) | collective-permute-done | bytes 262176 | tf_op jit(solution)/shard_map/ppermute | solution.py:31
  48.6 3.1 %convolution_convert_fusion.1 = bf16[16,36,2048]{2,1,0:T(8,128)(2,1)} fusion(bf16[512,2048]{1,0:T(8,128)(2,1)S(1)} %constant_dynamic-update-slice_fusion, pred[16,2,36,512]{3,2,0,1:T(8,128)(4,1)S(1)} %compare_or_fusion), kind=kOutput, calls=%fused_computation.14 | convolution fusion | flops 1209139200 | bytes 4784128 | tf_op jit(solution)/shard_map/dot_general | solution.py:79
  51.7 7.2 %all-to-all-start = ((bf16[16,36,2048]{2,1,0:T(8,128)(2,1)}), bf16[16,36,2048]{2,1,0:T(8,128)(2,1)S(1)}, u32[]{:S(2)}, u32[]{:S(2)}) async-start(bf16[16,36,2048]{2,1,0:T(8,128)(2,1)} %convolution_convert_fusion.1), calls=%async_computation | async-start | bytes 5242880 | tf_op jit(solution)/shard_map/all_to_all | solution.py:83
  59.0 4.6 %convolution_convert_fusion = bf16[16,36,2048]{2,1,0:T(8,128)(2,1)} fusion(bf16[512,2048]{1,0:T(8,128)(2,1)} %copy-done.5, pred[16,2,36,512]{3,2,0,1:T(8,128)(4,1)S(1)} %compare_or_fusion), kind=kOutput, calls=%fused_computation.13 | convolution fusion | flops 1209139200 | bytes 4784128 | tf_op jit(solution)/shard_map/dot_general | solution.py:79
  63.6 25.1 %all-to-all-done = bf16[16,36,2048]{2,1,0:T(8,128)(2,1)S(1)} async-done(((bf16[16,36,2048]{2,1,0:T(8,128)(2,1)}), bf16[16,36,2048]{2,1,0:T(8,128)(2,1)S(1)}, u32[]{:S(2)}, u32[]{:S(2)}) %all-to-all-start) | async-done | bytes 2359328 | tf_op jit(solution)/shard_map/all_to_all | solution.py:83
  88.6 7.6 %all-to-all-start.1 = ((bf16[16,36,2048]{2,1,0:T(8,128)(2,1)}), bf16[16,36,2048]{2,1,0:T(8,128)(2,1)}, u32[]{:S(2)}, u32[]{:S(2)}) async-start(bf16[16,36,2048]{2,1,0:T(8,128)(2,1)} %convolution_convert_fusion), calls=%async_computation.1 | async-start | bytes 5242880 | tf_op jit(solution)/shard_map/all_to_all | solution.py:83
  96.5 2.1 %reshape.89 = bf16[576,2048]{1,0:T(8,128)(2,1)} reshape(bf16[16,36,2048]{2,1,0:T(8,128)(2,1)S(1)} %all-to-all-done) | data formatting | bytes 4718592 | tf_op jit(solution)/shard_map/reshape | solution.py:85
  103.8 22.9 %all-to-all-done.1 = bf16[16,36,2048]{2,1,0:T(8,128)(2,1)} async-done(((bf16[16,36,2048]{2,1,0:T(8,128)(2,1)}), bf16[16,36,2048]{2,1,0:T(8,128)(2,1)}, u32[]{:S(2)}, u32[]{:S(2)}) %all-to-all-start.1) | async-done | bytes 2359328 | tf_op jit(solution)/shard_map/all_to_all | solution.py:83
  126.7 2.7 %reshape.90 = bf16[576,2048]{1,0:T(8,128)(2,1)S(1)} reshape(bf16[16,36,2048]{2,1,0:T(8,128)(2,1)} %all-to-all-done.1) | data formatting | bytes 4718592 | tf_op jit(solution)/shard_map/reshape | solution.py:85
  132.6 5.5 %fusion.1 = f32[576,896]{1,0:T(8,128)S(1)} fusion(bf16[576,2048]{1,0:T(8,128)(2,1)} %copy-done.1, bf16[2,896,2048]{2,1,0:T(8,128)(2,1)} %all-gather.2.cloned.1.call-done), kind=kOutput, calls=%fused_computation.8 | convolution fusion | flops 2113929216 | bytes 8093696 | tf_op jit(solution)/shard_map/dot_general | solution.py:86
  138.8 4.2 %fusion.8 = (f32[576]{0:T(1024)S(1)}, f32[576]{0:T(1024)S(1)}, bf16[1,576,896]{2,1,0:T(8,128)(2,1)}, bf16[1,576,896]{2,1,0:T(8,128)(2,1)}) fusion(bf16[2,576,896]{2,1,0:T(8,128)(2,1)S(1)} %copy-done.13, f32[576,896]{1,0:T(8,128)S(1)} %fusion.1, f32[576]{0:T(1024)S(1)} %mul.108, f32[576]{0:T(1024)S(1)} %mul.112, bf16[576,2048]{1,0:T(8,128)(2,1)S(1)} %copy-done, ...), kind=kOutput, calls=%fused_computation.26 | convolution fusion | flops 2119089152 | bytes 12235264 | tf_op jit(solution)/shard_map/dot_general | solution.py:86
  143.8 3.4 %convert_bitcast_fusion.3 = bf16[1,896,1024]{2,1,0:T(8,128)(2,1)S(1)} fusion(bf16[576,2048]{1,0:T(8,128)(2,1)} %copy-done.2, s32[]{:T(128)S(6)} %select_n.87, bf16[2,576,896]{2,1,0:T(8,128)(2,1)} %param.10), kind=kOutput, calls=%fused_computation.32 | convolution fusion | flops 1057882112 | bytes 4046852 | tf_op jit(solution)/shard_map/dot_general | solution.py:107
  148.9 3.2 %convert_bitcast_fusion.1 = bf16[1,896,1024]{2,1,0:T(8,128)(2,1)S(1)} fusion(bf16[576,1024]{1,0:T(8,128)(2,1)} %collective-permute-done.8, bf16[2,576,896]{2,1,0:T(8,128)(2,1)} %collective-permute-done.7), kind=kOutput, calls=%fused_computation.30 | convolution fusion | flops 1057882112 | bytes 4046848 | tf_op jit(solution)/shard_map/dot_general | solution.py:110
  152.1 3.2 %convert_bitcast_fusion = bf16[1,896,1024]{2,1,0:T(8,128)(2,1)S(1)} fusion(bf16[576,1024]{1,0:T(8,128)(2,1)} %collective-permute-done.9, bf16[2,576,896]{2,1,0:T(8,128)(2,1)} %collective-permute-done.7), kind=kOutput, calls=%fused_computation.29 | convolution fusion | flops 1057882112 | bytes 4046848 | tf_op jit(solution)/shard_map/dot_general | solution.py:110
  155.3 2.2 %pad_maximum_fusion.1 = bf16[2,896,1024]{2,1,0:T(8,128)(2,1)} fusion(bf16[1,896,1024]{2,1,0:T(8,128)(2,1)S(1)} %convert_bitcast_fusion, bf16[1,896,1024]{2,1,0:T(8,128)(2,1)S(1)} %convert_bitcast_fusion.1), kind=kLoop, calls=%fused_computation.12 | loop fusion | flops 1835008 | bytes 7340032 | tf_op jit(solution)/shard_map/stack | solution.py:123
  159.6 9.5 %all-to-all-start.3 = ((f32[128,2,36]{2,1,0:T(2,128)}), f32[128,2,36]{2,1,0:T(2,128)S(1)}, u32[]{:S(2)}, u32[]{:S(2)}) async-start(f32[128,2,36]{2,1,0:T(2,128)} %bitcast.10), calls=%async_computation.3 | async-start | bytes 262144 | tf_op jit(solution)/shard_map/all_to_all | solution.py:113
  169.1 7.0 %add_convert_fusion = bf16[2,896,1024]{2,1,0:T(8,128)(2,1)} fusion(bf16[2,896,1024]{2,1,0:T(8,128)(2,1)} %pad_maximum_fusion.1, bf16[2,896,1024]{2,1,0:T(8,128)(2,1)} %pad_maximum_fusion), kind=kLoop, calls=%fused_computation | loop fusion | flops 7340032 | bytes 11010048 | tf_op jit(solution)/shard_map/convert_element_type | solution.py:125
  177.6 3.0 %all-to-all-done.3 = f32[128,2,36]{2,1,0:T(2,128)S(1)} async-done(((f32[128,2,36]{2,1,0:T(2,128)}), f32[128,2,36]{2,1,0:T(2,128)S(1)}, u32[]{:S(2)}, u32[]{:S(2)}) %all-to-all-start.3) | async-done | bytes 36896 | tf_op jit(solution)/shard_map/all_to_all | solution.py:113
  (99 shorter events, 26.6 us)
Async XLA Ops:
  7.2 6.1 %copy-start.9 = (s32[512,2]{0,1:T(2,128)S(1)}, s32[512,2]{0,1:T(2,128)}, u32[]{:S(2)}) copy-start(s32[512,2]{0,1:T(2,128)} %param.7) | copy-start | bytes 12292
  7.2 125.4 %all-gather.2.cloned.1.call-start = ((), (), s32[]{:S(2)}) async-start(), calls=%async_computation.4 | async-start | bytes 11010048 | tf_op jit(solution)/shard_map/all_gather | solution.py:72
  7.2 17.2 %collective-permute-start = (bf16[512,256]{1,0:T(8,128)(2,1)}, bf16[512,256]{1,0:T(8,128)(2,1)}, u32[]{:S(2)}, u32[]{:S(2)}) collective-permute-start(bf16[512,256]{1,0:T(8,128)(2,1)} %param.6), channel_id=1, source_target_pairs={{0,2},{2,4},{4,6},{6,8},{8,10},{10,12},{12,14},{14,0},{1,3},{3,5},... | collective-permute-start | bytes 786440 | tf_op jit(solution)/shard_map/ppermute | solution.py:31
  9.2 15.8 %collective-permute-start.1 = (bf16[512,256]{1,0:T(8,128)(2,1)}, bf16[512,256]{1,0:T(8,128)(2,1)S(1)}, u32[]{:S(2)}, u32[]{:S(2)}) collective-permute-start(bf16[512,256]{1,0:T(8,128)(2,1)} %param.6), channel_id=1, source_target_pairs={{0,14},{2,0},{4,2},{6,4},{8,6},{10,8},{12,10},{14,12},{1,15},{3,1}... | collective-permute-start | bytes 786440 | tf_op jit(solution)/shard_map/ppermute | solution.py:36
  15.1 13.4 %copy-start.8 = (bf16[512,256]{1,0:T(8,128)(2,1)S(1)}, bf16[512,256]{1,0:T(8,128)(2,1)}, u32[]{:S(2)}) copy-start(bf16[512,256]{1,0:T(8,128)(2,1)} %param.6) | copy-start | bytes 786436
  16.9 34.8 %all-to-all-start.2 = ((bf16[16,2,36]{2,1,0:T(2,128)(2,1)}), bf16[16,2,36]{2,1,0:T(2,128)(2,1)S(1)}, u32[]{:S(2)}, u32[]{:S(2)}) async-start(bf16[16,2,36]{2,1,0:T(2,128)(2,1)} %reshape.92), calls=%async_computation.2 | async-start | bytes 16384 | tf_op jit(solution)/shard_map/all_to_all | solution.py:69
  24.4 8.8 %collective-permute-start.2 = (bf16[512,256]{1,0:T(8,128)(2,1)}, bf16[512,256]{1,0:T(8,128)(2,1)}, u32[]{:S(2)}, u32[]{:S(2)}) collective-permute-start(bf16[512,256]{1,0:T(8,128)(2,1)} %collective-permute-done), channel_id=1, source_target_pairs={{0,2},{2,4},{4,6},{6,8},{8,10},{10,12},{12,14},{14,0},{1,3},{3,5},... | collective-permute-start | bytes 786440 | tf_op jit(solution)/shard_map/ppermute | solution.py:31
  25.0 9.2 %collective-permute-start.3 = (bf16[512,256]{1,0:T(8,128)(2,1)S(1)}, bf16[512,256]{1,0:T(8,128)(2,1)}, u32[]{:S(2)}, u32[]{:S(2)}) collective-permute-start(bf16[512,256]{1,0:T(8,128)(2,1)S(1)} %collective-permute-done.1), channel_id=1, source_target_pairs={{0,14},{2,0},{4,2},{6,4},{8,6},{10,8},{12,10},{14,12},{1,15},{3,1}... | collective-permute-start | bytes 786440 | tf_op jit(solution)/shard_map/ppermute | solution.py:36
  33.2 7.8 %collective-permute-start.4 = (bf16[512,256]{1,0:T(8,128)(2,1)}, bf16[512,256]{1,0:T(8,128)(2,1)S(1)}, u32[]{:S(2)}, u32[]{:S(2)}) collective-permute-start(bf16[512,256]{1,0:T(8,128)(2,1)} %collective-permute-done.2), channel_id=1, source_target_pairs={{0,2},{2,4},{4,6},{6,8},{8,10},{10,12},{12,14},{14,0},{1,3},{3,5},... | collective-permute-start | bytes 786440 | tf_op jit(solution)/shard_map/ppermute | solution.py:31
  34.3 7.8 %collective-permute-start.5 = (bf16[512,256]{1,0:T(8,128)(2,1)}, bf16[512,256]{1,0:T(8,128)(2,1)S(1)}, u32[]{:S(2)}, u32[]{:S(2)}) collective-permute-start(bf16[512,256]{1,0:T(8,128)(2,1)} %collective-permute-done.3), channel_id=1, source_target_pairs={{0,14},{2,0},{4,2},{6,4},{8,6},{10,8},{12,10},{14,12},{1,15},{3,1}... | collective-permute-start | bytes 786440 | tf_op jit(solution)/shard_map/ppermute | solution.py:36
  41.0 7.6 %collective-permute-start.6 = (bf16[512,256]{1,0:T(8,128)(2,1)S(1)}, bf16[512,256]{1,0:T(8,128)(2,1)S(1)}, u32[]{:S(2)}, u32[]{:S(2)}) collective-permute-start(bf16[512,256]{1,0:T(8,128)(2,1)S(1)} %collective-permute-done.4), channel_id=1, source_target_pairs={{0,2},{2,4},{4,6},{6,8},{8,10},{10,12},{12,14},{14,0},{1,3},{3,5},... | collective-permute-start | bytes 786440 | tf_op jit(solution)/shard_map/ppermute | solution.py:31
  51.7 36.9 %all-to-all-start = ((bf16[16,36,2048]{2,1,0:T(8,128)(2,1)}), bf16[16,36,2048]{2,1,0:T(8,128)(2,1)S(1)}, u32[]{:S(2)}, u32[]{:S(2)}) async-start(bf16[16,36,2048]{2,1,0:T(8,128)(2,1)} %convolution_convert_fusion.1), calls=%async_computation | async-start | bytes 5242880 | tf_op jit(solution)/shard_map/all_to_all | solution.py:83
  88.6 38.0 %all-to-all-start.1 = ((bf16[16,36,2048]{2,1,0:T(8,128)(2,1)}), bf16[16,36,2048]{2,1,0:T(8,128)(2,1)}, u32[]{:S(2)}, u32[]{:S(2)}) async-start(bf16[16,36,2048]{2,1,0:T(8,128)(2,1)} %convolution_convert_fusion), calls=%async_computation.1 | async-start | bytes 5242880 | tf_op jit(solution)/shard_map/all_to_all | solution.py:83
  96.2 46.9 %collective-permute-start.7 = (bf16[2,576,896]{2,1,0:T(8,128)(2,1)}, bf16[2,576,896]{2,1,0:T(8,128)(2,1)}, u32[]{:S(2)}, u32[]{:S(2)}) collective-permute-start(bf16[2,576,896]{2,1,0:T(8,128)(2,1)} %param.10), channel_id=1, source_target_pairs={{0,1},{1,0},{2,3},{3,2},{4,5},{5,4},{6,7},{7,6},{8,9},{9,8},{10,11... | collective-permute-start | bytes 6193160 | tf_op jit(solution)/shard_map/ppermute | solution.py:10
  103.3 45.6 %collective-permute-start.8 = (bf16[576,1024]{1,0:T(8,128)(2,1)}, bf16[576,1024]{1,0:T(8,128)(2,1)}, u32[]{:S(2)}, u32[]{:S(2)}) collective-permute-start(bf16[576,1024]{1,0:T(8,128)(2,1)} %constant_dynamic-slice_fusion.1), channel_id=1, source_target_pairs={{0,1},{1,0},{2,3},{3,2},{4,5},{5,4},{6,7},{7,6},{8,9},{9,8},{10,11... | collective-permute-start | bytes 3538952 | tf_op jit(solution)/shard_map/ppermute | solution.py:10
  132.6 5.6 %copy-start = (bf16[576,2048]{1,0:T(8,128)(2,1)S(1)}, bf16[576,2048]{1,0:T(8,128)(2,1)}, u32[]{:S(2)}) copy-start(bf16[576,2048]{1,0:T(8,128)(2,1)} %reshape.89) | copy-start | bytes 7077892
  132.6 19.5 %collective-permute-start.9 = (bf16[576,1024]{1,0:T(8,128)(2,1)}, bf16[576,1024]{1,0:T(8,128)(2,1)}, u32[]{:S(2)}, u32[]{:S(2)}) collective-permute-start(bf16[576,1024]{1,0:T(8,128)(2,1)} %constant_dynamic-slice_fusion), channel_id=1, source_target_pairs={{0,1},{1,0},{2,3},{3,2},{4,5},{5,4},{6,7},{7,6},{8,9},{9,8},{10,11... | collective-permute-start | bytes 3538952 | tf_op jit(solution)/shard_map/ppermute | solution.py:10
  132.6 5.6 %copy-start.12 = (bf16[2,896,2048]{2,1,0:T(8,128)(2,1)S(1)}, bf16[2,896,2048]{2,1,0:T(8,128)(2,1)}, u32[]{:S(2)}) copy-start(bf16[2,896,2048]{2,1,0:T(8,128)(2,1)} %all-gather.2.cloned.1.call-done) | copy-start | bytes 22020100
  132.6 6.2 %copy-start.13 = (bf16[2,576,896]{2,1,0:T(8,128)(2,1)S(1)}, bf16[2,576,896]{2,1,0:T(8,128)(2,1)}, u32[]{:S(2)}) copy-start(bf16[2,576,896]{2,1,0:T(8,128)(2,1)} %param.10) | copy-start | bytes 6193156
  143.8 3.4 %copy-start.4 = (bf16[576,2048]{1,0:T(8,128)(2,1)S(1)}, bf16[576,2048]{1,0:T(8,128)(2,1)}, u32[]{:S(2)}) copy-start(bf16[576,2048]{1,0:T(8,128)(2,1)} %copy-done.3) | copy-start | bytes 7077892
  143.8 3.4 %copy-start.14 = (bf16[2,576,896]{2,1,0:T(8,128)(2,1)S(1)}, bf16[2,576,896]{2,1,0:T(8,128)(2,1)}, u32[]{:S(2)}) copy-start(bf16[2,576,896]{2,1,0:T(8,128)(2,1)} %param.10) | copy-start | bytes 6193156
  159.6 21.0 %all-to-all-start.3 = ((f32[128,2,36]{2,1,0:T(2,128)}), f32[128,2,36]{2,1,0:T(2,128)S(1)}, u32[]{:S(2)}, u32[]{:S(2)}) async-start(f32[128,2,36]{2,1,0:T(2,128)} %bitcast.10), calls=%async_computation.3 | async-start | bytes 262144 | tf_op jit(solution)/shard_map/all_to_all | solution.py:113
  169.0 7.0 %copy-start.6 = (bf16[1,576,896]{2,1,0:T(8,128)(2,1)S(1)}, bf16[1,576,896]{2,1,0:T(8,128)(2,1)}, u32[]{:S(2)}) copy-start(bf16[1,576,896]{2,1,0:T(8,128)(2,1)} %get-tuple-element.37) | copy-start | bytes 3096580
  169.1 7.0 %copy-start.7 = (bf16[1,576,896]{2,1,0:T(8,128)(2,1)S(1)}, bf16[1,576,896]{2,1,0:T(8,128)(2,1)}, u32[]{:S(2)}) copy-start(bf16[1,576,896]{2,1,0:T(8,128)(2,1)} %get-tuple-element.38) | copy-start | bytes 3096580
  (6 other events, 10.4 us)
Sparse Core Ops, SparseCore 0:
  13.4 23.8 all-gather.1

commit v8 on v7

--- a/solution.py
+++ b/solution.py
@@ -107,12 +107,14 @@
         own_terms[local] = jnp.dot(
             term_hidden[local].T, own_terms[local], preferred_element_type=jnp.float32
         ).astype(jnp.bfloat16)
+    returned = lax.all_to_all(
+        outgoing_scores, ("expert", "tensor"), split_axis=0, concat_axis=0, tiled=True
+    )
+    returned, term_peer = lax.optimization_barrier((returned, term_peer))
+    for local in range(local_experts):
         peer_terms[local] = jnp.dot(
             term_peer[local].T, peer_terms[local], preferred_element_type=jnp.float32
         ).astype(jnp.bfloat16)
-    returned = lax.all_to_all(
-        outgoing_scores, ("expert", "tensor"), split_axis=0, concat_axis=0, tiled=True
-    )
     returned = jnp.sum(
         returned.reshape(experts, tensor_size, local_experts, capacity), axis=1
     ).reshape(-1)

time: 191 us -> 191 us (level)
  transfers between devices with their start and end apart: 15 -> 15, of which waited for: 6 -> 6; matrix products, arithmetic and copies ran while one was open for 28% -> 25% of each run, Pallas kernels for 0% -> 0%
where the time goes in v8:
time: 191 us; the launch traced here: 189 us
  waiting for transfers between devices  64.2 us (34%)
  starting transfers between devices  45.1 us (24%)
  matrix products  30.3 us (16%)
  local copies, waits for them, and re-layouts  18.1 us (9%)
  other arithmetic  16.6 us (9%)
  between operations  14.7 us (8%)
    all_to_all x2, waiting for transfers between devices, body(): lax.all_to_all(outgoing, 'expert', split_axis=0, concat_axis=0, tiled=True)  48 us
    all_to_all x2, starting transfers between devices, body(): lax.all_to_all(outgoing, 'expert', split_axis=0, concat_axis=0, tiled=True)  14.8 us
    ppermute x4, waiting for transfers between devices, ring_gather(): going_right = lax.ppermute(going_right, axis, right)  13.5 us
    ppermute x3, starting transfers between devices, ring_gather(): going_left = lax.ppermute(going_left, axis, left)  10.6 us
    dot_general x2, matrix products, body(): jnp.dot(routed, full_weight[local].T, preferred_element_type=jnp.float32)  9.7 us
    all_to_all x1, starting transfers between devices, body(): lax.all_to_all(outgoing_scores, ('expert', 'tensor'), split_axis=0, conca...  9.49 us
    dot_general x2, matrix products, body(): lax.dot_general(placing[:, local], gathered, (((2,), (0,)), ((), ())), pr...  7.68 us
    all_to_all x1, starting transfers between devices, body(): lax.all_to_all(slot_scale, 'expert', split_axis=0, concat_axis=2, tiled=T...  7.48 us
  transfers between devices with their start and end apart: 15, of which 6 were waited for; matrix products, arithmetic and copies ran while one was open for 25% of the time, Pallas kernels for 0%

profile of v8, /device:TPU:2, one launch (start us, length us, event | category | flops | bytes accessed | tf_op | source)
XLA Modules:
  0.0 188.9 jit_solution(17258433161132037483)
XLA Ops:
  9.2 4.0 %collective-permute-start.1 = (bf16[512,256]{1,0:T(8,128)(2,1)}, bf16[512,256]{1,0:T(8,128)(2,1)S(1)}, u32[]{:S(2)}, u32[]{:S(2)}) collective-permute-start(bf16[512,256]{1,0:T(8,128)(2,1)} %param.6), channel_id=1, source_target_pairs={{0,14},{2,0},{4,2},{6,4},{8,6},{10,8},{12,10},{14,12},{1,15},{3,1}... | collective-permute-start | bytes 786440 | tf_op jit(solution)/shard_map/ppermute | solution.py:36
  16.9 7.5 %all-to-all-start.2 = ((bf16[16,2,36]{2,1,0:T(2,128)(2,1)}), bf16[16,2,36]{2,1,0:T(2,128)(2,1)S(1)}, u32[]{:S(2)}, u32[]{:S(2)}) async-start(bf16[16,2,36]{2,1,0:T(2,128)(2,1)} %reshape.92), calls=%async_computation.2 | async-start | bytes 16384 | tf_op jit(solution)/shard_map/all_to_all | solution.py:69
  25.0 3.3 %collective-permute-start.3 = (bf16[512,256]{1,0:T(8,128)(2,1)S(1)}, bf16[512,256]{1,0:T(8,128)(2,1)}, u32[]{:S(2)}, u32[]{:S(2)}) collective-permute-start(bf16[512,256]{1,0:T(8,128)(2,1)S(1)} %collective-permute-done.1), channel_id=1, source_target_pairs={{0,14},{2,0},{4,2},{6,4},{8,6},{10,8},{12,10},{14,12},{1,15},{3,1}... | collective-permute-start | bytes 786440 | tf_op jit(solution)/shard_map/ppermute | solution.py:36
  28.7 4.5 %collective-permute-done.2 = bf16[512,256]{1,0:T(8,128)(2,1)} collective-permute-done((bf16[512,256]{1,0:T(8,128)(2,1)}, bf16[512,256]{1,0:T(8,128)(2,1)}, u32[]{:S(2)}, u32[]{:S(2)}) %collective-permute-start.2) | collective-permute-done | bytes 262176 | tf_op jit(solution)/shard_map/ppermute | solution.py:31
  34.3 3.3 %collective-permute-start.5 = (bf16[512,256]{1,0:T(8,128)(2,1)}, bf16[512,256]{1,0:T(8,128)(2,1)S(1)}, u32[]{:S(2)}, u32[]{:S(2)}) collective-permute-start(bf16[512,256]{1,0:T(8,128)(2,1)} %collective-permute-done.3), channel_id=1, source_target_pairs={{0,14},{2,0},{4,2},{6,4},{8,6},{10,8},{12,10},{14,12},{1,15},{3,1}... | collective-permute-start | bytes 786440 | tf_op jit(solution)/shard_map/ppermute | solution.py:36
  38.5 2.5 %collective-permute-done.4 = bf16[512,256]{1,0:T(8,128)(2,1)S(1)} collective-permute-done((bf16[512,256]{1,0:T(8,128)(2,1)}, bf16[512,256]{1,0:T(8,128)(2,1)S(1)}, u32[]{:S(2)}, u32[]{:S(2)}) %collective-permute-start.4) | collective-permute-done | bytes 262176 | tf_op jit(solution)/shard_map/ppermute | solution.py:31
  42.1 6.5 %collective-permute-done.6 = bf16[512,256]{1,0:T(8,128)(2,1)S(1)} collective-permute-done((bf16[512,256]{1,0:T(8,128)(2,1)S(1)}, bf16[512,256]{1,0:T(8,128)(2,1)S(1)}, u32[]{:S(2)}, u32[]{:S(2)}) %collective-permute-start.6) | collective-permute-done | bytes 262176 | tf_op jit(solution)/shard_map/ppermute | solution.py:31
  48.6 3.1 %convolution_convert_fusion.1 = bf16[16,36,2048]{2,1,0:T(8,128)(2,1)} fusion(bf16[512,2048]{1,0:T(8,128)(2,1)S(1)} %constant_dynamic-update-slice_fusion, pred[16,2,36,512]{3,2,0,1:T(8,128)(4,1)S(1)} %compare_or_fusion), kind=kOutput, calls=%fused_computation.14 | convolution fusion | flops 1209139200 | bytes 4784128 | tf_op jit(solution)/shard_map/dot_general | solution.py:79
  51.7 7.2 %all-to-all-start = ((bf16[16,36,2048]{2,1,0:T(8,128)(2,1)}), bf16[16,36,2048]{2,1,0:T(8,128)(2,1)S(1)}, u32[]{:S(2)}, u32[]{:S(2)}) async-start(bf16[16,36,2048]{2,1,0:T(8,128)(2,1)} %convolution_convert_fusion.1), calls=%async_computation | async-start | bytes 5242880 | tf_op jit(solution)/shard_map/all_to_all | solution.py:83
  59.0 4.6 %convolution_convert_fusion = bf16[16,36,2048]{2,1,0:T(8,128)(2,1)} fusion(bf16[512,2048]{1,0:T(8,128)(2,1)} %copy-done.5, pred[16,2,36,512]{3,2,0,1:T(8,128)(4,1)S(1)} %compare_or_fusion), kind=kOutput, calls=%fused_computation.13 | convolution fusion | flops 1209139200 | bytes 4784128 | tf_op jit(solution)/shard_map/dot_general | solution.py:79
  63.6 25.1 %all-to-all-done = bf16[16,36,2048]{2,1,0:T(8,128)(2,1)S(1)} async-done(((bf16[16,36,2048]{2,1,0:T(8,128)(2,1)}), bf16[16,36,2048]{2,1,0:T(8,128)(2,1)S(1)}, u32[]{:S(2)}, u32[]{:S(2)}) %all-to-all-start) | async-done | bytes 2359328 | tf_op jit(solution)/shard_map/all_to_all | solution.py:83
  88.6 7.6 %all-to-all-start.1 = ((bf16[16,36,2048]{2,1,0:T(8,128)(2,1)}), bf16[16,36,2048]{2,1,0:T(8,128)(2,1)}, u32[]{:S(2)}, u32[]{:S(2)}) async-start(bf16[16,36,2048]{2,1,0:T(8,128)(2,1)} %convolution_convert_fusion), calls=%async_computation.1 | async-start | bytes 5242880 | tf_op jit(solution)/shard_map/all_to_all | solution.py:83
  96.5 2.1 %reshape.89 = bf16[576,2048]{1,0:T(8,128)(2,1)} reshape(bf16[16,36,2048]{2,1,0:T(8,128)(2,1)S(1)} %all-to-all-done) | data formatting | bytes 4718592 | tf_op jit(solution)/shard_map/reshape | solution.py:85
  103.8 22.9 %all-to-all-done.1 = bf16[16,36,2048]{2,1,0:T(8,128)(2,1)} async-done(((bf16[16,36,2048]{2,1,0:T(8,128)(2,1)}), bf16[16,36,2048]{2,1,0:T(8,128)(2,1)}, u32[]{:S(2)}, u32[]{:S(2)}) %all-to-all-start.1) | async-done | bytes 2359328 | tf_op jit(solution)/shard_map/all_to_all | solution.py:83
  126.7 2.7 %reshape.90 = bf16[576,2048]{1,0:T(8,128)(2,1)S(1)} reshape(bf16[16,36,2048]{2,1,0:T(8,128)(2,1)} %all-to-all-done.1) | data formatting | bytes 4718592 | tf_op jit(solution)/shard_map/reshape | solution.py:85
  132.6 5.5 %fusion.1 = f32[576,896]{1,0:T(8,128)S(1)} fusion(bf16[576,2048]{1,0:T(8,128)(2,1)} %copy-done.1, bf16[2,896,2048]{2,1,0:T(8,128)(2,1)} %all-gather.2.cloned.1.call-done), kind=kOutput, calls=%fused_computation.8 | convolution fusion | flops 2113929216 | bytes 8093696 | tf_op jit(solution)/shard_map/dot_general | solution.py:86
  138.8 4.2 %fusion.8 = (f32[576]{0:T(1024)S(1)}, f32[576]{0:T(1024)S(1)}, bf16[1,576,896]{2,1,0:T(8,128)(2,1)}, bf16[1,576,896]{2,1,0:T(8,128)(2,1)}) fusion(bf16[2,576,896]{2,1,0:T(8,128)(2,1)S(1)} %copy-done.13, f32[576,896]{1,0:T(8,128)S(1)} %fusion.1, f32[576]{0:T(1024)S(1)} %mul.108, f32[576]{0:T(1024)S(1)} %mul.112, bf16[576,2048]{1,0:T(8,128)(2,1)S(1)} %copy-done, ...), kind=kOutput, calls=%fused_computation.26 | convolution fusion | flops 2119089152 | bytes 12235264 | tf_op jit(solution)/shard_map/dot_general | solution.py:86
  143.9 9.5 %all-to-all-start.3 = ((f32[128,2,36]{2,1,0:T(2,128)}), f32[128,2,36]{2,1,0:T(2,128)S(1)}, u32[]{:S(2)}, u32[]{:S(2)}) async-start(f32[128,2,36]{2,1,0:T(2,128)} %bitcast.10), calls=%async_computation.3 | async-start | bytes 262144 | tf_op jit(solution)/shard_map/all_to_all | solution.py:110
  153.4 3.4 %convert_bitcast_fusion.3 = bf16[1,896,1024]{2,1,0:T(8,128)(2,1)S(1)} fusion(bf16[576,2048]{1,0:T(8,128)(2,1)} %copy-done.2, s32[]{:T(128)S(6)} %select_n.87, bf16[2,576,896]{2,1,0:T(8,128)(2,1)} %param.10), kind=kOutput, calls=%fused_computation.32 | convolution fusion | flops 1057882112 | bytes 4046852 | tf_op jit(solution)/shard_map/dot_general | solution.py:107
  162.1 2.7 %all-to-all-done.3 = f32[128,2,36]{2,1,0:T(2,128)S(1)} async-done(((f32[128,2,36]{2,1,0:T(2,128)}), f32[128,2,36]{2,1,0:T(2,128)S(1)}, u32[]{:S(2)}, u32[]{:S(2)}) %all-to-all-start.3) | async-done | bytes 36896 | tf_op jit(solution)/shard_map/all_to_all | solution.py:110
  164.8 3.2 %convert_bitcast_fusion.1 = bf16[1,896,1024]{2,1,0:T(8,128)(2,1)S(1)} fusion(bf16[576,1024]{1,0:T(8,128)(2,1)} %collective-permute-done.8, bf16[2,576,896]{2,1,0:T(8,128)(2,1)} %collective-permute-done.7), kind=kOutput, calls=%fused_computation.30 | convolution fusion | flops 1057882112 | bytes 4046848 | tf_op jit(solution)/shard_map/dot_general | solution.py:115
  168.0 3.2 %convert_bitcast_fusion = bf16[1,896,1024]{2,1,0:T(8,128)(2,1)S(1)} fusion(bf16[576,1024]{1,0:T(8,128)(2,1)} %collective-permute-done.9, bf16[2,576,896]{2,1,0:T(8,128)(2,1)} %collective-permute-done.7), kind=kOutput, calls=%fused_computation.29 | convolution fusion | flops 1057882112 | bytes 4046848 | tf_op jit(solution)/shard_map/dot_general | solution.py:115
  171.2 2.2 %pad_maximum_fusion.1 = bf16[2,896,1024]{2,1,0:T(8,128)(2,1)} fusion(bf16[1,896,1024]{2,1,0:T(8,128)(2,1)S(1)} %convert_bitcast_fusion, bf16[1,896,1024]{2,1,0:T(8,128)(2,1)S(1)} %convert_bitcast_fusion.1), kind=kLoop, calls=%fused_computation.12 | loop fusion | flops 1835008 | bytes 7340032 | tf_op jit(solution)/shard_map/stack | solution.py:125
  175.2 6.8 %add_convert_fusion = bf16[2,896,1024]{2,1,0:T(8,128)(2,1)} fusion(bf16[2,896,1024]{2,1,0:T(8,128)(2,1)} %pad_maximum_fusion.1, bf16[2,896,1024]{2,1,0:T(8,128)(2,1)} %pad_maximum_fusion), kind=kLoop, calls=%fused_computation | loop fusion | flops 7340032 | bytes 11010048 | tf_op jit(solution)/shard_map/convert_element_type | solution.py:127
  (99 shorter events, 26.7 us)
Async XLA Ops:
  7.2 6.1 %copy-start.9 = (s32[512,2]{0,1:T(2,128)S(1)}, s32[512,2]{0,1:T(2,128)}, u32[]{:S(2)}) copy-start(s32[512,2]{0,1:T(2,128)} %param.7) | copy-start | bytes 12292
  7.2 125.4 %all-gather.2.cloned.1.call-start = ((), (), s32[]{:S(2)}) async-start(), calls=%async_computation.4 | async-start | bytes 11010048 | tf_op jit(solution)/shard_map/all_gather | solution.py:72
  7.2 17.2 %collective-permute-start = (bf16[512,256]{1,0:T(8,128)(2,1)}, bf16[512,256]{1,0:T(8,128)(2,1)}, u32[]{:S(2)}, u32[]{:S(2)}) collective-permute-start(bf16[512,256]{1,0:T(8,128)(2,1)} %param.6), channel_id=1, source_target_pairs={{0,2},{2,4},{4,6},{6,8},{8,10},{10,12},{12,14},{14,0},{1,3},{3,5},... | collective-permute-start | bytes 786440 | tf_op jit(solution)/shard_map/ppermute | solution.py:31
  9.2 15.8 %collective-permute-start.1 = (bf16[512,256]{1,0:T(8,128)(2,1)}, bf16[512,256]{1,0:T(8,128)(2,1)S(1)}, u32[]{:S(2)}, u32[]{:S(2)}) collective-permute-start(bf16[512,256]{1,0:T(8,128)(2,1)} %param.6), channel_id=1, source_target_pairs={{0,14},{2,0},{4,2},{6,4},{8,6},{10,8},{12,10},{14,12},{1,15},{3,1}... | collective-permute-start | bytes 786440 | tf_op jit(solution)/shard_map/ppermute | solution.py:36
  15.1 13.4 %copy-start.8 = (bf16[512,256]{1,0:T(8,128)(2,1)S(1)}, bf16[512,256]{1,0:T(8,128)(2,1)}, u32[]{:S(2)}) copy-start(bf16[512,256]{1,0:T(8,128)(2,1)} %param.6) | copy-start | bytes 786436
  16.9 34.8 %all-to-all-start.2 = ((bf16[16,2,36]{2,1,0:T(2,128)(2,1)}), bf16[16,2,36]{2,1,0:T(2,128)(2,1)S(1)}, u32[]{:S(2)}, u32[]{:S(2)}) async-start(bf16[16,2,36]{2,1,0:T(2,128)(2,1)} %reshape.92), calls=%async_computation.2 | async-start | bytes 16384 | tf_op jit(solution)/shard_map/all_to_all | solution.py:69
  24.4 8.8 %collective-permute-start.2 = (bf16[512,256]{1,0:T(8,128)(2,1)}, bf16[512,256]{1,0:T(8,128)(2,1)}, u32[]{:S(2)}, u32[]{:S(2)}) collective-permute-start(bf16[512,256]{1,0:T(8,128)(2,1)} %collective-permute-done), channel_id=1, source_target_pairs={{0,2},{2,4},{4,6},{6,8},{8,10},{10,12},{12,14},{14,0},{1,3},{3,5},... | collective-permute-start | bytes 786440 | tf_op jit(solution)/shard_map/ppermute | solution.py:31
  25.0 9.2 %collective-permute-start.3 = (bf16[512,256]{1,0:T(8,128)(2,1)S(1)}, bf16[512,256]{1,0:T(8,128)(2,1)}, u32[]{:S(2)}, u32[]{:S(2)}) collective-permute-start(bf16[512,256]{1,0:T(8,128)(2,1)S(1)} %collective-permute-done.1), channel_id=1, source_target_pairs={{0,14},{2,0},{4,2},{6,4},{8,6},{10,8},{12,10},{14,12},{1,15},{3,1}... | collective-permute-start | bytes 786440 | tf_op jit(solution)/shard_map/ppermute | solution.py:36
  33.2 7.8 %collective-permute-start.4 = (bf16[512,256]{1,0:T(8,128)(2,1)}, bf16[512,256]{1,0:T(8,128)(2,1)S(1)}, u32[]{:S(2)}, u32[]{:S(2)}) collective-permute-start(bf16[512,256]{1,0:T(8,128)(2,1)} %collective-permute-done.2), channel_id=1, source_target_pairs={{0,2},{2,4},{4,6},{6,8},{8,10},{10,12},{12,14},{14,0},{1,3},{3,5},... | collective-permute-start | bytes 786440 | tf_op jit(solution)/shard_map/ppermute | solution.py:31
  34.3 7.8 %collective-permute-start.5 = (bf16[512,256]{1,0:T(8,128)(2,1)}, bf16[512,256]{1,0:T(8,128)(2,1)S(1)}, u32[]{:S(2)}, u32[]{:S(2)}) collective-permute-start(bf16[512,256]{1,0:T(8,128)(2,1)} %collective-permute-done.3), channel_id=1, source_target_pairs={{0,14},{2,0},{4,2},{6,4},{8,6},{10,8},{12,10},{14,12},{1,15},{3,1}... | collective-permute-start | bytes 786440 | tf_op jit(solution)/shard_map/ppermute | solution.py:36
  41.0 7.6 %collective-permute-start.6 = (bf16[512,256]{1,0:T(8,128)(2,1)S(1)}, bf16[512,256]{1,0:T(8,128)(2,1)S(1)}, u32[]{:S(2)}, u32[]{:S(2)}) collective-permute-start(bf16[512,256]{1,0:T(8,128)(2,1)S(1)} %collective-permute-done.4), channel_id=1, source_target_pairs={{0,2},{2,4},{4,6},{6,8},{8,10},{10,12},{12,14},{14,0},{1,3},{3,5},... | collective-permute-start | bytes 786440 | tf_op jit(solution)/shard_map/ppermute | solution.py:31
  48.6 3.1 %copy-start.5 = (bf16[512,2048]{1,0:T(8,128)(2,1)}, bf16[512,2048]{1,0:T(8,128)(2,1)S(1)}, u32[]{:S(2)}) copy-start(bf16[512,2048]{1,0:T(8,128)(2,1)S(1)} %constant_dynamic-update-slice_fusion) | copy-start | bytes 6291460
  51.7 36.9 %all-to-all-start = ((bf16[16,36,2048]{2,1,0:T(8,128)(2,1)}), bf16[16,36,2048]{2,1,0:T(8,128)(2,1)S(1)}, u32[]{:S(2)}, u32[]{:S(2)}) async-start(bf16[16,36,2048]{2,1,0:T(8,128)(2,1)} %convolution_convert_fusion.1), calls=%async_computation | async-start | bytes 5242880 | tf_op jit(solution)/shard_map/all_to_all | solution.py:83
  88.6 38.0 %all-to-all-start.1 = ((bf16[16,36,2048]{2,1,0:T(8,128)(2,1)}), bf16[16,36,2048]{2,1,0:T(8,128)(2,1)}, u32[]{:S(2)}, u32[]{:S(2)}) async-start(bf16[16,36,2048]{2,1,0:T(8,128)(2,1)} %convolution_convert_fusion), calls=%async_computation.1 | async-start | bytes 5242880 | tf_op jit(solution)/shard_map/all_to_all | solution.py:83
  96.2 46.9 %collective-permute-start.7 = (bf16[2,576,896]{2,1,0:T(8,128)(2,1)}, bf16[2,576,896]{2,1,0:T(8,128)(2,1)}, u32[]{:S(2)}, u32[]{:S(2)}) collective-permute-start(bf16[2,576,896]{2,1,0:T(8,128)(2,1)} %param.10), channel_id=1, source_target_pairs={{0,1},{1,0},{2,3},{3,2},{4,5},{5,4},{6,7},{7,6},{8,9},{9,8},{10,11... | collective-permute-start | bytes 6193160 | tf_op jit(solution)/shard_map/ppermute | solution.py:10
  103.3 61.5 %collective-permute-start.8 = (bf16[576,1024]{1,0:T(8,128)(2,1)}, bf16[576,1024]{1,0:T(8,128)(2,1)}, u32[]{:S(2)}, u32[]{:S(2)}) collective-permute-start(bf16[576,1024]{1,0:T(8,128)(2,1)} %constant_dynamic-slice_fusion.1), channel_id=1, source_target_pairs={{0,1},{1,0},{2,3},{3,2},{4,5},{5,4},{6,7},{7,6},{8,9},{9,8},{10,11... | collective-permute-start | bytes 3538952 | tf_op jit(solution)/shard_map/ppermute | solution.py:10
  132.6 5.6 %copy-start = (bf16[576,2048]{1,0:T(8,128)(2,1)S(1)}, bf16[576,2048]{1,0:T(8,128)(2,1)}, u32[]{:S(2)}) copy-start(bf16[576,2048]{1,0:T(8,128)(2,1)} %reshape.89) | copy-start | bytes 7077892
  132.6 35.4 %collective-permute-start.9 = (bf16[576,1024]{1,0:T(8,128)(2,1)}, bf16[576,1024]{1,0:T(8,128)(2,1)}, u32[]{:S(2)}, u32[]{:S(2)}) collective-permute-start(bf16[576,1024]{1,0:T(8,128)(2,1)} %constant_dynamic-slice_fusion), channel_id=1, source_target_pairs={{0,1},{1,0},{2,3},{3,2},{4,5},{5,4},{6,7},{7,6},{8,9},{9,8},{10,11... | collective-permute-start | bytes 3538952 | tf_op jit(solution)/shard_map/ppermute | solution.py:10
  132.6 5.6 %copy-start.12 = (bf16[2,896,2048]{2,1,0:T(8,128)(2,1)S(1)}, bf16[2,896,2048]{2,1,0:T(8,128)(2,1)}, u32[]{:S(2)}) copy-start(bf16[2,896,2048]{2,1,0:T(8,128)(2,1)} %all-gather.2.cloned.1.call-done) | copy-start | bytes 22020100
  132.6 6.2 %copy-start.13 = (bf16[2,576,896]{2,1,0:T(8,128)(2,1)S(1)}, bf16[2,576,896]{2,1,0:T(8,128)(2,1)}, u32[]{:S(2)}) copy-start(bf16[2,576,896]{2,1,0:T(8,128)(2,1)} %param.10) | copy-start | bytes 6193156
  143.9 20.9 %all-to-all-start.3 = ((f32[128,2,36]{2,1,0:T(2,128)}), f32[128,2,36]{2,1,0:T(2,128)S(1)}, u32[]{:S(2)}, u32[]{:S(2)}) async-start(f32[128,2,36]{2,1,0:T(2,128)} %bitcast.10), calls=%async_computation.3 | async-start | bytes 262144 | tf_op jit(solution)/shard_map/all_to_all | solution.py:110
  153.4 3.4 %copy-start.4 = (bf16[576,2048]{1,0:T(8,128)(2,1)S(1)}, bf16[576,2048]{1,0:T(8,128)(2,1)}, u32[]{:S(2)}) copy-start(bf16[576,2048]{1,0:T(8,128)(2,1)} %copy-done.3) | copy-start | bytes 7077892
  153.4 3.4 %copy-start.14 = (bf16[2,576,896]{2,1,0:T(8,128)(2,1)S(1)}, bf16[2,576,896]{2,1,0:T(8,128)(2,1)}, u32[]{:S(2)}) copy-start(bf16[2,576,896]{2,1,0:T(8,128)(2,1)} %param.10) | copy-start | bytes 6193156
  158.4 2.2 %copy-start.7 = (bf16[1,576,896]{2,1,0:T(8,128)(2,1)S(1)}, bf16[1,576,896]{2,1,0:T(8,128)(2,1)}, u32[]{:S(2)}) copy-start(bf16[1,576,896]{2,1,0:T(8,128)(2,1)} %get-tuple-element.42) | copy-start | bytes 3096580
  (6 other events, 9.4 us)
Sparse Core Ops, SparseCore 0:
  13.4 23.8 all-gather.1
